TPU v7x, 128 devices: a whole 4x4x4 slice. The times are simulated.
128 devices in a mesh: front: 4 (over z), row: 4 (over x_lo, core), col: 8 (over x_hi, y).
Axes of the slice: x: 4 (x_hi: 2, x_lo: 2; x = x_hi * 2 + x_lo), y: 4, z: 4, core: 2. Of those that a mesh axis runs over, the one named last changes fastest.
Arguments:
- front_orig: float32 [4, 8192, 8192], P('front', 'row', 'col'), may hold values from -6 to 6
- children: float32 [4, 2048, 2048], P('front', 'row', 'col'), may hold values from -6 to 6
- parent_of: int32 [4], P('front'), may hold values from 0 to 3, as said below
- child_map: int32 [4, 8], P('front'), may hold values from 0 to 31, as said below
- block_mask: int32 [4, 32, 32], P('front'), may hold values 0 or 1
- pivot: int32 [4, 32], P('front'), may hold values from 0 to 31, each once within a row
- diag_inverse: float32 [4, 2, 512, 512], P('front'), may hold values from -0.01171875 to 0.01171875
Outputs:
- factored: float32 [4, 8192, 8192], P('front', 'row', 'col')
Inputs may be any that keep to these rules, and one draw needn't show every extreme that they name: `parent_of`: each front is the parent of exactly one child update. Each row of child_map is strictly increasing.
All inputs are finite; a program needn't handle non-finite values. No bound on the sum of `block_mask` on one device may be relied on, other than what follows from the above.
Results may differ from a plain program's by a relative error of at most 0.00011.
Values sent between devices are 32-bit elements; how exact they have to be, the bound alone decides.
No kernel may reach another device: no remote copies, remote signals or barrier semaphores. Data moves between devices by JAX's collectives and lax.ppermute only.
A program may use at most 128 MiB of HBM per device.

v0:
```python
import jax
import jax.numpy as jnp
from jax import lax
from jax.sharding import PartitionSpec as P

BS = 256


HIGH = lax.Precision.HIGHEST


def from_root(x, axis, root):
    mine = lax.axis_index(axis) == root
    return lax.psum(jnp.where(mine, x, jnp.zeros_like(x)), axis)


def body(front_orig, children, parent_of, child_map, block_mask, pivot, diag_inverse):
    row_count = lax.axis_size("row")
    col_count = lax.axis_size("col")
    row_id = lax.axis_index("row")
    col_id = lax.axis_index("col")
    front_id = lax.axis_index("front")
    matrix_in = front_orig[0]
    loc_rows, loc_cols = matrix_in.shape
    row_blocks = loc_rows // BS
    col_blocks = loc_cols // BS
    kid_count = children.shape[0]
    kid_rows = children.shape[1] // BS
    kid_cols = children.shape[2] // BS

    def spread(grid):
        return jnp.broadcast_to(grid[:, None, :, None], (row_blocks, BS, col_blocks, BS)).reshape(
            loc_rows, loc_cols
        )

    all_kids, all_parents, all_maps = (
        lax.all_gather(children, "front", axis=0, tiled=True),
        lax.all_gather(parent_of, "front", axis=0, tiled=True),
        lax.all_gather(child_map, "front", axis=0, tiled=True),
    )
    child_count = all_parents.shape[0]
    serial = jnp.arange(child_count, dtype=jnp.int32)
    sort_keys = jnp.where(all_parents == front_id, serial, serial + child_count)
    owned_ids = jnp.argsort(sort_keys)[:kid_count]
    own_pieces = jnp.take(all_kids, owned_ids, axis=0)
    own_maps = jnp.take(all_maps, owned_ids, axis=0)
    child_blocks = own_maps.shape[1]
    block_ranks = jnp.arange(child_blocks, dtype=jnp.int32)

    def locate(first, width):
        target = first + jnp.arange(width, dtype=jnp.int32)
        matches = own_maps[:, :, None] == target[None, None, :]
        source = jnp.sum(jnp.where(matches, block_ranks[None, :, None], 0), axis=1)
        return (source, jnp.any(matches, axis=1).astype(jnp.float32))

    row_src, row_has = locate(row_id * row_blocks, row_blocks)
    col_src, col_has = locate(col_id * col_blocks, col_blocks)
    gathered = lax.all_gather(own_pieces[None], ("row", "col"), axis=0, tiled=True)
    child_tiles = gathered.reshape(row_count, col_count, kid_count, kid_rows, BS, kid_cols, BS)
    kid_ids = jnp.arange(kid_count, dtype=jnp.int32)
    picked = child_tiles[
        (row_src // kid_rows)[:, :, None],
        (col_src // kid_cols)[:, None, :],
        kid_ids[:, None, None],
        (row_src % kid_rows)[:, :, None],
        :,
        (col_src % kid_cols)[:, None, :],
        :,
    ]
    picked = picked * (row_has[:, :, None] * col_has[:, None, :])[:, :, :, None, None]
    extended = jnp.sum(picked, axis=0).transpose(0, 2, 1, 3).reshape(loc_rows, loc_cols)
    mask_local = lax.dynamic_slice(
        block_mask[0], (row_id * row_blocks, col_id * col_blocks), (row_blocks, col_blocks)
    ).astype(jnp.float32)
    matrix = spread(mask_local) * (matrix_in + extended)
    order = pivot[0]
    nblocks = order.shape[0]
    ranks = jnp.arange(nblocks, dtype=jnp.int32)
    position = jnp.sum(jnp.where(order[:, None] == ranks[None, :], ranks[:, None], 0), axis=0)
    for step in range(diag_inverse.shape[1]):
        alive = (position >= 2 * step + 2).astype(jnp.float32)
        alive_rows = lax.dynamic_slice_in_dim(alive, row_id * row_blocks, row_blocks)
        alive_cols = lax.dynamic_slice_in_dim(alive, col_id * col_blocks, col_blocks)
        row_live = jnp.repeat(alive_rows, BS)
        inverse = diag_inverse[0, step]
        col_parts = []
        row_parts = []
        col_owners = []
        col_slots = []
        for half in range(2):
            chosen = order[2 * step + half]
            owner_col = chosen // col_blocks
            slot_col = chosen % col_blocks
            piece = lax.dynamic_slice_in_dim(matrix, slot_col * BS, BS, 1)
            col_parts.append(from_root(piece, "col", owner_col))
            strip = lax.dynamic_slice_in_dim(matrix, chosen % row_blocks * BS, BS, 0)
            row_parts.append(from_root(strip, "row", chosen // row_blocks))
            col_owners.append(owner_col)
            col_slots.append(slot_col)
        column_panel = jnp.concatenate(col_parts, axis=1)
        row_panel = jnp.concatenate(row_parts, axis=0)
        lower = jnp.dot(column_panel, inverse, precision=HIGH, preferred_element_type=jnp.float32)
        update = jnp.dot(
            lower * row_live[:, None], row_panel, precision=HIGH, preferred_element_type=jnp.float32
        )
        lower_parts = [lower[:, :BS], lower[:, BS:]]
        live_mask = spread(mask_local * alive_rows[:, None] * alive_cols[None, :])
        fresh = matrix - update * live_mask
        for half in range(2):
            current = lax.dynamic_slice_in_dim(fresh, col_slots[half] * BS, BS, 1)
            written = jnp.where(row_live[:, None] > 0, lower_parts[half], current)
            replaced = lax.dynamic_update_slice_in_dim(fresh, written, col_slots[half] * BS, 1)
            fresh = jnp.where(col_id == col_owners[half], replaced, fresh)
        matrix = fresh
    return matrix[None]


def solution(mesh):
    placed = (
        P("front", "row", "col"),
        P("front", "row", "col"),
        P("front"),
        P("front", None),
        P("front", None, None),
        P("front", None),
        P("front", None, None, None),
    )
    return jax.shard_map(
        body, mesh=mesh, in_specs=placed, out_specs=P("front", "row", "col"), check_vma=False
    )
```

profile of v0, /device:TPU:1, one launch (start us, length us, event | category | flops | bytes accessed | tf_op | source)
XLA Modules:
  0.0 595.1 jit_solution(1748242243041129503)
XLA Ops:
  6.5 0.7 all-gather.5.cloned.1.call-update
  8.0 1.2 dynamic-slice.17
  9.2 0.8 dynamic-update-slice.7
  10.0 8.6 %all-reduce = s32[4]{0:T(128)S(1)} all-reduce(s32[4]{0:T(128)S(1)} %dynamic-update-slice.7), channel_id=1, replica_groups=mesh['front'=4,'row'=4,'col'=8] {'front'}, use_global_device_ids=true, to_apply=%add | all-reduce | flops 4 | bytes 32
  18.5 0.7 sort.17
  19.4 23.7 %all-gather.5.cloned.1.call-done = f32[4,512,256]{2,1,0:T(8,128)} async-done(((f32[1,512,256]{2,1,0:T(8,128)}), f32[4,512,256]{2,1,0:T(8,128)}) %all-gather.5.cloned.1.call-update) | async-done | bytes 2097168 | tf_op jit(solution)/shard_map/all_gather | solution.py:37
  43.1 1.9 dynamic-slice_select_fusion.8
  45.0 0.0 all-reduce.12.cloned.1.call-start
  45.0 5.9 all-gather.1
  50.9 1.5 fusion.45
  57.4 0.1 fusion.29
  57.5 0.2 fusion.39
  57.7 0.1 constant_dynamic-update-slice_fusion.4
  57.8 0.1 constant_dynamic-update-slice_fusion.1
  57.9 0.1 reshape.638
  58.0 0.1 compare_reduce_fusion
  58.1 0.2 compare_reduce_fusion.1
  58.2 0.8 fusion.28
  59.0 0.1 copy.22
  59.1 0.1 copy.23
  59.2 1.1 broadcast_in_dim.143
  60.3 5.5 copy.27
  65.8 0.1 broadcast_multiply_fusion
  65.9 81.7 %all-gather.7.cloned.1.call-done = f32[32,512,256]{2,1,0:T(8,128)} async-done(((f32[1,512,256]{2,1,0:T(8,128)}), f32[32,512,256]{2,1,0:T(8,128)}) %all-gather.7.cloned.1.call-update) | async-done | bytes 16777232 | tf_op jit(solution)/shard_map/all_gather | solution.py:58
  147.6 10.1 %gather_fusion = f32[32,256,256]{2,1,0:T(8,128)} fusion(f32[4,8,1,2,256,1,256]{6,4,3,1,0,5,2:T(8,128)} %bitcast.67, s32[32]{0:T(128)S(1)} %reshape.638), kind=kCustom, calls=%fused_computation | custom fusion | bytes 16777856 | tf_op jit(solution)/shard_map/gather | solution.py:61
  157.7 7.8 %multiply_bitcast_fusion = f32[8,256,4,256]{3,1,2,0:T(8,128)} fusion(f32[8,4,256,256]{3,2,1,0:T(8,128)} %bitcast.58, f32[8,4]{1,0:T(8,128)S(1)} %broadcast_multiply_fusion), kind=kLoop, calls=%fused_computation.5 | loop fusion | flops 2097152 | bytes 16777344 | tf_op jit(solution)/shard_map/transpose | solution.py:71
  165.4 12.0 %copy.24 = f32[8,256,4,256]{3,2,1,0:T(4,128)} copy(f32[8,256,4,256]{3,1,2,0:T(8,128)} %multiply_bitcast_fusion) | data formatting | bytes 16777216 | tf_op jit(solution)/shard_map/transpose | solution.py:71
  177.4 9.4 %copy.28 = f32[256,8,4,256]{3,1,2,0:T(8,128)} copy(f32[256,8,4,256]{3,2,1,0:T(4,128)} %bitcast.60) | data formatting | bytes 16777216
  186.8 7.4 %fusion = f32[2048,1024]{1,0:T(8,128)S(1)} fusion(f32[2048,1024]{1,0:T(8,128)S(1)} %bitcast.65, f32[2048,1024]{1,0:T(8,128)} %bitcast.66, f32[1,2048,1024]{2,1,0:T(8,128)} %param.7), kind=kLoop, calls=%fused_computation.2 | loop fusion | flops 4194304 | bytes 33554432 | tf_op jit(solution)/shard_map/mul | solution.py:75
  194.2 2.9 dynamic-slice_select_fusion.3
  197.2 1.7 copy-done.1
  198.9 0.0 all-reduce.16.cloned.1.call-start
  199.0 3.2 dynamic-slice_select_fusion.7
  202.3 0.1 select_reduce_fusion
  202.4 0.1 dynamic_slice.54
  202.5 0.1 dynamic_slice.57
  202.5 0.1 dynamic_slice.62
  202.6 0.1 dynamic_slice.65
  207.7 0.1 multiply_multiply_fusion
  207.8 0.1 copy.25
  207.8 1.1 broadcast_in_dim.159
  209.0 5.3 copy.30
  214.4 0.1 broadcast_bitcast_fusion.1
  214.4 94.9 %all-reduce.12.cloned.1.call-done = (f32[2048,256]{1,0:T(8,128)}, f32[2048,256]{1,0:T(8,128)}) async-done(((f32[2048,256]{1,0:T(8,128)}, f32[2048,256]{1,0:T(8,128)}), (f32[2048,256]{1,0:T(8,128)}, f32[2048,256]{1,0:T(8,128)})) %all-reduce.12.cloned.1.call-update) | async-done | bytes 4194320 | tf_op jit(solution)/shard_map/psum | solution.py:14
  309.3 9.9 %fusion.1 = f32[2048,512]{1,0:T(8,128)} fusion(f32[2048,256]{1,0:T(8,128)} %get-tuple-element.31, f32[2048,256]{1,0:T(8,128)} %get-tuple-element.32, f32[1,2,512,512]{3,2,1,0:T(8,128)S(1)} %copy-done.4), kind=kOutput, calls=%fused_computation.6 | convolution fusion | flops 6443499520 | bytes 9437184 | tf_op jit(solution)/shard_map/dot_general | solution.py:102
  319.2 49.1 %all-reduce.16.cloned.1.call-done = (f32[256,1024]{1,0:T(8,128)}, f32[256,1024]{1,0:T(8,128)}) async-done(((f32[256,1024]{1,0:T(8,128)}, f32[256,1024]{1,0:T(8,128)}), (f32[256,1024]{1,0:T(8,128)}, f32[256,1024]{1,0:T(8,128)})) %all-reduce.16.cloned.1.call-update) | async-done | bytes 2097168 | tf_op jit(solution)/shard_map/psum | solution.py:14
  368.3 19.3 %multiply_subtract_fusion.1 = f32[2048,1024]{1,0:T(8,128)S(1)} fusion(f32[2048,1024]{1,0:T(8,128)} %copy-done.1, f32[2048,1024]{1,0:T(8,128)} %bitcast.56, f32[2048,512]{1,0:T(8,128)} %fusion.1, f32[256,1024]{1,0:T(8,128)} %get-tuple-element.35, f32[256,1024]{1,0:T(8,128)} %get-tuple-element.36, f32[2048]{0:T(1024)S(1)} %bitcast.69), kind=kOutput, calls=%fused_computation.4 | convolution fusion | flops 12890669056 | bytes 31465472 | tf_op jit(solution)/shard_map/dot_general | solution.py:103
  387.6 0.7 fusion.11
  388.3 0.7 fusion.12
  389.1 2.9 dynamic-slice_select_fusion.1
  392.0 1.7 copy-done
  393.7 0.3 all-reduce.14.cloned.1.call-start
  394.1 3.2 dynamic-slice_select_fusion.5
  397.2 0.1 copy.26
  397.3 1.1 broadcast_in_dim.162
  398.5 5.3 copy.32
  403.8 0.1 broadcast_bitcast_fusion
  403.9 100.3 %all-reduce.10.cloned.1.call-done = (f32[2048,256]{1,0:T(8,128)}, f32[2048,256]{1,0:T(8,128)}) async-done(((f32[2048,256]{1,0:T(8,128)}, f32[2048,256]{1,0:T(8,128)}), (f32[2048,256]{1,0:T(8,128)}, f32[2048,256]{1,0:T(8,128)})) %all-reduce.10.cloned.1.call-update) | async-done | bytes 4194320 | tf_op jit(solution)/shard_map/psum | solution.py:14
  504.2 9.8 %fusion.5 = f32[2048,512]{1,0:T(8,128)} fusion(f32[2048,256]{1,0:T(8,128)} %get-tuple-element.29, f32[2048,256]{1,0:T(8,128)} %get-tuple-element.30, f32[1,2,512,512]{3,2,1,0:T(8,128)S(1)} %copy-done.4), kind=kOutput, calls=%fused_computation.10 | convolution fusion | flops 6443499520 | bytes 9437184 | tf_op jit(solution)/shard_map/dot_general | solution.py:102
  514.0 49.2 %all-reduce.14.cloned.1.call-done = (f32[256,1024]{1,0:T(8,128)}, f32[256,1024]{1,0:T(8,128)}) async-done(((f32[256,1024]{1,0:T(8,128)}, f32[256,1024]{1,0:T(8,128)}), (f32[256,1024]{1,0:T(8,128)}, f32[256,1024]{1,0:T(8,128)})) %all-reduce.14.cloned.1.call-update) | async-done | bytes 2097168 | tf_op jit(solution)/shard_map/psum | solution.py:14
  563.2 19.2 %multiply_subtract_fusion = f32[2048,1024]{1,0:T(8,128)S(1)} fusion(f32[2048,1024]{1,0:T(8,128)} %copy-done, f32[2048,1024]{1,0:T(8,128)} %bitcast.57, f32[2048,512]{1,0:T(8,128)} %fusion.5, f32[256,1024]{1,0:T(8,128)} %get-tuple-element.33, f32[256,1024]{1,0:T(8,128)} %get-tuple-element.34, f32[2048]{0:T(1024)S(1)} %bitcast.71), kind=kOutput, calls=%fused_computation.3 | convolution fusion | flops 12890669056 | bytes 31465472 | tf_op jit(solution)/shard_map/dot_general | solution.py:103
  582.4 0.7 fusion.13
  583.1 3.4 copy.49
  586.5 1.5 fusion.15
  (42 shorter events, 0.3 us)
Async XLA Ops:
  6.5 36.5 %all-gather.5.cloned.1.call-start = ((), (), s32[]{:S(2)}) async-start(), calls=%async_computation | async-start | bytes 2621440 | tf_op jit(solution)/shard_map/all_gather | solution.py:37
  7.3 140.3 %all-gather.7.cloned.1.call-start = ((), (), s32[]{:S(2)}) async-start(), calls=%async_computation.1 | async-start | bytes 17301504 | tf_op jit(solution)/shard_map/all_gather | solution.py:58
  45.0 264.4 %all-reduce.12.cloned.1.call-start = ((), (), s32[]{:S(2)}) async-start(), calls=%async_computation.3 | async-start | bytes 8388608 | tf_op jit(solution)/shard_map/psum | solution.py:14
  177.4 9.4 %slice-start = ((s8[8388608]{0:T(1024)(128)(4,1)}), s8[4194304]{0:T(1024)(128)(4,1)S(1)}, s32[]{:S(2)}) async-start(s8[8388608]{0:T(1024)(128)(4,1)} %bitcast.63), calls=%async_computation.6 | async-start | bytes 8388608
  177.4 9.4 %slice-start.1 = ((s8[8388608]{0:T(1024)(128)(4,1)}), s8[4194304]{0:T(1024)(128)(4,1)S(1)}, s32[]{:S(2)}) async-start(s8[8388608]{0:T(1024)(128)(4,1)} %bitcast.63), calls=%async_computation.7 | async-start | bytes 8388608
  194.2 4.7 copy-start.1
  198.9 3.4 copy-start.5
  198.9 169.4 %all-reduce.16.cloned.1.call-start = ((), (), s32[]{:S(2)}) async-start(), calls=%async_computation.5 | async-start | bytes 4194304 | tf_op jit(solution)/shard_map/psum | solution.py:14
  202.2 302.0 %all-reduce.10.cloned.1.call-start = ((), (), s32[]{:S(2)}) async-start(), calls=%async_computation.2 | async-start | bytes 8388608 | tf_op jit(solution)/shard_map/psum | solution.py:14
  209.0 100.3 %copy-start.4 = (f32[1,2,512,512]{3,2,1,0:T(8,128)S(1)}, f32[1,2,512,512]{3,2,1,0:T(8,128)}, u32[]{:S(2)}) copy-start(f32[1,2,512,512]{3,2,1,0:T(8,128)} %param.13) | copy-start | bytes 6291460
  368.3 19.3 %copy-start.3 = (f32[2048,512]{1,0:T(8,128)S(1)}, f32[2048,512]{1,0:T(8,128)}, u32[]{:S(2)}) copy-start(f32[2048,512]{1,0:T(8,128)} %fusion.1) | copy-start | bytes 12582916
  389.0 4.7 copy-start
  393.7 169.4 %all-reduce.14.cloned.1.call-start = ((), (), s32[]{:S(2)}) async-start(), calls=%async_computation.4 | async-start | bytes 4194304 | tf_op jit(solution)/shard_map/psum | solution.py:14
  563.2 19.2 %copy-start.2 = (f32[2048,512]{1,0:T(8,128)S(1)}, f32[2048,512]{1,0:T(8,128)}, u32[]{:S(2)}) copy-start(f32[2048,512]{1,0:T(8,128)} %fusion.5) | copy-start | bytes 12582916
Sparse Core Ops, SparseCore 0:
  9.0 34.0 all-gather.4
  45.1 102.4 all-gather.6
  199.0 110.2 all-reduce.11
  311.7 56.5 all-reduce.15
  393.8 110.2 all-reduce.9
  506.6 56.5 all-reduce.13
where the time goes:
time: 605 us; the launch traced here: 595 us
  waiting for transfers between devices  400 us (66%)
  local copies, waits for them, and re-layouts  62.3 us (10%)
  matrix products  58.1 us (10%)
  other arithmetic  35.3 us (6%)
  between operations  24.9 us (4%)
  blocking collectives  14.4 us (2%)
    psum x4, waiting for transfers between devices, from_root(): return lax.psum(jnp.where(mine, x, jnp.zeros_like(x)), axis)  293 us
    all_gather x1, waiting for transfers between devices, body(): lax.all_gather(own_pieces[None], ('row', 'col'), axis=0, tiled=True)  81.7 us
    dot_general x2, matrix products, body(): jnp.dot(lower * row_live[:, None], row_panel, precision=HIGH, preferred_e...  38.4 us
    unnamed x32, local copies, waits for them, and re-layouts  34.7 us
    all_gather x1, waiting for transfers between devices, body(): lax.all_gather(children, 'front', axis=0, tiled=True)  23.7 us
    dot_general x2, matrix products, body(): jnp.dot(column_panel, inverse, precision=HIGH, preferred_element_type=jnp...  19.7 us
    select_n x4, other arithmetic, from_root(): return lax.psum(jnp.where(mine, x, jnp.zeros_like(x)), axis)  12.2 us
  transfers between devices with their start and end apart: 6, of which 6 were waited for; matrix products, arithmetic and copies ran while one was open for 9% of the time, Pallas kernels for 0%

commit v1 on v0

v1 whole, which is shorter than its diff:
```python
import jax
import jax.numpy as jnp
from jax import lax
from jax.sharding import PartitionSpec as P

BS = 256


HIGH = lax.Precision.HIGHEST


def dot(a, b):
    return jnp.dot(a, b, precision=HIGH, preferred_element_type=jnp.float32)


def body(front_orig, children, parent_of, child_map, block_mask, pivot, diag_inverse):
    row_count = lax.axis_size("row")
    col_count = lax.axis_size("col")
    front_count = lax.axis_size("front")
    row_id = lax.axis_index("row")
    col_id = lax.axis_index("col")
    front_id = lax.axis_index("front")
    matrix_in = front_orig[0]
    loc_rows, loc_cols = matrix_in.shape
    row_blocks = loc_rows // BS
    col_blocks = loc_cols // BS
    kid_rows = children.shape[1] // BS
    kid_cols = children.shape[2] // BS

    def spread(grid):
        r, c = grid.shape
        return jnp.broadcast_to(grid[:, None, :, None], (r, BS, c, BS)).reshape(r * BS, c * BS)

    piece = children[0]
    tags = jnp.concatenate([parent_of, child_map[0]])
    best_piece = jnp.where(tags[0] == front_id, piece, jnp.zeros_like(piece))
    best_tags = jnp.where(tags[0] == front_id, tags, jnp.zeros_like(tags))
    for shift in range(1, front_count):
        perm = [(i, (i + shift) % front_count) for i in range(front_count)]
        got_piece = lax.ppermute(piece, "front", perm)
        got_tags = lax.ppermute(tags, "front", perm)
        hit = got_tags[0] == front_id
        best_piece = jnp.where(hit, got_piece, best_piece)
        best_tags = jnp.where(hit, got_tags, best_tags)
    own_map = best_tags[1:]
    child_blocks = own_map.shape[0]
    block_ranks = jnp.arange(child_blocks, dtype=jnp.int32)

    def locate(first, width):
        target = first + jnp.arange(width, dtype=jnp.int32)
        matches = own_map[:, None] == target[None, :]
        source = jnp.sum(jnp.where(matches, block_ranks[:, None], 0), axis=0)
        return source, jnp.any(matches, axis=0)

    row_src, row_has = locate(row_id * row_blocks, row_blocks)
    col_src, col_has = locate(col_id * col_blocks, col_blocks)
    gathered = lax.all_gather(best_piece, ("row", "col"), axis=0, tiled=False)
    child_tiles = gathered.reshape(row_count, col_count, kid_rows, BS, kid_cols, BS)
    picked = child_tiles[
        (row_src // kid_rows)[:, None],
        (col_src // kid_cols)[None, :],
        (row_src % kid_rows)[:, None],
        :,
        (col_src % kid_cols)[None, :],
        :,
    ]
    keep = row_has[:, None] & col_has[None, :]
    picked = jnp.where(keep[:, :, None, None], picked, 0.0)
    extended = picked.transpose(0, 2, 1, 3).reshape(loc_rows, loc_cols)

    mask_all = block_mask[0].astype(jnp.float32)
    mask_local = lax.dynamic_slice(
        mask_all, (row_id * row_blocks, col_id * col_blocks), (row_blocks, col_blocks)
    )
    assembled = spread(mask_local) * (matrix_in + extended)

    order = pivot[0]
    nblocks = order.shape[0]
    ranks = jnp.arange(nblocks, dtype=jnp.int32)
    position = jnp.sum(jnp.where(order[:, None] == ranks[None, :], ranks[:, None], 0), axis=0)
    alive0 = (position >= 2).astype(jnp.float32)
    alive1 = (position >= 4).astype(jnp.float32)
    piv = [order[k] for k in range(4)]

    col_parts = []
    for blk in piv:
        piece_c = lax.dynamic_slice_in_dim(assembled, (blk % col_blocks) * BS, BS, 1)
        col_parts.append(jnp.where(col_id == blk // col_blocks, piece_c, 0.0))
    col_panels = lax.psum(jnp.concatenate(col_parts, axis=1), "col")

    def rows_of(blk, cols):
        strip = lax.dynamic_slice_in_dim(cols, (blk % row_blocks) * BS, BS, 0)
        return jnp.where(row_id == blk // row_blocks, strip, 0.0)

    corner_x = jnp.concatenate([rows_of(piv[0], col_panels[:, 2 * BS:]), rows_of(piv[1], col_panels[:, 2 * BS:])], axis=0)
    corner_y = jnp.concatenate([rows_of(piv[2], col_panels[:, :2 * BS]), rows_of(piv[3], col_panels[:, :2 * BS])], axis=0)

    row_parts = [rows_of(blk, assembled) for blk in piv]
    row_payload = jnp.concatenate(row_parts + [jnp.concatenate([corner_x, corner_y], axis=1)], axis=0)
    row_payload = lax.psum(row_payload, "row")
    row_panels = row_payload[: 4 * BS]
    corner_x = row_payload[4 * BS:, : 2 * BS]
    corner_y = row_payload[4 * BS:, 2 * BS:]

    alive0_rows = jnp.repeat(lax.dynamic_slice_in_dim(alive0, row_id * row_blocks, row_blocks), BS)
    alive1_rows = jnp.repeat(lax.dynamic_slice_in_dim(alive1, row_id * row_blocks, row_blocks), BS)
    alive0_cb = lax.dynamic_slice_in_dim(alive0, col_id * col_blocks, col_blocks)
    alive1_cb = lax.dynamic_slice_in_dim(alive1, col_id * col_blocks, col_blocks)
    alive0_cols = jnp.repeat(alive0_cb, BS)
    alive1_cols = jnp.repeat(alive1_cb, BS)

    lower0 = dot(col_panels[:, : 2 * BS], diag_inverse[0, 0])
    w0 = lower0 * alive0_rows[:, None]
    mask_rows_p1q1 = lax.dynamic_slice_in_dim(
        jnp.stack([mask_all[:, piv[2]], mask_all[:, piv[3]]], axis=1), row_id * row_blocks, row_blocks, 0
    )
    cp1 = col_panels[:, 2 * BS:] - dot(w0, corner_x) * spread(mask_rows_p1q1)
    lower1 = dot(cp1, diag_inverse[0, 1])
    w1 = lower1 * alive1_rows[:, None]
    rp0 = row_panels[: 2 * BS]
    lower0_p1q1 = dot(corner_y, diag_inverse[0, 0])
    mask_p1q1_cols = lax.dynamic_slice_in_dim(
        jnp.stack([mask_all[piv[2]], mask_all[piv[3]]], axis=0), col_id * col_blocks, col_blocks, 1
    )
    rp1 = row_panels[2 * BS:] - dot(lower0_p1q1, rp0) * spread(mask_p1q1_cols * alive0_cb[None, :])

    lowers = jnp.concatenate([w0, w1], axis=1)
    uppers = jnp.concatenate([rp0 * alive0_cols[None, :], rp1 * alive1_cols[None, :]], axis=0)
    update = dot(lowers, uppers)
    fresh = assembled - update * spread(mask_local)

    replaced = [(piv[0], lower0[:, :BS], alive0_rows), (piv[1], lower0[:, BS:], alive0_rows),
                (piv[2], lower1[:, :BS], alive1_rows), (piv[3], lower1[:, BS:], alive1_rows)]
    for blk, values, live in replaced:
        slot = blk % col_blocks
        current = lax.dynamic_slice_in_dim(fresh, slot * BS, BS, 1)
        written = jnp.where((live[:, None] > 0) & (col_id == blk // col_blocks), values, current)
        fresh = lax.dynamic_update_slice_in_dim(fresh, written, slot * BS, 1)
    return fresh[None]


def solution(mesh):
    placed = (
        P("front", "row", "col"),
        P("front", "row", "col"),
        P("front"),
        P("front", None),
        P("front", None, None),
        P("front", None),
        P("front", None, None, None),
    )
    return jax.shard_map(
        body, mesh=mesh, in_specs=placed, out_specs=P("front", "row", "col"), check_vma=False
    )
```

time: 605 us -> 614 us (1.015)
  waiting for transfers between devices: 400 us -> 369 us
  local copies, waits for them, and re-layouts: 62.3 us -> 81 us
  matrix products: 58.1 us -> 73.1 us
  blocking collectives: 14.4 us -> 0 us
  starting transfers between devices: 0.42 us -> 12.1 us
  other arithmetic: 35.3 us -> 44.5 us
    all_gather x2 -> x1, waiting for transfers between devices: 105 us -> 74.4 us  [body(): gathered = lax.all_gather(best_piece, ('row', 'col'), axis=0, tiled=False)]
    ppermute x0 -> x6, waiting for transfers between devices: none -> 16.2 us  [the longest x3 16.2 us: body(): got_tags = lax.ppermute(tags, 'front', perm)]
    dot_general x4 -> x6, matrix products: 58.1 us -> 73.1 us  [dot(): return jnp.dot(a, b, precision=HIGH, preferred_element_type=jnp.float32)]
    psum x4 -> x2, waiting for transfers between devices: 293 us -> 279 us  [the longest x1 177 us: body(): col_panels = lax.psum(jnp.concatenate(col_parts, axis=1), 'col')]
    transpose x1 -> x0, local copies, waits for them, and re-layouts: 12 us -> none  [body(): jnp.sum(picked, axis=0).transpose(0, 2, 1, 3).reshape(loc_rows, loc_cols)]
    ppermute x0 -> x6, starting transfers between devices: none -> 11.8 us  [the longest x3 6.49 us: body(): got_piece = lax.ppermute(piece, 'front', perm)]
    select_n x0 -> x1, local copies, waits for them, and re-layouts: none -> 10.4 us  [body(): picked = jnp.where(keep[:, :, None, None], picked, 0.0)]
    dynamic_update_slice x0 -> x1, local copies, waits for them, and re-layouts: none -> 9.24 us  [body(): fresh = lax.dynamic_update_slice_in_dim(fresh, written, slot * BS, 1)]
  transfers between devices with their start and end apart: 6 -> 9, of which waited for: 6 -> 5; matrix products, arithmetic and copies ran while one was open for 9% -> 8% of each run, Pallas kernels for 0% -> 0%
where the time goes in v1:
time: 614 us; the launch traced here: 608 us
  waiting for transfers between devices  369 us (60%)
  local copies, waits for them, and re-layouts  81 us (13%)
  matrix products  73.1 us (12%)
  other arithmetic  44.5 us (7%)
  between operations  27.7 us (5%)
  starting transfers between devices  12.1 us (2%)
    psum x1, waiting for transfers between devices, body(): col_panels = lax.psum(jnp.concatenate(col_parts, axis=1), 'col')  177 us
    psum x1, waiting for transfers between devices, body(): row_payload = lax.psum(row_payload, 'row')  102 us
    all_gather x1, waiting for transfers between devices, body(): gathered = lax.all_gather(best_piece, ('row', 'col'), axis=0, tiled=False)  74.4 us
    dot_general x6, matrix products, dot(): return jnp.dot(a, b, precision=HIGH, preferred_element_type=jnp.float32)  73.1 us
    unnamed x50, local copies, waits for them, and re-layouts  43.2 us
    ppermute x3, waiting for transfers between devices, body(): got_tags = lax.ppermute(tags, 'front', perm)  16.2 us
  transfers between devices with their start and end apart: 9, of which 5 were waited for; matrix products, arithmetic and copies ran while one was open for 8% of the time, Pallas kernels for 0%

profile of v1, /device:TPU:1, one launch (start us, length us, event | category | flops | bytes accessed | tf_op | source)
XLA Modules:
  0.0 607.6 jit_solution(11421719632197137091)
XLA Ops:
  6.5 2.5 collective-permute-start.5
  9.0 3.3 collective-permute-start.4
  12.3 0.7 collective-permute-start.3
  13.7 0.7 pad_add_fusion
  14.4 0.7 collective-permute-start.2
  15.1 0.4 collective-permute-start.1
  15.6 15.6 %collective-permute-done.2 = s32[9]{0:T(128)S(1)} collective-permute-done((s32[9]{0:T(128)S(1)}, s32[9]{0:T(128)S(1)}, u32[]{:S(2)}, u32[]{:S(2)}) %collective-permute-start.2) | collective-permute-done | bytes 68 | tf_op jit(solution)/shard_map/ppermute | solution.py:41
  31.2 4.2 collective-permute-start
  35.5 0.6 collective-permute-done
  36.2 2.0 select_select_fusion
  38.3 1.5 fusion.51
  50.2 0.7 convert_element_type.10
  51.0 0.1 copy.19
  51.1 0.6 broadcast_in_dim.170
  51.7 7.5 %copy.30 = f32[128,8,8,256]{3,1,2,0:T(8,128)} copy(f32[128,8,8,256]{3,2,1,0:T(8,128)S(1)} %bitcast.98) | data formatting | bytes 16777216
  59.2 9.8 %copy.20 = f32[1,2048,1024]{1,2,0:T(8,128)} copy(f32[1,2048,1024]{2,1,0:T(8,128)} %param.7) | data formatting | bytes 16777216 | tf_op args[0]
  69.2 0.2 fusion.37
  69.4 0.1 fusion.36
  69.5 0.1 reshape.174
  69.6 0.2 compare_reduce_fusion.1
  69.8 0.1 compare_reduce_fusion
  70.0 74.4 %all-gather.3.cloned.1.call-done = f32[16384,256]{1,0:T(8,128)} async-done(((f32[512,256]{1,0:T(8,128)}), f32[16384,256]{1,0:T(8,128)}) %all-gather.3.cloned.1.call-update) | async-done | bytes 16777232 | tf_op jit(solution)/shard_map/all_gather | solution.py:57
  144.4 10.1 %gather_fusion = f32[32,256,256]{2,1,0:T(8,128)} fusion(f32[4,8,2,256,1,256]{5,3,2,1,0,4:T(8,128)} %bitcast.105, s32[32]{0:T(128)S(1)} %reshape.174), kind=kCustom, calls=%fused_computation | custom fusion | bytes 16777728 | tf_op jit(solution)/shard_map/gather | solution.py:59
  154.5 7.9 %select_bitcast_fusion = f32[8,256,4,256]{3,1,2,0:T(8,128)} fusion(f32[8,4,256,256]{3,2,1,0:T(8,128)} %bitcast.97, pred[8,4]{1,0:T(8,128)(4,1)S(1)} %broadcast_and_fusion.4), kind=kLoop, calls=%fused_computation.9 | loop fusion | flops 2097152 | bytes 16777248 | tf_op jit(solution)/shard_map/jit(_where)/select_n | solution.py:68
  162.3 10.4 %copy.21 = f32[8,256,4,256]{1,0,3,2:T(8,128)} copy(f32[8,256,4,256]{3,1,2,0:T(8,128)} %select_bitcast_fusion) | data formatting | bytes 16777216 | tf_op jit(solution)/shard_map/jit(_where)/select_n | solution.py:68
  172.8 11.0 %copy.31 = f32[128,8,8,256]{3,1,2,0:T(8,128)} copy(f32[128,8,8,256]{3,2,1,0:T(8,128)} %bitcast.99) | data formatting | bytes 16777216
  183.8 7.3 %fusion.4 = f32[2048,1024]{0,1:T(8,128)S(1)} fusion(f32[2048,1024]{0,1:T(8,128)S(1)} %bitcast.89, f32[2048,1024]{0,1:T(8,128)} %bitcast.100, f32[1,2048,1024]{1,2,0:T(8,128)} %copy.20), kind=kLoop, calls=%fused_computation.7 | loop fusion | flops 4194304 | bytes 33554432 | tf_op jit(solution)/shard_map/mul | solution.py:75
  191.1 1.7 dynamic-slice_select_fusion.3
  192.8 2.1 copy-done
  194.9 3.7 pad_maximum_fusion
  198.6 0.2 all-reduce.5.cloned.1.call-start
  199.0 2.3 select_dynamic-update-slice_fusion.3
  201.3 2.3 select_dynamic-update-slice_fusion.2
  203.6 2.3 select_dynamic-update-slice_fusion.1
  205.9 2.3 select_dynamic-update-slice_fusion
  208.2 176.6 %all-reduce.3.cloned.1.call-done = f32[2048,1024]{0,1:T(8,128)} async-done(((f32[2048,1024]{0,1:T(8,128)}), f32[2048,1024]{0,1:T(8,128)}) %all-reduce.3.cloned.1.call-update) | async-done | bytes 8388624 | tf_op jit(solution)/shard_map/psum | solution.py:89
  384.8 4.0 fusion.50
  388.9 0.3 dynamic-slice_select_fusion.5
  389.1 1.7 fusion.20
  390.9 0.6 copy-done.6
  391.5 0.1 select_reduce_fusion
  395.0 0.1 copy.23
  395.1 0.6 broadcast_in_dim.191
  395.7 1.6 copy.36
  397.3 0.2 dynamic-slice_reduce_fusion.1
  397.5 0.3 broadcast_in_dim.188
  397.9 4.1 copy.33
  402.0 1.0 copy-done.5
  403.0 9.4 %broadcast_multiply_fusion.1 = (f32[2048,512]{0,1:T(8,128)}, f32[2048,512]{0,1:T(8,128)}) fusion(f32[2048]{0:T(1024)S(1)} %bitcast.112, f32[1,2,512,512]{3,2,1,0:T(8,128)S(1)} %copy-done.5, f32[2048,1024]{0,1:T(8,128)S(1)} %bitcast.94), kind=kOutput, calls=%fused_computation.32 | convolution fusion | flops 6443499520 | bytes 13639680 | tf_op jit(solution)/shard_map/dot_general | solution.py:13
  412.4 102.0 %all-reduce.5.cloned.1.call-done = f32[1536,1024]{0,1:T(8,128)} async-done(((f32[1536,1024]{0,1:T(8,128)}), f32[1536,1024]{0,1:T(8,128)}) %all-reduce.5.cloned.1.call-update) | async-done | bytes 6291472 | tf_op jit(solution)/shard_map/psum | solution.py:100
  514.4 4.2 fusion.25
  518.6 3.3 slice_multiply_fusion
  522.0 9.0 %fusion.27 = f32[2048,512]{0,1:T(8,128)S(1)} fusion(f32[2048,512]{0,1:T(8,128)S(1)} %copy-done.1, f32[1536,1024]{0,1:T(8,128)} %all-reduce.5.cloned.1.call-done), kind=kOutput, calls=%fused_computation.42 | convolution fusion | flops 6442450944 | bytes 9437184 | tf_op jit(solution)/shard_map/dot_general | solution.py:13
  531.1 12.1 %broadcast_multiply_fusion = (f32[2048,512]{0,1:T(8,128)}, f32[2048,512]{0,1:T(8,128)}) fusion(f32[2048]{0:T(1024)S(1)} %bitcast.110, f32[1,2,512,512]{3,2,1,0:T(8,128)} %param.13, f32[2048,512]{0,1:T(8,128)S(1)} %fusion.27, f32[2048,512]{0,1:T(8,128)} %bitcast.101, f32[2048,1024]{0,1:T(8,128)S(1)} %bitcast.96), kind=kOutput, calls=%fused_computation.31 | convolution fusion | flops 6445596672 | bytes 22028288 | tf_op jit(solution)/shard_map/dot_general | solution.py:13
  543.1 7.6 %fusion.18 = f32[512,1024]{0,1:T(8,128)} fusion(f32[1536,1024]{0,1:T(8,128)} %all-reduce.5.cloned.1.call-done, f32[512,1024]{0,1:T(8,128)S(1)} %bitcast.103, f32[512,512]{1,0:T(8,128)} %fusion.25, f32[1024]{0:T(1024)S(1)} %bitcast.113), kind=kOutput, calls=%fused_computation.26 | convolution fusion | flops 3222798336 | bytes 9441280 | tf_op jit(solution)/shard_map/dot_general | solution.py:13
  550.8 30.8 %multiply_subtract_fusion = f32[2048,1024]{0,1:T(8,128)S(1)} fusion(f32[2048,1024]{0,1:T(8,128)S(1)} %bitcast.85, f32[2048,1024]{0,1:T(8,128)S(1)} %bitcast.92, f32[2048,512]{0,1:T(8,128)} %get-tuple-element.33, f32[2048,512]{0,1:T(8,128)} %get-tuple-element.31, f32[512,1024]{0,1:T(8,128)} %fusion.18, f32[512,1024]{0,1:T(8,128)} %slice_multiply_fusion), kind=kOutput, calls=%fused_computation.8 | convolution fusion | flops 25777143808 | bytes 37748736 | tf_op jit(solution)/shard_map/dot_general | solution.py:13
  581.6 2.2 fusion.17
  583.8 0.6 copy-done.2
  584.4 0.5 fusion.16
  584.9 1.3 copy-done.3
  586.1 0.5 fusion.15
  586.6 3.3 copy.47
  589.9 1.8 fusion.14
  591.7 9.2 %copy.26 = f32[1,2048,1024]{2,1,0:T(8,128)} copy(f32[1,2048,1024]{1,2,0:T(8,128)} %fusion.14) | data formatting | bytes 16777216 | tf_op jit(solution)/shard_map/dynamic_update_slice | solution.py:138
  (76 shorter events, 1.4 us)
Async XLA Ops:
  6.5 137.8 %all-gather.3.cloned.1.call-start = ((), (), s32[]{:S(2)}) async-start(), calls=%async_computation.2 | async-start | bytes 17301504 | tf_op jit(solution)/shard_map/all_gather | solution.py:57
  6.5 29.6 %collective-permute-start.5 = (f32[512,256]{1,0:T(8,128)}, f32[512,256]{1,0:T(8,128)S(1)}, u32[]{:S(2)}, u32[]{:S(2)}) collective-permute-start(f32[512,256]{1,0:T(8,128)} %bitcast.106), channel_id=1, source_target_pairs={{0,32},{32,64},{64,96},{96,0},{1,33},{33,65},{65,97},{97,1},{2,34}... | collective-permute-start | bytes 1572872 | tf_op jit(solution)/shard_map/ppermute | solution.py:40
  9.0 27.2 %collective-permute-start.4 = (f32[512,256]{1,0:T(8,128)}, f32[512,256]{1,0:T(8,128)S(1)}, u32[]{:S(2)}, u32[]{:S(2)}) collective-permute-start(f32[512,256]{1,0:T(8,128)} %bitcast.107), channel_id=1, source_target_pairs={{0,64},{32,96},{64,0},{96,32},{1,65},{33,97},{65,1},{97,33},{2,66}... | collective-permute-start | bytes 1572872 | tf_op jit(solution)/shard_map/ppermute | solution.py:40
  12.3 23.9 %collective-permute-start.3 = (f32[512,256]{1,0:T(8,128)}, f32[512,256]{1,0:T(8,128)S(1)}, u32[]{:S(2)}, u32[]{:S(2)}) collective-permute-start(f32[512,256]{1,0:T(8,128)} %bitcast.108), channel_id=1, source_target_pairs={{0,96},{32,0},{64,32},{96,64},{1,97},{33,1},{65,33},{97,65},{2,98}... | collective-permute-start | bytes 1572872 | tf_op jit(solution)/shard_map/ppermute | solution.py:40
  14.4 16.8 %collective-permute-start.2 = (s32[9]{0:T(128)S(1)}, s32[9]{0:T(128)S(1)}, u32[]{:S(2)}, u32[]{:S(2)}) collective-permute-start(s32[9]{0:T(128)S(1)} %pad_add_fusion), channel_id=1, source_target_pairs={{0,32},{32,64},{64,96},{96,0},{1,33},{33,65},{65,97},{97,1},{2,34}... | collective-permute-start | bytes 116 | tf_op jit(solution)/shard_map/ppermute | solution.py:41
  15.1 20.3 %collective-permute-start.1 = (s32[9]{0:T(128)S(1)}, s32[9]{0:T(128)S(1)}, u32[]{:S(2)}, u32[]{:S(2)}) collective-permute-start(s32[9]{0:T(128)S(1)} %pad_add_fusion), channel_id=1, source_target_pairs={{0,64},{32,96},{64,0},{96,32},{1,65},{33,97},{65,1},{97,33},{2,66}... | collective-permute-start | bytes 116 | tf_op jit(solution)/shard_map/ppermute | solution.py:41
  31.2 4.9 collective-permute-start
  38.2 346.6 %all-reduce.3.cloned.1.call-start = ((), (), s32[]{:S(2)}) async-start(), calls=%async_computation | async-start | bytes 16777216 | tf_op jit(solution)/shard_map/psum | solution.py:89
  59.2 9.8 %copy-start.7 = (s32[1,8]{1,0:T(1,128)S(1)}, s32[1,8]{1,0:T(1,128)}, u32[]{:S(2)}) copy-start(s32[1,8]{1,0:T(1,128)} %param.10) | copy-start | bytes 100
  172.7 11.0 %slice-start.2 = ((s8[8388608]{0:T(1024)(128)(4,1)}), s8[4194304]{0:T(1024)(128)(4,1)S(1)}, s32[]{:S(2)}) async-start(s8[8388608]{0:T(1024)(128)(4,1)} %bitcast.87), calls=%async_computation.5 | async-start | bytes 8388608
  172.8 11.0 %slice-start.3 = ((s8[8388608]{0:T(1024)(128)(4,1)}), s8[4194304]{0:T(1024)(128)(4,1)S(1)}, s32[]{:S(2)}) async-start(s8[8388608]{0:T(1024)(128)(4,1)} %bitcast.87), calls=%async_computation.6 | async-start | bytes 8388608
  191.1 3.8 copy-start
  198.6 315.8 %all-reduce.5.cloned.1.call-start = ((), (), s32[]{:S(2)}) async-start(), calls=%async_computation.1 | async-start | bytes 12582912 | tf_op jit(solution)/shard_map/psum | solution.py:100
  390.9 0.7 copy-start.6
  395.7 6.4 %slice-start.6 = ((s8[8388608]{0:T(1024)(128)(4,1)}), s8[4194304]{0:T(1024)(128)(4,1)S(1)}, s32[]{:S(2)}) async-start(s8[8388608]{0:T(1024)(128)(4,1)} %bitcast.93), calls=%async_computation.9 | async-start | bytes 8388608
  397.5 4.5 slice-start.7
  397.9 5.1 copy-start.5
  514.4 7.5 %copy-start.1 = (f32[2048,512]{0,1:T(8,128)S(1)}, f32[2048,512]{0,1:T(8,128)}, u32[]{:S(2)}) copy-start(f32[2048,512]{0,1:T(8,128)} %get-tuple-element.31) | copy-start | bytes 12582916
  518.6 12.4 %slice-start.8 = ((s8[8388608]{0:T(1024)(128)(4,1)}), s8[4194304]{0:T(1024)(128)(4,1)S(1)}, s32[]{:S(2)}) async-start(s8[8388608]{0:T(1024)(128)(4,1)} %bitcast.95), calls=%async_computation.11 | async-start | bytes 8388608
  522.0 9.0 %slice-start.9 = ((s8[8388608]{0:T(1024)(128)(4,1)}), s8[4194304]{0:T(1024)(128)(4,1)S(1)}, s32[]{:S(2)}) async-start(s8[8388608]{0:T(1024)(128)(4,1)} %bitcast.95), calls=%async_computation.12 | async-start | bytes 8388608
  531.0 19.7 %slice-start = ((s8[8388608]{0:T(1024)(128)(4,1)}), s8[4194304]{0:T(1024)(128)(4,1)S(1)}, s32[]{:S(2)}) async-start(s8[8388608]{0:T(1024)(128)(4,1)} %bitcast.84), calls=%async_computation.3 | async-start | bytes 8388608
  531.0 19.7 %slice-start.4 = ((s8[8388608]{0:T(1024)(128)(4,1)}), s8[4194304]{0:T(1024)(128)(4,1)S(1)}, s32[]{:S(2)}) async-start(s8[8388608]{0:T(1024)(128)(4,1)} %bitcast.90), calls=%async_computation.7 | async-start | bytes 8388608
  531.0 12.1 %copy-start.4 = (f32[128,8,2,256]{3,1,2,0:T(8,128)S(1)}, f32[128,8,2,256]{3,1,2,0:T(8,128)}, u32[]{:S(2)}) copy-start(f32[128,8,2,256]{3,1,2,0:T(8,128)} %copy.36) | copy-start | bytes 6291460
  531.0 19.7 %slice-start.1 = ((s8[8388608]{0:T(1024)(128)(4,1)}), s8[4194304]{0:T(1024)(128)(4,1)S(1)}, s32[]{:S(2)}) async-start(s8[8388608]{0:T(1024)(128)(4,1)} %bitcast.84), calls=%async_computation.4 | async-start | bytes 8388608
  531.1 19.7 %slice-start.5 = ((s8[8388608]{0:T(1024)(128)(4,1)}), s8[4194304]{0:T(1024)(128)(4,1)S(1)}, s32[]{:S(2)}) async-start(s8[8388608]{0:T(1024)(128)(4,1)} %bitcast.90), calls=%async_computation.8 | async-start | bytes 8388608
  581.6 2.8 copy-start.2
  583.8 2.3 copy-start.3
Sparse Core Ops, SparseCore 0:
  38.4 105.9 all-gather.2
  198.7 186.0 all-reduce.2
  391.0 123.3 all-reduce.4

commit v2 on v1

--- a/solution.py
+++ b/solution.py
@@ -82,25 +82,55 @@
     alive1 = (position >= 4).astype(jnp.float32)
     piv = [order[k] for k in range(4)]
 
-    col_parts = []
-    for blk in piv:
-        piece_c = lax.dynamic_slice_in_dim(assembled, (blk % col_blocks) * BS, BS, 1)
-        col_parts.append(jnp.where(col_id == blk // col_blocks, piece_c, 0.0))
-    col_panels = lax.psum(jnp.concatenate(col_parts, axis=1), "col")
-
-    def rows_of(blk, cols):
-        strip = lax.dynamic_slice_in_dim(cols, (blk % row_blocks) * BS, BS, 0)
+    def rows_of(blk, mat):
+        strip = lax.dynamic_slice_in_dim(mat, (blk % row_blocks) * BS, BS, 0)
         return jnp.where(row_id == blk // row_blocks, strip, 0.0)
 
-    corner_x = jnp.concatenate([rows_of(piv[0], col_panels[:, 2 * BS:]), rows_of(piv[1], col_panels[:, 2 * BS:])], axis=0)
-    corner_y = jnp.concatenate([rows_of(piv[2], col_panels[:, :2 * BS]), rows_of(piv[3], col_panels[:, :2 * BS])], axis=0)
+    def xor_perm(n, bit):
+        return [(i, i ^ bit) for i in range(n)]
 
-    row_parts = [rows_of(blk, assembled) for blk in piv]
-    row_payload = jnp.concatenate(row_parts + [jnp.concatenate([corner_x, corner_y], axis=1)], axis=0)
-    row_payload = lax.psum(row_payload, "row")
-    row_panels = row_payload[: 4 * BS]
-    corner_x = row_payload[4 * BS:, : 2 * BS]
-    corner_y = row_payload[4 * BS:, 2 * BS:]
+    f_rows = jnp.concatenate([rows_of(blk, matrix_in) for blk in piv], axis=0)
+    f_rows = f_rows + lax.ppermute(f_rows, "row", xor_perm(row_count, 1))
+    half = f_rows.shape[0] // 2
+    core = row_id % 2
+    mine = jnp.where(core == 0, f_rows[:half], f_rows[half:])
+    mine = mine + lax.ppermute(mine, "row", xor_perm(row_count, 2))
+    other = lax.ppermute(mine, "row", xor_perm(row_count, 1))
+    f_rows = jnp.where(core == 0, jnp.concatenate([mine, other], axis=0), jnp.concatenate([other, mine], axis=0))
+
+    piv_arr = jnp.stack(piv)
+    pmatch = own_map[:, None] == piv_arr[None, :]
+    prow_src = jnp.sum(jnp.where(pmatch, block_ranks[:, None], 0), axis=0)
+    prow_has = jnp.any(pmatch, axis=0)
+    picked_rows = child_tiles[
+        (prow_src // kid_rows)[:, None],
+        (col_src // kid_cols)[None, :],
+        (prow_src % kid_rows)[:, None],
+        :,
+        (col_src % kid_cols)[None, :],
+        :,
+    ]
+    keep_rows = prow_has[:, None] & col_has[None, :]
+    picked_rows = jnp.where(keep_rows[:, :, None, None], picked_rows, 0.0)
+    placed_rows = picked_rows.transpose(0, 2, 1, 3).reshape(4 * BS, loc_cols)
+    mask_piv_rows = lax.dynamic_slice_in_dim(mask_all[piv_arr], col_id * col_blocks, col_blocks, 1)
+    row_panels = spread(mask_piv_rows) * (f_rows + placed_rows)
+
+    def cols_of(blk, mat):
+        strip = lax.dynamic_slice_in_dim(mat, (blk % col_blocks) * BS, BS, 1)
+        return jnp.where(col_id == blk // col_blocks, strip, 0.0)
+
+    corner_x = jnp.concatenate([cols_of(piv[2], row_panels[: 2 * BS]), cols_of(piv[3], row_panels[: 2 * BS])], axis=1)
+    corner_y = jnp.concatenate([cols_of(piv[0], row_panels[2 * BS:]), cols_of(piv[1], row_panels[2 * BS:])], axis=1)
+
+    col_parts = [cols_of(blk, assembled) for blk in piv]
+    col_payload = jnp.concatenate(
+        [jnp.concatenate(col_parts, axis=1), jnp.concatenate([corner_x, corner_y], axis=1)], axis=0
+    )
+    col_payload = lax.psum(col_payload, "col")
+    col_panels = col_payload[:loc_rows]
+    corner_x = col_payload[loc_rows:, : 2 * BS]
+    corner_y = col_payload[loc_rows:, 2 * BS:]
 
     alive0_rows = jnp.repeat(lax.dynamic_slice_in_dim(alive0, row_id * row_blocks, row_blocks), BS)
     alive1_rows = jnp.repeat(lax.dynamic_slice_in_dim(alive1, row_id * row_blocks, row_blocks), BS)

time: 614 us -> 615 us (level)
  waiting for transfers between devices: 369 us -> 325 us
  local copies, waits for them, and re-layouts: 81 us -> 109 us
  other arithmetic: 44.5 us -> 60.2 us
    ppermute x0 -> x3, waiting for transfers between devices: none -> 64.9 us  [the longest x1 64.9 us: body(): mine = mine + lax.ppermute(mine, 'row', xor_perm(row_count, 2))]
    psum x2 -> x1, waiting for transfers between devices: 279 us -> 217 us  [body(): col_payload = lax.psum(col_payload, 'col')]
    all_gather x1, waiting for transfers between devices: 74.4 us -> 26.5 us  [body(): gathered = lax.all_gather(best_piece, ('row', 'col'), axis=0, tiled=False)]
    reshape x0 -> x1, local copies, waits for them, and re-layouts: none -> 17.4 us  [body(): gathered.reshape(row_count, col_count, kid_rows, BS, kid_cols, BS)]
    gather x1 -> x2, local copies, waits for them, and re-layouts: 10.1 us -> 20.5 us  [body(): child_tiles[(row_src // kid_rows)[:, None], (col_src // kid_cols)[None, :...]
    unnamed x9 -> x1, other arithmetic: 9.22 us -> 0.01 us
    gather x0 -> x2, local copies, waits for them, and re-layouts: none -> 9.15 us  [the longest x1 8.59 us: body(): child_tiles[(prow_src // kid_rows)[:, None], (col_src // kid_cols)[None,...]
    add x0 -> x2, other arithmetic: none -> 7.04 us  [the longest x1 3.7 us: body(): mine = mine + lax.ppermute(mine, 'row', xor_perm(row_count, 2))]
  transfers between devices with their start and end apart: 9 -> 11, of which waited for: 5 -> 5; matrix products, arithmetic and copies ran while one was open for 8% -> 21% of each run, Pallas kernels for 0% -> 0%
where the time goes in v2:
time: 615 us; the launch traced here: 610 us
  waiting for transfers between devices  325 us (53%)
  local copies, waits for them, and re-layouts  109 us (18%)
  matrix products  72.3 us (12%)
  other arithmetic  60.2 us (10%)
  between operations  27.1 us (4%)
  starting transfers between devices  17.2 us (3%)
    psum x1, waiting for transfers between devices, body(): col_payload = lax.psum(col_payload, 'col')  217 us
    dot_general x6, matrix products, dot(): return jnp.dot(a, b, precision=HIGH, preferred_element_type=jnp.float32)  72.3 us
    ppermute x1, waiting for transfers between devices, body(): mine = mine + lax.ppermute(mine, 'row', xor_perm(row_count, 2))  64.9 us
    unnamed x47, local copies, waits for them, and re-layouts  43.3 us
    all_gather x1, waiting for transfers between devices, body(): gathered = lax.all_gather(best_piece, ('row', 'col'), axis=0, tiled=False)  26.5 us
    gather x2, local copies, waits for them, and re-layouts, body(): child_tiles[(row_src // kid_rows)[:, None], (col_src // kid_cols)[None, :...  20.5 us
    reshape x1, local copies, waits for them, and re-layouts, body(): gathered.reshape(row_count, col_count, kid_rows, BS, kid_cols, BS)  17.4 us
    ppermute x3, waiting for transfers between devices, body(): got_tags = lax.ppermute(tags, 'front', perm)  16 us
  transfers between devices with their start and end apart: 11, of which 5 were waited for; matrix products, arithmetic and copies ran while one was open for 21% of the time, Pallas kernels for 0%

profile of v2, /device:TPU:1, one launch (start us, length us, event | category | flops | bytes accessed | tf_op | source)
XLA Modules:
  0.0 610.3 jit_solution(1756604972807040928)
XLA Ops:
  6.5 1.2 copy.58
  7.8 2.5 collective-permute-start.5
  10.3 3.3 collective-permute-start.4
  13.6 0.7 collective-permute-start.3
  15.0 0.7 pad_add_fusion
  15.7 0.7 collective-permute-start.2
  16.5 0.4 collective-permute-start.1
  16.9 15.3 %collective-permute-done.2 = s32[9]{0:T(128)S(1)} collective-permute-done((s32[9]{0:T(128)S(1)}, s32[9]{0:T(128)S(1)}, u32[]{:S(2)}, u32[]{:S(2)}) %collective-permute-start.2) | collective-permute-done | bytes 68 | tf_op jit(solution)/shard_map/ppermute | solution.py:41
  32.3 4.2 collective-permute-start
  36.6 0.6 collective-permute-done
  37.3 1.1 select_select_fusion
  38.5 0.7 fusion.51
  49.0 9.3 %copy.57 = f32[1,2048,1024]{1,2,0:T(8,128)} copy(f32[1,2048,1024]{2,1,0:T(8,128)} %param.7) | data formatting | bytes 16777216 | tf_op args[0]
  58.4 2.6 select_bitcast_fusion.4
  61.0 2.6 pad_maximum_fusion
  63.6 2.6 collective-permute-start.6
  66.4 2.5 fusion.41
  69.0 0.6 gather_fusion.1
  69.9 0.6 broadcast_in_dim.236
  70.5 3.0 copy.87
  73.5 0.6 broadcast_in_dim.223
  74.1 7.5 %copy.85 = f32[128,8,8,256]{3,1,2,0:T(8,128)} copy(f32[128,8,8,256]{3,2,1,0:T(8,128)S(1)} %bitcast.135) | data formatting | bytes 16777216
  81.6 3.3 fusion.50
  85.0 1.9 copy-done.1
  86.9 0.5 slice_select_fusion.4
  87.4 1.3 collective-permute-start.7
  88.7 2.5 pad_add_fusion.1
  92.5 64.9 %collective-permute-done.7 = f32[512,1024]{0,1:T(8,128)} collective-permute-done((f32[512,1024]{0,1:T(8,128)S(1)}, f32[512,1024]{0,1:T(8,128)}, u32[]{:S(2)}, u32[]{:S(2)}) %collective-permute-start.7) | collective-permute-done | bytes 2097184 | tf_op jit(solution)/shard_map/ppermute | solution.py:97
  157.3 3.7 fusion.54
  161.0 1.3 collective-permute-start.8
  162.4 26.5 %all-gather.3.cloned.1.call-done = f32[16384,256]{0,1:T(8,128)} async-done(((f32[512,256]{0,1:T(8,128)}), f32[16384,256]{0,1:T(8,128)}) %all-gather.3.cloned.1.call-update) | async-done | bytes 16777232 | tf_op jit(solution)/shard_map/all_gather | solution.py:57
  188.8 17.4 %copy.80 = f32[16384,256]{1,0:T(8,128)} copy(f32[16384,256]{0,1:T(8,128)} %all-gather.3.cloned.1.call-done) | data formatting | bytes 33554432 | tf_op jit(solution)/shard_map/reshape | solution.py:58
  206.2 8.6 %gather_fusion.2 = f32[16,256,256]{2,1,0:T(8,128)} fusion(f32[4,8,2,256,1,256]{5,3,4,2,1,0:T(8,128)} %bitcast.131, s32[16]{0:T(128)S(1)} %reshape.414), kind=kCustom, calls=%fused_computation.2 | custom fusion | bytes 8388864 | tf_op jit(solution)/shard_map/gather | solution.py:105
  214.8 10.0 %gather_fusion = f32[32,256,256]{2,1,0:T(8,128)} fusion(f32[4,8,2,256,1,256]{5,3,4,2,1,0:T(8,128)} %bitcast.132, s32[32]{0:T(128)S(1)} %reshape.400), kind=kCustom, calls=%fused_computation | custom fusion | bytes 16777728 | tf_op jit(solution)/shard_map/gather | solution.py:59
  224.9 10.4 %copy.60 = f32[8,4,256,256]{2,0,3,1:T(8,128)} copy(f32[8,4,256,256]{3,2,1,0:T(8,128)} %bitcast.133) | data formatting | bytes 16777216 | tf_op jit(solution)/shard_map/gather | solution.py:59
  235.3 4.1 broadcast_select_fusion
  239.4 7.4 %copy.86 = f32[128,8,8,256]{3,1,2,0:T(8,128)} copy(f32[128,8,8,256]{3,2,1,0:T(8,128)S(1)} %bitcast.134) | data formatting | bytes 16777216
  246.8 2.5 select_bitcast_fusion
  249.2 5.3 copy.71
  254.5 3.2 copy.88
  257.7 9.7 %fusion.4 = f32[2048,1024]{0,1:T(8,128)S(1)} fusion(f32[2048,1024]{0,1:T(8,128)} %bitcast.129, f32[2048,1024]{0,1:T(8,128)} %bitcast.136, f32[1,2048,1024]{1,2,0:T(8,128)} %copy.57), kind=kLoop, calls=%fused_computation.9 | loop fusion | flops 4194304 | bytes 33554432 | tf_op jit(solution)/shard_map/mul | solution.py:75
  267.5 6.6 %fusion.11 = f32[1024,1024]{0,1:T(8,128)S(1)} fusion(f32[1024,1024]{0,1:T(8,128)S(1)} %bitcast.137, f32[1024,1024]{0,1:T(8,128)S(1)} %bitcast.139, f32[512,1024]{0,1:T(8,128)} %collective-permute-done.8, f32[512,1024]{0,1:T(8,128)S(1)} %fusion.54, pred[]{:T(512)S(6)} %eq.139), kind=kLoop, calls=%fused_computation.18 | loop fusion | flops 5242880 | bytes 16777216 | tf_op jit(solution)/shard_map/mul | solution.py:117
  274.1 2.4 broadcast_multiply_fusion.2
  276.5 0.3 copy-done.2
  277.0 1.7 dynamic-slice_select_fusion.3
  278.7 7.4 %maximum_maximum_fusion = f32[2560,1024]{0,1:T(8,128)} fusion(f32[512,256]{0,1:T(8,128)S(1)} %get-tuple-element.29, f32[512,256]{0,1:T(8,128)S(1)} %get-tuple-element.28, f32[512,256]{0,1:T(8,128)S(1)} %get-tuple-element.27, f32[512,256]{0,1:T(8,128)S(1)} %get-tuple-element.26, f32[2048,256]{0,1:T(8,128)S(1)} %get-tuple-element.16, ...), kind=kLoop, calls=%fused_computation.3 | loop fusion | flops 18350080 | bytes 20971520 | tf_op jit(solution)/shard_map/concatenate | solution.py:127
  289.1 0.6 broadcast_in_dim.251
  290.2 0.3 broadcast_in_dim.248
  290.5 3.9 copy.90
  294.5 217.2 %all-reduce.2.cloned.1.call-done = f32[2560,1024]{0,1:T(8,128)} async-done(((f32[2560,1024]{0,1:T(8,128)}), f32[2560,1024]{0,1:T(8,128)}) %all-reduce.2.cloned.1.call-update) | async-done | bytes 10485776 | tf_op jit(solution)/shard_map/psum | solution.py:130
  511.8 3.4 fusion.21
  515.2 6.9 %subtract_multiply_fusion = f32[512,1024]{0,1:T(8,128)} fusion(f32[512,1024]{0,1:T(8,128)S(1)} %bitcast.144, f32[512,512]{1,0:T(8,128)S(1)} %fusion.21, f32[1024]{0:T(1024)S(1)} %bitcast.154, f32[1024,1024]{0,1:T(8,128)} %copy-done.2), kind=kOutput, calls=%fused_computation.35 | convolution fusion | flops 3222798336 | bytes 9441280 | tf_op jit(solution)/shard_map/dot_general | solution.py:13
  522.0 10.5 %broadcast_multiply_fusion.1 = (f32[2048,512]{0,1:T(8,128)S(1)}, f32[2048,512]{0,1:T(8,128)}) fusion(f32[2048]{0:T(1024)S(1)} %bitcast.152, f32[1,2,512,512]{3,2,1,0:T(8,128)S(1)} %copy-done.9, f32[2560,1024]{0,1:T(8,128)} %all-reduce.2.cloned.1.call-done), kind=kOutput, calls=%fused_computation.37 | convolution fusion | flops 6443499520 | bytes 13639680 | tf_op jit(solution)/shard_map/dot_general | solution.py:13
  532.5 9.0 %fusion.23 = f32[2048,512]{0,1:T(8,128)S(1)} fusion(f32[2048,512]{0,1:T(8,128)S(1)} %get-tuple-element.44, f32[2560,1024]{0,1:T(8,128)} %all-reduce.2.cloned.1.call-done), kind=kOutput, calls=%fused_computation.44 | convolution fusion | flops 6442450944 | bytes 9437184 | tf_op jit(solution)/shard_map/dot_general | solution.py:13
  541.5 11.5 %broadcast_multiply_fusion = (f32[2048,512]{0,1:T(8,128)}, f32[2048,512]{0,1:T(8,128)}) fusion(f32[2048]{0:T(1024)S(1)} %bitcast.150, f32[1,2,512,512]{3,2,1,0:T(8,128)S(1)} %copy-done.9, f32[2560,1024]{0,1:T(8,128)} %all-reduce.2.cloned.1.call-done, f32[2048,512]{0,1:T(8,128)S(1)} %fusion.23, f32[2048,512]{0,1:T(8,128)S(1)} %bitcast.138), kind=kOutput, calls=%fused_computation.36 | convolution fusion | flops 6445596672 | bytes 22028288 | tf_op jit(solution)/shard_map/dot_general | solution.py:13
  553.0 31.0 %multiply_subtract_fusion = f32[2048,1024]{0,1:T(8,128)S(1)} fusion(f32[2048,1024]{0,1:T(8,128)S(1)} %bitcast.128, f32[2048,1024]{0,1:T(8,128)} %bitcast.130, f32[2048,512]{0,1:T(8,128)} %get-tuple-element.46, f32[2048,512]{0,1:T(8,128)S(1)} %get-tuple-element.44, f32[512,1024]{0,1:T(8,128)} %subtract_multiply_fusion, f32[512,1024]{0,1:T(8,128)} %get-tuple-element.23), kind=kOutput, calls=%fused_computation.10 | convolution fusion | flops 25777143808 | bytes 37748736 | tf_op jit(solution)/shard_map/dot_general | solution.py:13
  584.1 2.2 fusion.20
  586.3 0.6 copy-done.6
  586.9 0.5 fusion.19
  587.4 1.3 copy-done.5
  588.7 0.5 fusion.18
  589.1 3.2 copy.99
  592.4 1.6 fusion.17
  594.0 9.2 %copy.76 = f32[1,2048,1024]{2,1,0:T(8,128)} copy(f32[1,2048,1024]{1,2,0:T(8,128)} %fusion.17) | data formatting | bytes 16777216 | tf_op jit(solution)/shard_map/dynamic_update_slice | solution.py:168
  (87 shorter events, 3.3 us)
Async XLA Ops:
  6.5 31.9 %copy-start.11 = (s32[1,32]{1,0:T(1,128)S(1)}, s32[1,32]{1,0:T(1,128)}, u32[]{:S(2)}) copy-start(s32[1,32]{1,0:T(1,128)} %param.12) | copy-start | bytes 388
  6.5 182.3 %all-gather.3.cloned.1.call-start = ((), (), s32[]{:S(2)}) async-start(), calls=%async_computation.1 | async-start | bytes 17301504 | tf_op jit(solution)/shard_map/all_gather | solution.py:57
  7.8 29.5 %collective-permute-start.5 = (f32[512,256]{0,1:T(8,128)S(1)}, f32[512,256]{0,1:T(8,128)S(1)}, u32[]{:S(2)}, u32[]{:S(2)}) collective-permute-start(f32[512,256]{0,1:T(8,128)S(1)} %bitcast.146), channel_id=1, source_target_pairs={{0,32},{32,64},{64,96},{96,0},{1,33},{33,65},{65,97},{97,1},{2,34}... | collective-permute-start | bytes 1572872 | tf_op jit(solution)/shard_map/ppermute | solution.py:40
  10.3 27.0 %collective-permute-start.4 = (f32[512,256]{0,1:T(8,128)S(1)}, f32[512,256]{0,1:T(8,128)S(1)}, u32[]{:S(2)}, u32[]{:S(2)}) collective-permute-start(f32[512,256]{0,1:T(8,128)S(1)} %bitcast.147), channel_id=1, source_target_pairs={{0,64},{32,96},{64,0},{96,32},{1,65},{33,97},{65,1},{97,33},{2,66}... | collective-permute-start | bytes 1572872 | tf_op jit(solution)/shard_map/ppermute | solution.py:40
  13.6 23.7 %collective-permute-start.3 = (f32[512,256]{0,1:T(8,128)S(1)}, f32[512,256]{0,1:T(8,128)S(1)}, u32[]{:S(2)}, u32[]{:S(2)}) collective-permute-start(f32[512,256]{0,1:T(8,128)S(1)} %bitcast.148), channel_id=1, source_target_pairs={{0,96},{32,0},{64,32},{96,64},{1,97},{33,1},{65,33},{97,65},{2,98}... | collective-permute-start | bytes 1572872 | tf_op jit(solution)/shard_map/ppermute | solution.py:40
  15.7 16.5 %collective-permute-start.2 = (s32[9]{0:T(128)S(1)}, s32[9]{0:T(128)S(1)}, u32[]{:S(2)}, u32[]{:S(2)}) collective-permute-start(s32[9]{0:T(128)S(1)} %pad_add_fusion), channel_id=1, source_target_pairs={{0,32},{32,64},{64,96},{96,0},{1,33},{33,65},{65,97},{97,1},{2,34}... | collective-permute-start | bytes 116 | tf_op jit(solution)/shard_map/ppermute | solution.py:41
  16.5 20.1 %collective-permute-start.1 = (s32[9]{0:T(128)S(1)}, s32[9]{0:T(128)S(1)}, u32[]{:S(2)}, u32[]{:S(2)}) collective-permute-start(s32[9]{0:T(128)S(1)} %pad_add_fusion), channel_id=1, source_target_pairs={{0,64},{32,96},{64,0},{96,32},{1,65},{33,97},{65,1},{97,33},{2,66}... | collective-permute-start | bytes 116 | tf_op jit(solution)/shard_map/ppermute | solution.py:41
  32.3 5.0 collective-permute-start
  38.4 473.4 %all-reduce.2.cloned.1.call-start = ((), (), s32[]{:S(2)}) async-start(), calls=%async_computation | async-start | bytes 20971520 | tf_op jit(solution)/shard_map/psum | solution.py:130
  61.0 2.6 copy-start.8
  61.0 8.0 %copy-start.10 = (s32[1,32,32]{2,1,0:T(8,128)S(1)}, s32[1,32,32]{2,1,0:T(8,128)}, u32[]{:S(2)}) copy-start(s32[1,32,32]{2,1,0:T(8,128)} %param.11) | copy-start | bytes 12292
  63.6 18.0 %collective-permute-start.6 = (f32[1024,1024]{0,1:T(8,128)}, f32[1024,1024]{0,1:T(8,128)}, u32[]{:S(2)}, u32[]{:S(2)}) collective-permute-start(f32[1024,1024]{0,1:T(8,128)} %pad_maximum_fusion), channel_id=1, source_target_pairs={{0,8},{8,0},{16,24},{24,16},{1,9},{9,1},{17,25},{25,17},{2,10},{10... | collective-permute-start | bytes 12582920 | tf_op jit(solution)/shard_map/ppermute | solution.py:93
  84.9 1.9 copy-start.1
  86.9 4.3 copy-start.12
  87.4 70.0 %collective-permute-start.7 = (f32[512,1024]{0,1:T(8,128)S(1)}, f32[512,1024]{0,1:T(8,128)}, u32[]{:S(2)}, u32[]{:S(2)}) collective-permute-start(f32[512,1024]{0,1:T(8,128)S(1)} %slice_select_fusion.4), channel_id=1, source_target_pairs={{0,16},{8,24},{16,0},{24,8},{1,17},{9,25},{17,1},{25,9},{2,18},{10... | collective-permute-start | bytes 6291464 | tf_op jit(solution)/shard_map/ppermute | solution.py:97
  161.0 106.4 %collective-permute-start.8 = (f32[512,1024]{0,1:T(8,128)S(1)}, f32[512,1024]{0,1:T(8,128)}, u32[]{:S(2)}, u32[]{:S(2)}) collective-permute-start(f32[512,1024]{0,1:T(8,128)S(1)} %fusion.54), channel_id=1, source_target_pairs={{0,8},{8,0},{16,24},{24,16},{1,9},{9,1},{17,25},{25,17},{2,10},{10... | collective-permute-start | bytes 6291464 | tf_op jit(solution)/shard_map/ppermute | solution.py:98
  239.4 7.4 %copy-start.7 = (f32[16,256,256]{2,1,0:T(8,128)S(1)}, f32[16,256,256]{2,1,0:T(8,128)}, u32[]{:S(2)}) copy-start(f32[16,256,256]{2,1,0:T(8,128)} %gather_fusion.2) | copy-start | bytes 12582916
  257.7 9.8 %copy-start.3 = (f32[128,8,4,256]{3,1,2,0:T(8,128)S(1)}, f32[128,8,4,256]{3,1,2,0:T(8,128)}, u32[]{:S(2)}) copy-start(f32[128,8,4,256]{3,1,2,0:T(8,128)} %copy.87) | copy-start | bytes 12582916
  267.5 9.5 %copy-start = (f32[2048,1024]{0,1:T(8,128)}, f32[2048,1024]{0,1:T(8,128)S(1)}, u32[]{:S(2)}) copy-start(f32[2048,1024]{0,1:T(8,128)S(1)} %fusion.4) | copy-start | bytes 25165828
  274.1 2.7 copy-start.2
  515.1 6.9 %copy-start.9 = (f32[1,2,512,512]{3,2,1,0:T(8,128)S(1)}, f32[1,2,512,512]{3,2,1,0:T(8,128)}, u32[]{:S(2)}) copy-start(f32[1,2,512,512]{3,2,1,0:T(8,128)} %param.13) | copy-start | bytes 6291460
  532.5 9.0 %copy-start.4 = (f32[64,8,8,256]{3,1,2,0:T(8,128)S(1)}, f32[64,8,8,256]{3,1,2,0:T(8,128)}, u32[]{:S(2)}) copy-start(f32[64,8,8,256]{3,1,2,0:T(8,128)} %copy.90) | copy-start | bytes 12582916
  541.5 11.6 %slice-start = ((s8[8388608]{0:T(1024)(128)(4,1)}), s8[4194304]{0:T(1024)(128)(4,1)S(1)}, s32[]{:S(2)}) async-start(s8[8388608]{0:T(1024)(128)(4,1)} %bitcast.127), calls=%async_computation.2 | async-start | bytes 8388608
  541.5 11.5 %slice-start.1 = ((s8[8388608]{0:T(1024)(128)(4,1)}), s8[4194304]{0:T(1024)(128)(4,1)S(1)}, s32[]{:S(2)}) async-start(s8[8388608]{0:T(1024)(128)(4,1)} %bitcast.127), calls=%async_computation.3 | async-start | bytes 8388608
  584.1 2.8 copy-start.6
  586.3 2.3 copy-start.5
Sparse Core Ops, SparseCore 0:
  38.5 150.2 all-gather.2
  286.2 225.5 all-reduce.1

commit v3 on v2

--- a/solution.py
+++ b/solution.py
@@ -120,17 +120,37 @@
         strip = lax.dynamic_slice_in_dim(mat, (blk % col_blocks) * BS, BS, 1)
         return jnp.where(col_id == blk // col_blocks, strip, 0.0)
 
-    corner_x = jnp.concatenate([cols_of(piv[2], row_panels[: 2 * BS]), cols_of(piv[3], row_panels[: 2 * BS])], axis=1)
-    corner_y = jnp.concatenate([cols_of(piv[0], row_panels[2 * BS:]), cols_of(piv[1], row_panels[2 * BS:])], axis=1)
-
-    col_parts = [cols_of(blk, assembled) for blk in piv]
+    f_x = jnp.concatenate([cols_of(piv[2], f_rows[: 2 * BS]), cols_of(piv[3], f_rows[: 2 * BS])], axis=1)
+    f_y = jnp.concatenate([cols_of(piv[0], f_rows[2 * BS:]), cols_of(piv[1], f_rows[2 * BS:])], axis=1)
     col_payload = jnp.concatenate(
-        [jnp.concatenate(col_parts, axis=1), jnp.concatenate([corner_x, corner_y], axis=1)], axis=0
+        [jnp.concatenate([cols_of(blk, matrix_in) for blk in piv], axis=1), jnp.concatenate([f_x, f_y], axis=1)],
+        axis=0,
     )
     col_payload = lax.psum(col_payload, "col")
-    col_panels = col_payload[:loc_rows]
-    corner_x = col_payload[loc_rows:, : 2 * BS]
-    corner_y = col_payload[loc_rows:, 2 * BS:]
+
+    def child_blocks_at(rsrc, rhas, csrc, chas):
+        got = child_tiles[
+            (rsrc // kid_rows)[:, None],
+            (csrc // kid_cols)[None, :],
+            (rsrc % kid_rows)[:, None],
+            :,
+            (csrc % kid_cols)[None, :],
+            :,
+        ]
+        got = jnp.where((rhas[:, None] & chas[None, :])[:, :, None, None], got, 0.0)
+        nr, nc = got.shape[0], got.shape[1]
+        return got.transpose(0, 2, 1, 3).reshape(nr * BS, nc * BS)
+
+    mask_rows_local = lax.dynamic_slice_in_dim(mask_all, row_id * row_blocks, row_blocks, 0)
+    col_panels = spread(mask_rows_local[:, piv_arr]) * (
+        col_payload[:loc_rows] + child_blocks_at(row_src, row_has, prow_src, prow_has)
+    )
+    corner_x = spread(mask_all[piv_arr[:2]][:, piv_arr[2:]]) * (
+        col_payload[loc_rows:, : 2 * BS] + child_blocks_at(prow_src[:2], prow_has[:2], prow_src[2:], prow_has[2:])
+    )
+    corner_y = spread(mask_all[piv_arr[2:]][:, piv_arr[:2]]) * (
+        col_payload[loc_rows:, 2 * BS:] + child_blocks_at(prow_src[2:], prow_has[2:], prow_src[:2], prow_has[:2])
+    )
 
     alive0_rows = jnp.repeat(lax.dynamic_slice_in_dim(alive0, row_id * row_blocks, row_blocks), BS)
     alive1_rows = jnp.repeat(lax.dynamic_slice_in_dim(alive1, row_id * row_blocks, row_blocks), BS)

time: 615 us -> 565 us (0.919)
  waiting for transfers between devices: 325 us -> 204 us
  local copies, waits for them, and re-layouts: 109 us -> 156 us
  other arithmetic: 60.2 us -> 85 us
    psum x1, waiting for transfers between devices: 217 us -> 84.4 us  [body(): col_payload = lax.psum(col_payload, 'col')]
    gather x0 -> x13, local copies, waits for them, and re-layouts: none -> 26.5 us  [the longest x3 23.3 us: child_blocks_at(): child_tiles[(rsrc // kid_rows)[:, None], (csrc // kid_cols)[None, :], (rs...]
    unnamed x47 -> x62, local copies, waits for them, and re-layouts: 43.3 us -> 65.4 us
    select_n x0 -> x3, local copies, waits for them, and re-layouts: none -> 12.3 us  [the longest x1 10.7 us: body(): picked = jnp.where(keep[:, :, None, None], picked, 0.0)]
    select_n x1 -> x5, other arithmetic: 2.52 us -> 13.2 us  [the longest x3 8.17 us: child_blocks_at(): got = jnp.where((rhas[:, None] & chas[None, :])[:, :, None, None], got, 0.0)]
    gather x2 -> x1, local copies, waits for them, and re-layouts: 20.5 us -> 10.4 us  [body(): child_tiles[(row_src // kid_rows)[:, None], (col_src // kid_cols)[None, :...]
    ppermute x1, waiting for transfers between devices: 0.01 us -> 7.97 us  [body(): f_rows = f_rows + lax.ppermute(f_rows, 'row', xor_perm(row_count, 1))]
  transfers between devices with their start and end apart: 11 -> 11, of which waited for: 5 -> 7; matrix products, arithmetic and copies ran while one was open for 21% -> 34% of each run, Pallas kernels for 0% -> 0%
where the time goes in v3:
time: 565 us; the launch traced here: 557 us
  waiting for transfers between devices  204 us (36%)
  local copies, waits for them, and re-layouts  156 us (28%)
  other arithmetic  85 us (15%)
  matrix products  70.5 us (12%)
  between operations  27.3 us (5%)
  starting transfers between devices  14.1 us (2%)
    psum x1, waiting for transfers between devices, body(): col_payload = lax.psum(col_payload, 'col')  84.4 us
    dot_general x6, matrix products, dot(): return jnp.dot(a, b, precision=HIGH, preferred_element_type=jnp.float32)  70.5 us
    unnamed x62, local copies, waits for them, and re-layouts  65.4 us
    ppermute x1, waiting for transfers between devices, body(): mine = mine + lax.ppermute(mine, 'row', xor_perm(row_count, 2))  61.7 us
    all_gather x1, waiting for transfers between devices, body(): gathered = lax.all_gather(best_piece, ('row', 'col'), axis=0, tiled=False)  29.5 us
    gather x3, local copies, waits for them, and re-layouts, child_blocks_at(): child_tiles[(rsrc // kid_rows)[:, None], (csrc // kid_cols)[None, :], (rs...  23.3 us
    ppermute x3, waiting for transfers between devices, body(): got_tags = lax.ppermute(tags, 'front', perm)  20.7 us
    reshape x1, local copies, waits for them, and re-layouts, child_blocks_at(): return got.transpose(0, 2, 1, 3).reshape(nr * BS, nc * BS)  12.1 us
  transfers between devices with their start and end apart: 11, of which 7 were waited for; matrix products, arithmetic and copies ran while one was open for 34% of the time, Pallas kernels for 0%

profile of v3, /device:TPU:1, one launch (start us, length us, event | category | flops | bytes accessed | tf_op | source)
XLA Modules:
  0.0 557.2 jit_solution(2585331034705938660)
XLA Ops:
  6.5 4.6 collective-permute-start.3
  13.2 2.0 collective-permute-start
  15.2 1.8 collective-permute-start.1
  16.9 16.2 %collective-permute-done = s32[9]{0:T(128)S(1)} collective-permute-done((s32[9]{0:T(128)S(1)}, s32[9]{0:T(128)S(1)}, u32[]{:S(2)}, u32[]{:S(2)}) %collective-permute-start) | collective-permute-done | bytes 68 | tf_op jit(solution)/shard_map/ppermute | solution.py:41
  33.2 3.2 collective-permute-done.1
  36.4 1.3 collective-permute-done.2
  37.8 2.0 select_select_fusion
  39.9 1.5 fusion.75
  51.3 2.8 select_bitcast_fusion.12
  54.1 2.5 pad_maximum_fusion
  56.6 2.3 collective-permute-start.6
  58.9 8.0 %collective-permute-done.6 = f32[1024,1024]{1,0:T(8,128)} collective-permute-done((f32[1024,1024]{1,0:T(8,128)}, f32[1024,1024]{1,0:T(8,128)}, u32[]{:S(2)}, u32[]{:S(2)}) %collective-permute-start.6) | collective-permute-done | bytes 4194336 | tf_op jit(solution)/shard_map/ppermute | solution.py:93
  66.9 3.5 fusion.72
  70.4 1.9 copy-done
  72.8 1.3 collective-permute-start.7
  74.1 2.5 fusion.54
  77.9 3.0 copy.127
  81.0 61.7 %collective-permute-done.7 = f32[512,1024]{1,0:T(8,128)} collective-permute-done((f32[512,1024]{1,0:T(8,128)S(1)}, f32[512,1024]{1,0:T(8,128)}, u32[]{:S(2)}, u32[]{:S(2)}) %collective-permute-start.7) | collective-permute-done | bytes 2097184 | tf_op jit(solution)/shard_map/ppermute | solution.py:97
  142.6 5.2 fusion.78
  147.8 1.4 collective-permute-start.8
  149.2 2.5 pad_add_fusion.1
  151.7 6.5 %select_bitcast_fusion.6 = (f32[2048,256]{1,0:T(8,128)S(1)}, f32[2048,256]{1,0:T(8,128)}, f32[2048,256]{1,0:T(8,128)}, f32[2048,256]{1,0:T(8,128)}) fusion(f32[1,2048,1024]{2,1,0:T(8,128)} %param.7, s32[]{:T(128)S(6)} %select_n.624, pred[]{:T(512)S(6)} %eq.142, s32[]{:T(128)S(6)} %select_n.642, pred[]{:T(512)S(6)} %eq.145, s32[]{:T(128)S(6)} %select_n.636, ...), kind=kLoop, calls=%fused_computation.52 | loop fusion | flops 2097152 | bytes 16777236 | tf_op jit(solution)/shard_map/jit(_where)/select_n | solution.py:121
  159.1 29.5 %all-gather.3.cloned.1.call-done = f32[16384,256]{1,0:T(8,128)} async-done(((f32[512,256]{1,0:T(8,128)}), f32[16384,256]{1,0:T(8,128)}) %all-gather.3.cloned.1.call-update) | async-done | bytes 16777232 | tf_op jit(solution)/shard_map/all_gather | solution.py:57
  188.6 8.5 %gather_fusion.7 = f32[16,256,256]{2,1,0:T(8,128)} fusion(f32[4,8,2,256,1,256]{5,3,2,1,0,4:T(8,128)} %bitcast.183, s32[16]{0:T(128)S(1)} %reshape.741), kind=kCustom, calls=%fused_computation.7 | custom fusion | bytes 8388864 | tf_op jit(solution)/shard_map/gather | solution.py:105
  197.1 2.7 select_bitcast_fusion.2
  199.8 2.7 copy.105
  203.6 1.1 copy-done.6
  204.7 6.0 %add_multiply_fusion = (f32[1024,1024]{1,0:T(8,128)}, f32[1024,1024]{1,0:T(8,128)S(1)}) fusion(f32[1024,1024]{1,0:T(8,128)S(1)} %bitcast.193, f32[1024,1024]{1,0:T(8,128)S(1)} %bitcast.194, f32[512,1024]{1,0:T(8,128)} %fusion.78, f32[512,1024]{1,0:T(8,128)} %collective-permute-done.8, pred[]{:T(512)S(6)} %eq.146), kind=kLoop, calls=%fused_computation.32 | loop fusion | flops 5242880 | bytes 20971520 | tf_op jit(solution)/shard_map/mul | solution.py:117
  213.6 10.9 %maximum_maximum_fusion = f32[2560,1024]{1,0:T(8,128)} fusion(f32[512,256]{1,0:T(8,128)S(1)} %get-tuple-element.34, f32[512,256]{1,0:T(8,128)S(1)} %get-tuple-element.33, f32[512,256]{1,0:T(8,128)S(1)} %get-tuple-element.32, f32[512,256]{1,0:T(8,128)S(1)} %get-tuple-element.31, f32[2048,256]{1,0:T(8,128)S(1)} %copy-done.8, f32[2048,256]{1,0:T(8,128)S(1)} %copy-done.9, ...), kind=kLoop, calls=%fused_computation.11 | loop fusion | flops 18350080 | bytes 20971520 | tf_op jit(solution)/shard_map/concatenate | solution.py:125
  226.1 9.3 %copy.91 = f32[1,2048,1024]{1,2,0:T(8,128)} copy(f32[1,2048,1024]{2,1,0:T(8,128)} %param.7) | data formatting | bytes 16777216 | tf_op args[0]
  235.5 2.5 fusion.55
  242.9 1.8 copy.132
  245.6 1.1 broadcast_in_dim.201
  246.7 5.4 copy.120
  253.3 1.1 copy.123
  254.7 1.1 broadcast_in_dim.371
  255.9 2.5 copy.125
  259.3 7.5 %copy.118 = f32[128,8,8,256]{3,1,2,0:T(8,128)} copy(f32[128,8,8,256]{3,2,1,0:T(8,128)S(1)} %bitcast.178) | data formatting | bytes 16777216
  268.3 6.6 %gather_fusion.10 = f32[4,256,256]{2,1,0:T(8,128)S(1)} fusion(f32[4,8,2,256,1,256]{5,3,2,1,0,4:T(8,128)} %bitcast.184, s32[4]{0:T(128)S(1)} %reshape.763), kind=kCustom, calls=%fused_computation.10 | custom fusion | bytes 2097216 | tf_op jit(solution)/shard_map/gather | solution.py:132
  275.8 1.1 copy.131
  276.9 10.2 %gather_fusion.2 = f32[32,256,256]{2,1,0:T(8,128)} fusion(f32[4,8,2,256,1,256]{5,3,2,1,0,4:T(8,128)} %bitcast.185, s32[32]{0:T(128)S(1)} %reshape.705), kind=kCustom, calls=%fused_computation.2 | custom fusion | bytes 16777728 | tf_op jit(solution)/shard_map/gather | solution.py:132
  287.1 7.9 %select_bitcast_fusion = f32[8,256,4,256]{3,1,2,0:T(8,128)} fusion(f32[8,4,256,256]{3,2,1,0:T(8,128)} %bitcast.176, pred[8,4]{1,0:T(8,128)(4,1)S(1)} %get-tuple-element.54), kind=kLoop, calls=%fused_computation.21 | loop fusion | flops 2097152 | bytes 16777248 | tf_op jit(solution)/shard_map/jit(_where)/select_n | solution.py:140
  295.0 12.1 %copy.112 = f32[8,256,4,256]{3,2,1,0:T(4,128)} copy(f32[8,256,4,256]{3,1,2,0:T(8,128)} %select_bitcast_fusion) | data formatting | bytes 16777216 | tf_op jit(solution)/shard_map/reshape | solution.py:142
  307.1 8.7 %copy.121 = f32[256,8,4,256]{3,1,2,0:T(8,128)} copy(f32[256,8,4,256]{3,2,1,0:T(4,128)} %bitcast.179) | data formatting | bytes 16777216
  315.8 6.5 %gather_fusion.5 = f32[4,256,256]{2,1,0:T(8,128)S(1)} fusion(f32[4,8,2,256,1,256]{5,3,2,1,0,4:T(8,128)} %bitcast.186, s32[4]{0:T(128)S(1)} %reshape.727), kind=kCustom, calls=%fused_computation.5 | custom fusion | bytes 2097216 | tf_op jit(solution)/shard_map/gather | solution.py:132
  323.3 1.1 copy.124
  324.4 10.4 %gather_fusion = f32[32,256,256]{2,1,0:T(8,128)} fusion(f32[4,8,2,256,1,256]{5,3,2,1,0,4:T(8,128)} %bitcast.187, s32[32]{0:T(128)S(1)} %reshape.691), kind=kCustom, calls=%fused_computation | custom fusion | bytes 16777728 | tf_op jit(solution)/shard_map/gather | solution.py:59
  334.8 8.0 %select_bitcast_fusion.1 = f32[8,256,4,256]{3,1,2,0:T(8,128)} fusion(f32[8,4,256,256]{3,2,1,0:T(8,128)} %bitcast.175, pred[8,4]{1,0:T(8,128)(4,1)S(1)} %get-tuple-element.55), kind=kLoop, calls=%fused_computation.22 | loop fusion | flops 2097152 | bytes 16777248 | tf_op jit(solution)/shard_map/jit(_where)/select_n | solution.py:68
  342.8 10.7 %copy.92 = f32[8,256,4,256]{1,0,3,2:T(8,128)} copy(f32[8,256,4,256]{3,1,2,0:T(8,128)} %select_bitcast_fusion.1) | data formatting | bytes 16777216 | tf_op jit(solution)/shard_map/jit(_where)/select_n | solution.py:68
  353.4 11.0 %copy.119 = f32[128,8,8,256]{3,1,2,0:T(8,128)} copy(f32[128,8,8,256]{3,2,1,0:T(8,128)} %bitcast.180) | data formatting | bytes 16777216
  364.4 1.6 slice_multiply_fusion
  366.0 84.4 %all-reduce.2.cloned.1.call-done = f32[2560,1024]{1,0:T(8,128)} async-done(((f32[2560,1024]{1,0:T(8,128)}), f32[2560,1024]{1,0:T(8,128)}) %all-reduce.2.cloned.1.call-update) | async-done | bytes 10485776 | tf_op jit(solution)/shard_map/psum | solution.py:129
  450.4 9.9 %fusion = f32[2048,1024]{1,0:T(8,128)S(1)} fusion(f32[2048,1024]{1,0:T(8,128)} %bitcast.181, f32[2048,1024]{1,0:T(8,128)} %bitcast.182, f32[2560,1024]{1,0:T(8,128)} %all-reduce.2.cloned.1.call-done), kind=kLoop, calls=%fused_computation.13 | loop fusion | flops 4194304 | bytes 33554432 | tf_op jit(solution)/shard_map/mul | solution.py:145
  460.3 9.0 %broadcast_multiply_fusion.1 = (f32[2048,512]{0,1:T(8,128)S(1)}, f32[2048,512]{0,1:T(8,128)}) fusion(f32[2048]{0:T(1024)S(1)} %bitcast.214, f32[1,2,512,512]{3,2,1,0:T(8,128)S(1)} %copy-done.12, f32[2048,1024]{1,0:T(8,128)S(1)} %fusion), kind=kOutput, calls=%fused_computation.48 | convolution fusion | flops 6443499520 | bytes 13639680 | tf_op jit(solution)/shard_map/dot_general | solution.py:13
  469.3 8.2 %fusion.30 = f32[2048,512]{1,0:T(8,128)S(1)} fusion(f32[2048,512]{0,1:T(8,128)S(1)} %get-tuple-element.62, f32[512,512]{1,0:T(8,128)S(1)} %bitcast.198, f32[512,512]{1,0:T(8,128)S(1)} %bitcast.200, f32[2560,1024]{1,0:T(8,128)} %all-reduce.2.cloned.1.call-done), kind=kOutput, calls=%fused_computation.61 | convolution fusion | flops 6442975232 | bytes 11534336 | tf_op jit(solution)/shard_map/dot_general | solution.py:13
  477.5 11.7 %broadcast_multiply_fusion = (f32[2048,512]{0,1:T(8,128)}, f32[2048,512]{0,1:T(8,128)}) fusion(f32[2048]{0:T(1024)S(1)} %bitcast.212, f32[1,2,512,512]{3,2,1,0:T(8,128)} %param.13, f32[2048,1024]{1,0:T(8,128)S(1)} %fusion, f32[2048,512]{1,0:T(8,128)S(1)} %fusion.30, f32[2048,512]{1,0:T(8,128)S(1)} %bitcast.188), kind=kOutput, calls=%fused_computation.47 | convolution fusion | flops 6445596672 | bytes 22028288 | tf_op jit(solution)/shard_map/dot_general | solution.py:13
  489.3 4.2 fusion.27
  493.5 5.1 fusion.21
  498.6 32.3 %fusion.6 = f32[2048,1024]{0,1:T(8,128)S(1)} fusion(f32[2048,1024]{0,1:T(8,128)} %bitcast.173, f32[2048,1024]{0,1:T(8,128)} %bitcast.174, f32[1,2048,1024]{1,2,0:T(8,128)S(1)} %bitcast.172, f32[2048,512]{0,1:T(8,128)} %get-tuple-element.64, f32[2048,512]{0,1:T(8,128)S(1)} %get-tuple-element.62, f32[512,1024]{1,0:T(8,128)} %fusion.21, ...), kind=kOutput, calls=%fused_computation.20 | convolution fusion | flops 25781338112 | bytes 46137344 | tf_op jit(solution)/shard_map/dot_general | solution.py:13
  530.9 2.2 fusion.20
  534.2 1.2 copy-done.2
  535.9 3.3 copy.138
  539.2 1.7 fusion.17
  540.9 9.2 %copy.110 = f32[1,2048,1024]{2,1,0:T(8,128)} copy(f32[1,2048,1024]{1,2,0:T(8,128)} %fusion.17) | data formatting | bytes 16777216 | tf_op jit(solution)/shard_map/dynamic_update_slice | solution.py:188
  (137 shorter events, 20.3 us)
Async XLA Ops:
  6.5 182.0 %all-gather.3.cloned.1.call-start = ((), (), s32[]{:S(2)}) async-start(), calls=%async_computation.1 | async-start | bytes 17301504 | tf_op jit(solution)/shard_map/all_gather | solution.py:57
  6.5 31.2 %collective-permute-start.3 = (f32[512,256]{1,0:T(8,128)}, f32[512,256]{1,0:T(8,128)S(1)}, u32[]{:S(2)}, u32[]{:S(2)}) collective-permute-start(f32[512,256]{1,0:T(8,128)} %bitcast.207), channel_id=1, source_target_pairs={{0,96},{32,0},{64,32},{96,64},{1,97},{33,1},{65,33},{97,65},{2,98}... | collective-permute-start | bytes 1572872 | tf_op jit(solution)/shard_map/ppermute | solution.py:40
  11.1 26.7 %collective-permute-start.4 = (f32[512,256]{1,0:T(8,128)}, f32[512,256]{1,0:T(8,128)S(1)}, u32[]{:S(2)}, u32[]{:S(2)}) collective-permute-start(f32[512,256]{1,0:T(8,128)} %bitcast.208), channel_id=1, source_target_pairs={{0,64},{32,96},{64,0},{96,32},{1,65},{33,97},{65,1},{97,33},{2,66}... | collective-permute-start | bytes 1572872 | tf_op jit(solution)/shard_map/ppermute | solution.py:40
  11.1 26.7 %collective-permute-start.5 = (f32[512,256]{1,0:T(8,128)}, f32[512,256]{1,0:T(8,128)S(1)}, u32[]{:S(2)}, u32[]{:S(2)}) collective-permute-start(f32[512,256]{1,0:T(8,128)} %bitcast.209), channel_id=1, source_target_pairs={{0,32},{32,64},{64,96},{96,0},{1,33},{33,65},{65,97},{97,1},{2,34}... | collective-permute-start | bytes 1572872 | tf_op jit(solution)/shard_map/ppermute | solution.py:40
  13.2 19.9 %collective-permute-start = (s32[9]{0:T(128)S(1)}, s32[9]{0:T(128)S(1)}, u32[]{:S(2)}, u32[]{:S(2)}) collective-permute-start(s32[9]{0:T(128)S(1)} %pad_add_fusion), channel_id=1, source_target_pairs={{0,96},{32,0},{64,32},{96,64},{1,97},{33,1},{65,33},{97,65},{2,98}... | collective-permute-start | bytes 116 | tf_op jit(solution)/shard_map/ppermute | solution.py:41
  15.2 21.2 %collective-permute-start.1 = (s32[9]{0:T(128)S(1)}, s32[9]{0:T(128)S(1)}, u32[]{:S(2)}, u32[]{:S(2)}) collective-permute-start(s32[9]{0:T(128)S(1)} %pad_add_fusion), channel_id=1, source_target_pairs={{0,64},{32,96},{64,0},{96,32},{1,65},{33,97},{65,1},{97,33},{2,66}... | collective-permute-start | bytes 116 | tf_op jit(solution)/shard_map/ppermute | solution.py:41
  33.1 4.6 collective-permute-start.2
  39.8 410.5 %all-reduce.2.cloned.1.call-start = ((), (), s32[]{:S(2)}) async-start(), calls=%async_computation | async-start | bytes 20971520 | tf_op jit(solution)/shard_map/psum | solution.py:129
  54.1 2.5 copy-start.7
  56.6 10.3 %collective-permute-start.6 = (f32[1024,1024]{1,0:T(8,128)}, f32[1024,1024]{1,0:T(8,128)}, u32[]{:S(2)}, u32[]{:S(2)}) collective-permute-start(f32[1024,1024]{1,0:T(8,128)} %pad_maximum_fusion), channel_id=1, source_target_pairs={{0,8},{8,0},{16,24},{24,16},{1,9},{9,1},{17,25},{25,17},{2,10},{10... | collective-permute-start | bytes 12582920 | tf_op jit(solution)/shard_map/ppermute | solution.py:93
  70.4 2.0 copy-start
  72.4 4.3 copy-start.15
  72.8 69.9 %collective-permute-start.7 = (f32[512,1024]{1,0:T(8,128)S(1)}, f32[512,1024]{1,0:T(8,128)}, u32[]{:S(2)}, u32[]{:S(2)}) collective-permute-start(f32[512,1024]{1,0:T(8,128)S(1)} %slice_select_fusion.4), channel_id=1, source_target_pairs={{0,16},{8,24},{16,0},{24,8},{1,17},{9,25},{17,1},{25,9},{2,18},{10... | collective-permute-start | bytes 6291464 | tf_op jit(solution)/shard_map/ppermute | solution.py:97
  147.8 55.7 %collective-permute-start.8 = (f32[512,1024]{1,0:T(8,128)}, f32[512,1024]{1,0:T(8,128)}, u32[]{:S(2)}, u32[]{:S(2)}) collective-permute-start(f32[512,1024]{1,0:T(8,128)} %fusion.78), channel_id=1, source_target_pairs={{0,8},{8,0},{16,24},{24,16},{1,9},{9,1},{17,25},{25,17},{2,10},{10... | collective-permute-start | bytes 6291464 | tf_op jit(solution)/shard_map/ppermute | solution.py:98
  151.7 6.5 %copy-start.17 = (s32[1,8]{1,0:T(1,128)S(1)}, s32[1,8]{1,0:T(1,128)}, u32[]{:S(2)}) copy-start(s32[1,8]{1,0:T(1,128)} %param.10) | copy-start | bytes 100
  202.5 2.2 copy-start.6
  210.7 1.6 copy-start.10
  211.0 2.0 copy-start.8
  211.0 2.6 copy-start.9
  224.5 1.2 copy-start.16
  353.4 11.0 %copy-start.4 = (f32[1024,1024]{1,0:T(8,128)S(1)}, f32[1024,1024]{1,0:T(8,128)}, u32[]{:S(2)}) copy-start(f32[1024,1024]{1,0:T(8,128)} %get-tuple-element.17) | copy-start | bytes 12582916
  450.3 9.9 %copy-start.12 = (f32[1,2,512,512]{3,2,1,0:T(8,128)S(1)}, f32[1,2,512,512]{3,2,1,0:T(8,128)}, u32[]{:S(2)}) copy-start(f32[1,2,512,512]{3,2,1,0:T(8,128)} %param.13) | copy-start | bytes 6291460
  460.2 9.0 %copy-start.13 = (f32[64,8,2,256]{3,1,2,0:T(8,128)S(1)}, f32[64,8,2,256]{3,1,2,0:T(8,128)}, u32[]{:S(2)}) copy-start(f32[64,8,2,256]{3,1,2,0:T(8,128)} %copy.123) | copy-start | bytes 3145732
  460.2 9.0 %copy-start.14 = (f32[64,8,2,256]{3,1,2,0:T(8,128)S(1)}, f32[64,8,2,256]{3,1,2,0:T(8,128)}, u32[]{:S(2)}) copy-start(f32[64,8,2,256]{3,1,2,0:T(8,128)} %copy.124) | copy-start | bytes 3145732
  469.2 8.3 %copy-start.1 = (f32[256,8,2,256]{3,1,2,0:T(8,128)S(1)}, f32[256,8,2,256]{3,1,2,0:T(8,128)}, u32[]{:S(2)}) copy-start(f32[256,8,2,256]{3,1,2,0:T(8,128)} %copy.125) | copy-start | bytes 12582916
  477.5 21.1 %slice-start = ((s8[8388608]{0:T(1024)(128)(4,1)}), s8[4194304]{0:T(1024)(128)(4,1)S(1)}, s32[]{:S(2)}) async-start(s8[8388608]{0:T(1024)(128)(4,1)} %bitcast.171), calls=%async_computation.2 | async-start | bytes 8388608
  477.5 16.0 %copy-start.11 = (f32[64,8,4,256]{3,1,2,0:T(8,128)S(1)}, f32[64,8,4,256]{3,1,2,0:T(8,128)}, u32[]{:S(2)}) copy-start(f32[64,8,4,256]{3,1,2,0:T(8,128)} %copy.132) | copy-start | bytes 6291460
  477.5 21.1 %slice-start.1 = ((s8[8388608]{0:T(1024)(128)(4,1)}), s8[4194304]{0:T(1024)(128)(4,1)S(1)}, s32[]{:S(2)}) async-start(s8[8388608]{0:T(1024)(128)(4,1)} %bitcast.171), calls=%async_computation.3 | async-start | bytes 8388608
  489.3 4.3 copy-start.5
  530.9 2.8 copy-start.3
  533.1 2.3 copy-start.2
Sparse Core Ops, SparseCore 0:
  39.9 148.5 all-gather.2
  224.6 225.6 all-reduce.1

commit v4 on v3

--- a/solution.py
+++ b/solution.py
@@ -55,18 +55,20 @@
     row_src, row_has = locate(row_id * row_blocks, row_blocks)
     col_src, col_has = locate(col_id * col_blocks, col_blocks)
     gathered = lax.all_gather(best_piece, ("row", "col"), axis=0, tiled=False)
-    child_tiles = gathered.reshape(row_count, col_count, kid_rows, BS, kid_cols, BS)
-    picked = child_tiles[
-        (row_src // kid_rows)[:, None],
-        (col_src // kid_cols)[None, :],
-        (row_src % kid_rows)[:, None],
-        :,
-        (col_src % kid_cols)[None, :],
-        :,
-    ]
-    keep = row_has[:, None] & col_has[None, :]
-    picked = jnp.where(keep[:, :, None, None], picked, 0.0)
-    extended = picked.transpose(0, 2, 1, 3).reshape(loc_rows, loc_cols)
+    child4 = (
+        gathered.reshape(row_count, col_count, kid_rows, BS, kid_cols, BS)
+        .transpose(0, 2, 3, 1, 4, 5)
+        .reshape(row_count * kid_rows, BS, col_count * kid_cols, BS)
+    )
+
+    def child_blocks_at(rsrc, rhas, csrc, chas):
+        got = jnp.take(child4, rsrc, axis=0, mode="clip")
+        got = jnp.take(got, csrc, axis=2, mode="clip")
+        keep = rhas[:, None, None, None] & chas[None, None, :, None]
+        got = jnp.where(keep, got, 0.0)
+        return got.reshape(got.shape[0] * BS, got.shape[2] * BS)
+
+    extended = child_blocks_at(row_src, row_has, col_src, col_has)
 
     mask_all = block_mask[0].astype(jnp.float32)
     mask_local = lax.dynamic_slice(
@@ -102,17 +104,7 @@
     pmatch = own_map[:, None] == piv_arr[None, :]
     prow_src = jnp.sum(jnp.where(pmatch, block_ranks[:, None], 0), axis=0)
     prow_has = jnp.any(pmatch, axis=0)
-    picked_rows = child_tiles[
-        (prow_src // kid_rows)[:, None],
-        (col_src // kid_cols)[None, :],
-        (prow_src % kid_rows)[:, None],
-        :,
-        (col_src % kid_cols)[None, :],
-        :,
-    ]
-    keep_rows = prow_has[:, None] & col_has[None, :]
-    picked_rows = jnp.where(keep_rows[:, :, None, None], picked_rows, 0.0)
-    placed_rows = picked_rows.transpose(0, 2, 1, 3).reshape(4 * BS, loc_cols)
+    placed_rows = child_blocks_at(prow_src, prow_has, col_src, col_has)
     mask_piv_rows = lax.dynamic_slice_in_dim(mask_all[piv_arr], col_id * col_blocks, col_blocks, 1)
     row_panels = spread(mask_piv_rows) * (f_rows + placed_rows)
 
@@ -127,19 +119,6 @@
         axis=0,
     )
     col_payload = lax.psum(col_payload, "col")
-
-    def child_blocks_at(rsrc, rhas, csrc, chas):
-        got = child_tiles[
-            (rsrc // kid_rows)[:, None],
-            (csrc // kid_cols)[None, :],
-            (rsrc % kid_rows)[:, None],
-            :,
-            (csrc % kid_cols)[None, :],
-            :,
-        ]
-        got = jnp.where((rhas[:, None] & chas[None, :])[:, :, None, None], got, 0.0)
-        nr, nc = got.shape[0], got.shape[1]
-        return got.transpose(0, 2, 1, 3).reshape(nr * BS, nc * BS)
 
     mask_rows_local = lax.dynamic_slice_in_dim(mask_all, row_id * row_blocks, row_blocks, 0)
     col_panels = spread(mask_rows_local[:, piv_arr]) * (
@@ -179,13 +158,18 @@
     update = dot(lowers, uppers)
     fresh = assembled - update * spread(mask_local)
 
-    replaced = [(piv[0], lower0[:, :BS], alive0_rows), (piv[1], lower0[:, BS:], alive0_rows),
-                (piv[2], lower1[:, :BS], alive1_rows), (piv[3], lower1[:, BS:], alive1_rows)]
-    for blk, values, live in replaced:
-        slot = blk % col_blocks
-        current = lax.dynamic_slice_in_dim(fresh, slot * BS, BS, 1)
-        written = jnp.where((live[:, None] > 0) & (col_id == blk // col_blocks), values, current)
-        fresh = lax.dynamic_update_slice_in_dim(fresh, written, slot * BS, 1)
+    lower_blocks = jnp.stack([lower0[:, :BS], lower0[:, BS:], lower1[:, :BS], lower1[:, BS:]])
+    live_blocks = jnp.stack([alive0_rows, alive0_rows, alive1_rows, alive1_rows]) > 0
+    local_blk = col_id * col_blocks + jnp.arange(col_blocks, dtype=jnp.int32)
+    hits = piv_arr[None, :] == local_blk[:, None]
+    which = jnp.sum(jnp.where(hits, jnp.arange(4, dtype=jnp.int32)[None, :], 0), axis=1)
+    owned = jnp.any(hits, axis=1)
+    take_lower = jnp.concatenate(
+        [jnp.broadcast_to((live_blocks[which[j]] & owned[j])[:, None], (loc_rows, BS)) for j in range(col_blocks)],
+        axis=1,
+    )
+    lower_cols = jnp.concatenate([lower_blocks[which[j]] for j in range(col_blocks)], axis=1)
+    fresh = jnp.where(take_lower, lower_cols, fresh)
     return fresh[None]
 
 

time: 565 us -> 611 us (1.081)
  local copies, waits for them, and re-layouts: 156 us -> 232 us
  waiting for transfers between devices: 204 us -> 152 us
  other arithmetic: 85 us -> 97.2 us
  between operations: 27.3 us -> 35.9 us
    gather x5 -> x13, local copies, waits for them, and re-layouts: 42.2 us -> 110 us  [the longest x8 75.6 us: child_blocks_at(): got = jnp.take(child4, rsrc, axis=0, mode='clip')]
    psum x1, waiting for transfers between devices: 84.4 us -> 32.7 us  [body(): col_payload = lax.psum(col_payload, 'col')]
    unnamed x62 -> x58, local copies, waits for them, and re-layouts: 65.4 us -> 44.9 us
    transpose x0 -> x1, local copies, waits for them, and re-layouts: none -> 17.9 us  [body(): child4 = gathered.reshape(row_count, col_count, kid_rows, BS, kid_cols, B...]
    dynamic_slice x0 -> x5, local copies, waits for them, and re-layouts: none -> 15.3 us  [body(): lower_blocks[which[j]]]
    select_n x4 -> x5, local copies, waits for them, and re-layouts: 15 us -> 28.5 us  [child_blocks_at(): got = jnp.where(keep, got, 0.0)]
    reshape x1 -> x0, local copies, waits for them, and re-layouts: 12.1 us -> none  [child_blocks_at(): return got.transpose(0, 2, 1, 3).reshape(nr * BS, nc * BS)]
    concatenate x1, other arithmetic: 10.9 us -> 20.7 us  [body(): jnp.concatenate([jnp.concatenate([cols_of(blk, matrix_in) for blk in piv]...]
  transfers between devices with their start and end apart: 11 -> 11, of which waited for: 7 -> 7; matrix products, arithmetic and copies ran while one was open for 34% -> 44% of each run, Pallas kernels for 0% -> 0%
where the time goes in v4:
time: 611 us; the launch traced here: 602 us
  local copies, waits for them, and re-layouts  232 us (38%)
  waiting for transfers between devices  152 us (25%)
  other arithmetic  97.2 us (16%)
  matrix products  70.2 us (11%)
  between operations  35.9 us (6%)
  starting transfers between devices  13.9 us (2%)
    gather x8, local copies, waits for them, and re-layouts, child_blocks_at(): got = jnp.take(child4, rsrc, axis=0, mode='clip')  75.6 us
    dot_general x6, matrix products, dot(): return jnp.dot(a, b, precision=HIGH, preferred_element_type=jnp.float32)  70.2 us
    ppermute x1, waiting for transfers between devices, body(): mine = mine + lax.ppermute(mine, 'row', xor_perm(row_count, 2))  66 us
    unnamed x58, local copies, waits for them, and re-layouts  44.9 us
    gather x5, local copies, waits for them, and re-layouts, child_blocks_at(): got = jnp.take(got, csrc, axis=2, mode='clip')  34.4 us
    psum x1, waiting for transfers between devices, body(): col_payload = lax.psum(col_payload, 'col')  32.7 us
    select_n x5, local copies, waits for them, and re-layouts, child_blocks_at(): got = jnp.where(keep, got, 0.0)  28.5 us
    all_gather x1, waiting for transfers between devices, body(): gathered = lax.all_gather(best_piece, ('row', 'col'), axis=0, tiled=False)  24.7 us
  transfers between devices with their start and end apart: 11, of which 7 were waited for; matrix products, arithmetic and copies ran while one was open for 44% of the time, Pallas kernels for 0%

profile of v4, /device:TPU:1, one launch (start us, length us, event | category | flops | bytes accessed | tf_op | source)
XLA Modules:
  0.0 601.7 jit_solution(5551386148758852269)
XLA Ops:
  6.5 4.6 collective-permute-start.6
  13.2 2.0 collective-permute-start.3
  15.2 1.8 collective-permute-start.4
  16.9 16.2 %collective-permute-done.3 = s32[9]{0:T(128)S(1)} collective-permute-done((s32[9]{0:T(128)S(1)}, s32[9]{0:T(128)S(1)}, u32[]{:S(2)}, u32[]{:S(2)}) %collective-permute-start.3) | collective-permute-done | bytes 68 | tf_op jit(solution)/shard_map/ppermute | solution.py:41
  33.2 3.2 collective-permute-done.4
  37.8 2.0 select_select_fusion
  39.9 1.5 fusion.52
  51.9 2.8 select_bitcast_fusion.7
  54.7 2.5 pad_maximum_fusion.1
  57.2 2.4 collective-permute-start
  59.5 8.0 %collective-permute-done = f32[1024,1024]{1,0:T(8,128)} collective-permute-done((f32[1024,1024]{1,0:T(8,128)}, f32[1024,1024]{1,0:T(8,128)}, u32[]{:S(2)}, u32[]{:S(2)}) %collective-permute-start) | collective-permute-done | bytes 4194336 | tf_op jit(solution)/shard_map/ppermute | solution.py:95
  67.5 3.5 fusion.46
  71.0 2.0 copy-done
  74.8 2.7 fusion.40
  77.5 66.0 %collective-permute-done.1 = f32[512,1024]{1,0:T(8,128)} collective-permute-done((f32[512,1024]{1,0:T(8,128)S(1)}, f32[512,1024]{1,0:T(8,128)}, u32[]{:S(2)}, u32[]{:S(2)}) %collective-permute-start.1) | collective-permute-done | bytes 2097184 | tf_op jit(solution)/shard_map/ppermute | solution.py:99
  143.4 5.1 fusion.55
  150.9 3.1 copy.132
  154.0 2.7 pad_add_fusion
  156.7 6.5 %select_bitcast_fusion.3 = (f32[2048,256]{1,0:T(8,128)S(1)}, f32[2048,256]{1,0:T(8,128)}, f32[2048,256]{1,0:T(8,128)}, f32[2048,256]{1,0:T(8,128)}) fusion(f32[1,2048,1024]{2,1,0:T(8,128)} %param.7, s32[]{:T(128)S(6)} %select_n.417, pred[]{:T(512)S(6)} %eq.131, s32[]{:T(128)S(6)} %select_n.435, pred[]{:T(512)S(6)} %eq.134, s32[]{:T(128)S(6)} %select_n.429, ...), kind=kLoop, calls=%fused_computation.54 | loop fusion | flops 2097152 | bytes 16777236 | tf_op jit(solution)/shard_map/jit(_where)/select_n | solution.py:113
  163.9 24.7 %all-gather.3.cloned.1.call-done = f32[16384,256]{1,0:T(8,128)} async-done(((f32[512,256]{1,0:T(8,128)}), f32[16384,256]{1,0:T(8,128)}) %all-gather.3.cloned.1.call-update) | async-done | bytes 16777232 | tf_op jit(solution)/shard_map/all_gather | solution.py:57
  188.6 17.9 %copy.91 = f32[4,2,256,8,1,256]{5,3,2,1,0,4:T(8,128)} copy(f32[4,2,256,8,1,256]{5,2,1,3,0,4:T(8,128)} %bitcast.193) | data formatting | bytes 33554432 | tf_op jit(solution)/shard_map/transpose | solution.py:60
  206.5 10.2 %gather_fusion.9 = f32[4,256,8,256]{3,2,1,0:T(8,128)} fusion(f32[8,256,8,256]{3,2,1,0:T(8,128)} %bitcast.182, s32[1024]{0:T(1024)S(1)} %pad_clamp_fusion.5), kind=kCustom, calls=%fused_computation.9 | custom fusion | bytes 16777232 | tf_op jit(solution)/shard_map/jit(_take)/gather | solution.py:65
  216.8 9.2 %copy.108 = f32[4,256,8,256]{3,1,2,0:T(8,128)} copy(f32[4,256,8,256]{3,2,1,0:T(8,128)} %gather_fusion.9) | data formatting | bytes 16777216 | tf_op jit(solution)/shard_map/jit(_take)/gather | solution.py:65
  225.9 6.2 %gather_fusion.10 = f32[4,4,256,256]{3,2,1,0:T(8,128)} fusion(f32[4,256,8,256]{3,1,2,0:T(8,128)} %copy.108, s32[1024]{0:T(1024)S(1)} %pad_clamp_fusion), kind=kCustom, calls=%fused_computation.10 | custom fusion | bytes 8388624 | tf_op jit(solution)/shard_map/jit(_take)/gather | solution.py:66
  232.1 2.7 bitcast_select_fusion.2
  234.8 2.7 copy.109
  239.7 5.9 add_multiply_fusion
  248.6 20.7 %maximum_maximum_fusion = f32[2560,1024]{1,0:T(8,128)} fusion(f32[512,256]{1,0:T(8,128)S(1)} %get-tuple-element.38, f32[512,256]{1,0:T(8,128)S(1)} %get-tuple-element.37, f32[512,256]{1,0:T(8,128)S(1)} %get-tuple-element.36, f32[512,256]{1,0:T(8,128)S(1)} %get-tuple-element.35, f32[2048,256]{1,0:T(8,128)S(1)} %copy-done.9, f32[2048,256]{1,0:T(8,128)S(1)} %copy-done.10, ...), kind=kLoop, calls=%fused_computation.15 | loop fusion | flops 18350080 | bytes 20971520 | tf_op jit(solution)/shard_map/concatenate | solution.py:117
  277.1 2.7 fusion.41
  286.3 5.5 copy.123
  295.5 2.4 copy.128
  299.4 5.3 copy.129
  308.1 2.6 and_reduce_fusion.3
  311.3 13.8 %gather_fusion.1 = f32[8,256,8,256]{3,2,1,0:T(8,128)} fusion(f32[8,256,8,256]{3,2,1,0:T(8,128)} %bitcast.183, s32[1024]{0:T(1024)S(1)} %pad_clamp_fusion.6), kind=kCustom, calls=%fused_computation.1 | custom fusion | bytes 33554464 | tf_op jit(solution)/shard_map/jit(_take)/gather | solution.py:65
  325.1 16.3 %copy.92 = f32[8,256,8,256]{3,1,0,2:T(8,128)} copy(f32[8,256,8,256]{3,2,1,0:T(8,128)} %gather_fusion.1) | data formatting | bytes 33554432 | tf_op jit(solution)/shard_map/jit(_take)/gather | solution.py:65
  341.4 10.2 %gather_fusion.2 = f32[4,8,256,256]{3,2,1,0:T(8,128)} fusion(f32[8,256,8,256]{3,1,0,2:T(8,128)} %copy.92, s32[1024]{0:T(1024)S(1)} %pad_clamp_fusion.5), kind=kCustom, calls=%fused_computation.2 | custom fusion | bytes 16777232 | tf_op jit(solution)/shard_map/jit(_take)/gather | solution.py:66
  351.6 10.3 %gather_fusion.7 = f32[4,8,256,256]{3,2,1,0:T(8,128)} fusion(f32[8,256,8,256]{3,1,0,2:T(8,128)} %copy.92, s32[1024]{0:T(1024)S(1)} %pad_clamp_fusion), kind=kCustom, calls=%fused_computation.7 | custom fusion | bytes 16777232 | tf_op jit(solution)/shard_map/jit(_take)/gather | solution.py:66
  361.9 8.8 %gather_fusion.13 = f32[2,256,8,256]{3,2,1,0:T(8,128)} fusion(f32[8,256,8,256]{3,2,1,0:T(8,128)} %bitcast.184, s32[1024]{0:T(1024)S(1)} %pad_clamp_fusion.1), kind=kCustom, calls=%fused_computation.13 | custom fusion | bytes 8388616 | tf_op jit(solution)/shard_map/jit(_take)/gather | solution.py:65
  370.6 5.4 copy.112
  376.0 8.8 %gather_fusion.5 = f32[2,256,8,256]{3,2,1,0:T(8,128)} fusion(f32[8,256,8,256]{3,2,1,0:T(8,128)} %bitcast.185, s32[1024]{0:T(1024)S(1)} %pad_clamp_fusion.2), kind=kCustom, calls=%fused_computation.5 | custom fusion | bytes 8388616 | tf_op jit(solution)/shard_map/jit(_take)/gather | solution.py:65
  384.8 3.9 gather_fusion.14
  388.6 1.4 bitcast_select_fusion.3
  391.9 8.3 %bitcast_select_fusion.1 = f32[8,256,4,256]{3,1,0,2:T(8,128)} fusion(f32[4,8,256,256]{3,2,1,0:T(8,128)} %gather_fusion.2, pred[8,4]{0,1:T(4,128)(4,1)S(1)} %get-tuple-element.56), kind=kLoop, calls=%fused_computation.29 | loop fusion | flops 2097152 | bytes 16777248 | tf_op jit(solution)/shard_map/jit(_where)/select_n | solution.py:68
  400.3 12.1 %copy.114 = f32[8,256,4,256]{3,2,1,0:T(4,128)} copy(f32[8,256,4,256]{3,1,0,2:T(8,128)} %bitcast_select_fusion.1) | data formatting | bytes 16777216 | tf_op jit(solution)/shard_map/jit(_where)/select_n | solution.py:68
  412.4 9.1 %copy.124 = f32[256,8,4,256]{3,1,2,0:T(8,128)} copy(f32[256,8,4,256]{3,2,1,0:T(4,128)} %bitcast.188) | data formatting | bytes 16777216
  421.5 3.2 copy.97
  424.6 3.9 gather_fusion.6
  431.8 7.9 %bitcast_select_fusion = f32[8,256,4,256]{3,1,0,2:T(8,128)} fusion(f32[4,8,256,256]{3,2,1,0:T(8,128)} %gather_fusion.7, pred[8,4]{0,1:T(4,128)(4,1)S(1)} %get-tuple-element.55), kind=kLoop, calls=%fused_computation.25 | loop fusion | flops 2097152 | bytes 16777248 | tf_op jit(solution)/shard_map/jit(_where)/select_n | solution.py:68
  439.7 12.1 %copy.107 = f32[8,256,4,256]{3,2,1,0:T(4,128)} copy(f32[8,256,4,256]{3,1,0,2:T(8,128)} %bitcast_select_fusion) | data formatting | bytes 16777216 | tf_op jit(solution)/shard_map/jit(_where)/select_n | solution.py:68
  451.8 9.0 %copy.130 = f32[256,8,4,256]{3,1,2,0:T(8,128)} copy(f32[256,8,4,256]{3,2,1,0:T(4,128)} %bitcast.189) | data formatting | bytes 16777216
  460.7 1.8 slice_multiply_fusion
  462.6 32.7 %all-reduce.2.cloned.1.call-done = f32[2560,1024]{1,0:T(8,128)} async-done(((f32[2560,1024]{1,0:T(8,128)}), f32[2560,1024]{1,0:T(8,128)}) %all-reduce.2.cloned.1.call-update) | async-done | bytes 10485776 | tf_op jit(solution)/shard_map/psum | solution.py:121
  495.2 9.9 %fusion = f32[2048,1024]{1,0:T(8,128)S(1)} fusion(f32[2048,1024]{1,0:T(8,128)} %bitcast.190, f32[2048,1024]{1,0:T(8,128)} %bitcast.191, f32[2560,1024]{1,0:T(8,128)} %all-reduce.2.cloned.1.call-done), kind=kLoop, calls=%fused_computation.17 | loop fusion | flops 4194304 | bytes 33554432 | tf_op jit(solution)/shard_map/mul | solution.py:124
  505.1 7.1 %broadcast_multiply_fusion.1 = (f32[2048,512]{0,1:T(8,128)S(1)}, f32[2048,512]{0,1:T(8,128)S(1)}) fusion(f32[2048]{0:T(1024)S(1)} %bitcast.220, f32[1,2,512,512]{3,2,1,0:T(8,128)S(1)} %copy-done.12, f32[2048,1024]{1,0:T(8,128)S(1)} %fusion), kind=kOutput, calls=%fused_computation.50 | convolution fusion | flops 6443499520 | bytes 13639680 | tf_op jit(solution)/shard_map/dot_general | solution.py:13
  512.3 9.7 %fusion.26 = f32[2048,512]{1,0:T(8,128)S(1)} fusion(f32[2048,512]{0,1:T(8,128)S(1)} %get-tuple-element.69, f32[512,512]{1,0:T(8,128)S(1)} %bitcast.204, f32[512,512]{1,0:T(8,128)S(1)} %bitcast.206, f32[2560,1024]{1,0:T(8,128)} %all-reduce.2.cloned.1.call-done), kind=kOutput, calls=%fused_computation.63 | convolution fusion | flops 6442975232 | bytes 11534336 | tf_op jit(solution)/shard_map/dot_general | solution.py:13
  522.1 9.0 %broadcast_multiply_fusion = (f32[2048,512]{0,1:T(8,128)}, f32[2048,512]{0,1:T(8,128)S(1)}) fusion(f32[2048]{0:T(1024)S(1)} %bitcast.219, f32[1,2,512,512]{3,2,1,0:T(8,128)S(1)} %copy-done.12, f32[2048,1024]{1,0:T(8,128)S(1)} %fusion, f32[2048,512]{1,0:T(8,128)S(1)} %fusion.26, f32[2048,512]{1,0:T(8,128)S(1)} %bitcast.192), kind=kOutput, calls=%fused_computation.49 | convolution fusion | flops 6445596672 | bytes 22028288 | tf_op jit(solution)/shard_map/dot_general | solution.py:13
  533.1 3.5 constant_dynamic-slice_fusion.8
  536.6 2.9 copy.100
  539.5 2.9 copy.101
  542.4 2.9 copy.102
  545.3 3.1 copy.103
  548.4 3.9 fusion.23
  552.3 5.1 fusion.17
  559.2 35.4 %fusion.1 = f32[1,2048,1024]{2,1,0:T(8,128)} fusion(f32[2048,256]{1,0:T(8,128)} %bitcast.214, f32[2048,256]{1,0:T(8,128)} %bitcast.213, f32[2048,256]{1,0:T(8,128)} %bitcast.212, f32[2048,256]{1,0:T(8,128)} %bitcast.211, f32[2048,1024]{1,0:T(8,128)} %bitcast.200, f32[2048,1024]{1,0:T(8,128)} %bitcast.201, f32[1,2048,1024]{2,1,0:T(8,128)} %param.7, ...), kind=kOutput, calls=%fused_computation.20 | convolution fusion | flops 25796018176 | bytes 56623104 | tf_op jit(solution)/shard_map/dot_general | solution.py:13
  (141 shorter events, 34.4 us)
Async XLA Ops:
  6.5 182.1 %all-gather.3.cloned.1.call-start = ((), (), s32[]{:S(2)}) async-start(), calls=%async_computation.1 | async-start | bytes 17301504 | tf_op jit(solution)/shard_map/all_gather | solution.py:57
  6.5 31.2 %collective-permute-start.6 = (f32[512,256]{1,0:T(8,128)}, f32[512,256]{1,0:T(8,128)S(1)}, u32[]{:S(2)}, u32[]{:S(2)}) collective-permute-start(f32[512,256]{1,0:T(8,128)} %bitcast.215), channel_id=1, source_target_pairs={{0,96},{32,0},{64,32},{96,64},{1,97},{33,1},{65,33},{97,65},{2,98}... | collective-permute-start | bytes 1572872 | tf_op jit(solution)/shard_map/ppermute | solution.py:40
  11.1 26.7 %collective-permute-start.7 = (f32[512,256]{1,0:T(8,128)}, f32[512,256]{1,0:T(8,128)S(1)}, u32[]{:S(2)}, u32[]{:S(2)}) collective-permute-start(f32[512,256]{1,0:T(8,128)} %bitcast.216), channel_id=1, source_target_pairs={{0,64},{32,96},{64,0},{96,32},{1,65},{33,97},{65,1},{97,33},{2,66}... | collective-permute-start | bytes 1572872 | tf_op jit(solution)/shard_map/ppermute | solution.py:40
  11.1 26.7 %collective-permute-start.8 = (f32[512,256]{1,0:T(8,128)}, f32[512,256]{1,0:T(8,128)S(1)}, u32[]{:S(2)}, u32[]{:S(2)}) collective-permute-start(f32[512,256]{1,0:T(8,128)} %bitcast.217), channel_id=1, source_target_pairs={{0,32},{32,64},{64,96},{96,0},{1,33},{33,65},{65,97},{97,1},{2,34}... | collective-permute-start | bytes 1572872 | tf_op jit(solution)/shard_map/ppermute | solution.py:40
  13.2 19.9 %collective-permute-start.3 = (s32[9]{0:T(128)S(1)}, s32[9]{0:T(128)S(1)}, u32[]{:S(2)}, u32[]{:S(2)}) collective-permute-start(s32[9]{0:T(128)S(1)} %pad_add_fusion.1), channel_id=1, source_target_pairs={{0,96},{32,0},{64,32},{96,64},{1,97},{33,1},{65,33},{97,65},{2,98}... | collective-permute-start | bytes 116 | tf_op jit(solution)/shard_map/ppermute | solution.py:41
  15.2 21.2 %collective-permute-start.4 = (s32[9]{0:T(128)S(1)}, s32[9]{0:T(128)S(1)}, u32[]{:S(2)}, u32[]{:S(2)}) collective-permute-start(s32[9]{0:T(128)S(1)} %pad_add_fusion.1), channel_id=1, source_target_pairs={{0,64},{32,96},{64,0},{96,32},{1,65},{33,97},{65,1},{97,33},{2,66}... | collective-permute-start | bytes 116 | tf_op jit(solution)/shard_map/ppermute | solution.py:41
  33.1 4.6 collective-permute-start.5
  39.8 455.4 %all-reduce.2.cloned.1.call-start = ((), (), s32[]{:S(2)}) async-start(), calls=%async_computation | async-start | bytes 20971520 | tf_op jit(solution)/shard_map/psum | solution.py:121
  54.7 2.5 copy-start.8
  57.2 10.3 %collective-permute-start = (f32[1024,1024]{1,0:T(8,128)}, f32[1024,1024]{1,0:T(8,128)}, u32[]{:S(2)}, u32[]{:S(2)}) collective-permute-start(f32[1024,1024]{1,0:T(8,128)} %pad_maximum_fusion.1), channel_id=1, source_target_pairs={{0,8},{8,0},{16,24},{24,16},{1,9},{9,1},{17,25},{25,17},{2,10},{10... | collective-permute-start | bytes 12582920 | tf_op jit(solution)/shard_map/ppermute | solution.py:95
  71.0 2.0 copy-start
  73.0 4.4 copy-start.15
  73.4 70.0 %collective-permute-start.1 = (f32[512,1024]{1,0:T(8,128)S(1)}, f32[512,1024]{1,0:T(8,128)}, u32[]{:S(2)}, u32[]{:S(2)}) collective-permute-start(f32[512,1024]{1,0:T(8,128)S(1)} %slice_select_fusion), channel_id=1, source_target_pairs={{0,16},{8,24},{16,0},{24,8},{1,17},{9,25},{17,1},{25,9},{2,18},{10... | collective-permute-start | bytes 6291464 | tf_op jit(solution)/shard_map/ppermute | solution.py:99
  148.6 90.0 %collective-permute-start.2 = (f32[512,1024]{1,0:T(8,128)}, f32[512,1024]{1,0:T(8,128)}, u32[]{:S(2)}, u32[]{:S(2)}) collective-permute-start(f32[512,1024]{1,0:T(8,128)} %fusion.55), channel_id=1, source_target_pairs={{0,8},{8,0},{16,24},{24,16},{1,9},{9,1},{17,25},{25,17},{2,10},{10... | collective-permute-start | bytes 6291464 | tf_op jit(solution)/shard_map/ppermute | solution.py:100
  156.7 6.5 %copy-start.17 = (s32[1,8]{1,0:T(1,128)S(1)}, s32[1,8]{1,0:T(1,128)}, u32[]{:S(2)}) copy-start(s32[1,8]{1,0:T(1,128)} %param.10) | copy-start | bytes 100
  237.5 2.2 copy-start.7
  245.7 1.6 copy-start.11
  246.0 2.0 copy-start.9
  246.0 2.6 copy-start.10
  269.4 1.3 copy-start.16
  412.4 9.1 %copy-start.6 = (f32[2,256,8,256]{3,2,1,0:T(8,128)S(1)}, f32[2,256,8,256]{3,2,1,0:T(8,128)}, u32[]{:S(2)}) copy-start(f32[2,256,8,256]{3,2,1,0:T(8,128)} %gather_fusion.5) | copy-start | bytes 12582916
  451.8 9.0 %copy-start.4 = (f32[1024,1024]{1,0:T(8,128)S(1)}, f32[1024,1024]{1,0:T(8,128)}, u32[]{:S(2)}) copy-start(f32[1024,1024]{1,0:T(8,128)} %get-tuple-element.15) | copy-start | bytes 12582916
  495.2 9.9 %copy-start.12 = (f32[1,2,512,512]{3,2,1,0:T(8,128)S(1)}, f32[1,2,512,512]{3,2,1,0:T(8,128)}, u32[]{:S(2)}) copy-start(f32[1,2,512,512]{3,2,1,0:T(8,128)} %param.13) | copy-start | bytes 6291460
  505.1 7.2 %copy-start.13 = (f32[64,8,2,256]{3,1,2,0:T(8,128)S(1)}, f32[64,8,2,256]{3,1,2,0:T(8,128)}, u32[]{:S(2)}) copy-start(f32[64,8,2,256]{3,1,2,0:T(8,128)} %copy.126) | copy-start | bytes 3145732
  505.1 7.2 %copy-start.14 = (f32[64,8,2,256]{3,1,2,0:T(8,128)S(1)}, f32[64,8,2,256]{3,1,2,0:T(8,128)}, u32[]{:S(2)}) copy-start(f32[64,8,2,256]{3,1,2,0:T(8,128)} %copy.127) | copy-start | bytes 3145732
  512.3 9.8 %copy-start.1 = (f32[2048,512]{0,1:T(8,128)}, f32[2048,512]{0,1:T(8,128)S(1)}, u32[]{:S(2)}) copy-start(f32[2048,512]{0,1:T(8,128)S(1)} %get-tuple-element.69) | copy-start | bytes 12582916
  512.3 9.8 %copy-start.3 = (f32[256,8,2,256]{3,1,2,0:T(8,128)S(1)}, f32[256,8,2,256]{3,1,2,0:T(8,128)}, u32[]{:S(2)}) copy-start(f32[256,8,2,256]{3,1,2,0:T(8,128)} %copy.128) | copy-start | bytes 12582916
  548.4 3.9 copy-start.5
  552.3 6.9 %copy-start.2 = (f32[2048,512]{0,1:T(8,128)S(1)}, f32[2048,512]{0,1:T(8,128)}, u32[]{:S(2)}) copy-start(f32[2048,512]{0,1:T(8,128)} %copy-done.1) | copy-start | bytes 12582916
Sparse Core Ops, SparseCore 0:
  40.0 148.6 all-gather.2
  269.5 225.6 all-reduce.1

commit v5 on v4

--- a/solution.py
+++ b/solution.py
@@ -55,18 +55,16 @@
     row_src, row_has = locate(row_id * row_blocks, row_blocks)
     col_src, col_has = locate(col_id * col_blocks, col_blocks)
     gathered = lax.all_gather(best_piece, ("row", "col"), axis=0, tiled=False)
-    child4 = (
-        gathered.reshape(row_count, col_count, kid_rows, BS, kid_cols, BS)
-        .transpose(0, 2, 3, 1, 4, 5)
-        .reshape(row_count * kid_rows, BS, col_count * kid_cols, BS)
-    )
+    def child_block(blk_r, blk_c):
+        start = ((blk_r // kid_rows) * col_count + blk_c // kid_cols, (blk_r % kid_rows) * BS, (blk_c % kid_cols) * BS)
+        return lax.dynamic_slice(gathered, start, (1, BS, BS))[0]
 
     def child_blocks_at(rsrc, rhas, csrc, chas):
-        got = jnp.take(child4, rsrc, axis=0, mode="clip")
-        got = jnp.take(got, csrc, axis=2, mode="clip")
-        keep = rhas[:, None, None, None] & chas[None, None, :, None]
-        got = jnp.where(keep, got, 0.0)
-        return got.reshape(got.shape[0] * BS, got.shape[2] * BS)
+        rows = []
+        for i in range(rsrc.shape[0]):
+            row = [jnp.where(rhas[i] & chas[j], child_block(rsrc[i], csrc[j]), 0.0) for j in range(csrc.shape[0])]
+            rows.append(jnp.concatenate(row, axis=1))
+        return jnp.concatenate(rows, axis=0)
 
     extended = child_blocks_at(row_src, row_has, col_src, col_has)
 

time: 611 us -> 591 us (0.967)
  between operations: 35.9 us -> 228 us
  local copies, waits for them, and re-layouts: 232 us -> 59.4 us
  waiting for transfers between devices: 152 us -> 101 us
  other arithmetic: 97.2 us -> 109 us
    gather x13 -> x0, local copies, waits for them, and re-layouts: 110 us -> none  [the longest x8 75.6 us: child_blocks_at(): got = jnp.take(child4, rsrc, axis=0, mode='clip')]
    select_n x5 -> x0, local copies, waits for them, and re-layouts: 28.5 us -> none  [child_blocks_at(): got = jnp.where(keep, got, 0.0)]
    all_gather x1, waiting for transfers between devices: 24.7 us -> 0.02 us  [body(): gathered = lax.all_gather(best_piece, ('row', 'col'), axis=0, tiled=False)]
    unnamed x58 -> x63, local copies, waits for them, and re-layouts: 44.9 us -> 22.2 us
    psum x1, waiting for transfers between devices: 32.7 us -> 13.7 us  [body(): col_payload = lax.psum(col_payload, 'col')]
    transpose x1 -> x0, local copies, waits for them, and re-layouts: 17.9 us -> none  [body(): child4 = gathered.reshape(row_count, col_count, kid_rows, BS, kid_cols, B...]
    concatenate x1, other arithmetic: 20.7 us -> 11.2 us  [body(): jnp.concatenate([jnp.concatenate([cols_of(blk, matrix_in) for blk in piv]...]
    unnamed x0 -> x14, other arithmetic: none -> 8.64 us
  transfers between devices with their start and end apart: 11 -> 11, of which waited for: 7 -> 6; matrix products, arithmetic and copies ran while one was open for 44% -> 19% of each run, Pallas kernels for 0% -> 0%
where the time goes in v5:
time: 591 us; the launch traced here: 582 us
  between operations  228 us (39%)
  other arithmetic  109 us (18%)
  waiting for transfers between devices  101 us (17%)
  matrix products  70.2 us (12%)
  local copies, waits for them, and re-layouts  59.4 us (10%)
  starting transfers between devices  14.1 us (2%)
    dot_general x6, matrix products, dot(): return jnp.dot(a, b, precision=HIGH, preferred_element_type=jnp.float32)  70.2 us
    ppermute x1, waiting for transfers between devices, body(): mine = mine + lax.ppermute(mine, 'row', xor_perm(row_count, 2))  58.9 us
    select_n x12, other arithmetic, child_blocks_at(): jnp.where(rhas[i] & chas[j], child_block(rsrc[i], csrc[j]), 0.0)  29.7 us
    unnamed x63, local copies, waits for them, and re-layouts  22.2 us
    ppermute x3, waiting for transfers between devices, body(): got_tags = lax.ppermute(tags, 'front', perm)  20.7 us
    dynamic_slice x5, local copies, waits for them, and re-layouts, body(): lower_blocks[which[j]]  15.6 us
    psum x1, waiting for transfers between devices, body(): col_payload = lax.psum(col_payload, 'col')  13.7 us
  transfers between devices with their start and end apart: 11, of which 6 were waited for; matrix products, arithmetic and copies ran while one was open for 19% of the time, Pallas kernels for 0%

profile of v5, /device:TPU:1, one launch (start us, length us, event | category | flops | bytes accessed | tf_op | source)
XLA Modules:
  0.0 581.9 jit_solution(4907457246996747880)
XLA Ops:
  6.5 4.6 collective-permute-start.6
  13.2 2.0 collective-permute-start.3
  15.2 1.8 collective-permute-start.4
  16.9 16.2 %collective-permute-done.3 = s32[9]{0:T(128)S(1)} collective-permute-done((s32[9]{0:T(128)S(1)}, s32[9]{0:T(128)S(1)}, u32[]{:S(2)}, u32[]{:S(2)}) %collective-permute-start.3) | collective-permute-done | bytes 68 | tf_op jit(solution)/shard_map/ppermute | solution.py:41
  33.2 3.2 collective-permute-done.4
  36.4 1.3 collective-permute-done.5
  37.8 2.0 select_select_fusion
  39.9 1.5 fusion.75
  51.7 2.8 select_bitcast_fusion.7
  54.5 2.5 pad_maximum_fusion.1
  56.9 2.3 collective-permute-start
  59.3 8.1 %collective-permute-done = f32[1024,1024]{1,0:T(8,128)} collective-permute-done((f32[1024,1024]{1,0:T(8,128)}, f32[1024,1024]{1,0:T(8,128)}, u32[]{:S(2)}, u32[]{:S(2)}) %collective-permute-start) | collective-permute-done | bytes 4194336 | tf_op jit(solution)/shard_map/ppermute | solution.py:93
  67.3 3.5 fusion.65
  70.9 2.0 copy-done
  72.9 1.8 slice_select_fusion
  74.7 1.3 collective-permute-start.1
  75.9 2.6 fusion.57
  79.2 6.5 %select_bitcast_fusion.3 = (f32[2048,256]{1,0:T(8,128)S(1)}, f32[2048,256]{1,0:T(8,128)}, f32[2048,256]{1,0:T(8,128)}, f32[2048,256]{1,0:T(8,128)}) fusion(f32[1,2048,1024]{2,1,0:T(8,128)} %param.7, s32[]{:T(128)S(6)} %select_n.2205, pred[]{:T(512)S(6)} %eq.307, s32[]{:T(128)S(6)} %select_n.2223, pred[]{:T(512)S(6)} %eq.310, s32[]{:T(128)S(6)} %select_n.2217, ...), kind=kLoop, calls=%fused_computation.43 | loop fusion | flops 2097152 | bytes 16777236 | tf_op jit(solution)/shard_map/jit(_where)/select_n | solution.py:111
  85.7 58.9 %collective-permute-done.1 = f32[512,1024]{1,0:T(8,128)} collective-permute-done((f32[512,1024]{1,0:T(8,128)}, f32[512,1024]{1,0:T(8,128)}, u32[]{:S(2)}, u32[]{:S(2)}) %collective-permute-start.1) | collective-permute-done | bytes 2097184 | tf_op jit(solution)/shard_map/ppermute | solution.py:97
  144.6 3.7 fusion.78
  148.4 1.5 collective-permute-start.2
  150.5 3.0 copy.77
  153.5 2.6 pad_add_fusion
  215.6 3.2 select_bitcast_fusion.31
  218.8 3.2 select_bitcast_fusion.30
  222.0 3.2 select_bitcast_fusion.11
  225.2 9.9 %fusion.13 = (f32[1024,1024]{1,0:T(8,128)}, f32[1024,1024]{1,0:T(8,128)}) fusion(f32[1024,1024]{1,0:T(8,128)} %bitcast.448, f32[256,256]{1,0:T(8,128)S(1)} %get-tuple-element.21, f32[256,256]{1,0:T(8,128)S(1)} %get-tuple-element.22, f32[256,256]{1,0:T(8,128)S(1)} %get-tuple-element.23, f32[256,256]{1,0:T(8,128)S(1)} %get-tuple-element.24, ...), kind=kLoop, calls=%fused_computation.26 | loop fusion | flops 20971520 | bytes 20971520 | tf_op jit(solution)/shard_map/mul | solution.py:107
  235.1 2.7 fusion.66
  238.1 1.3 copy-done.8
  240.0 11.2 %maximum_maximum_fusion = f32[2560,1024]{1,0:T(8,128)} fusion(f32[512,256]{1,0:T(8,128)S(1)} %get-tuple-element.126, f32[512,256]{1,0:T(8,128)S(1)} %get-tuple-element.125, f32[512,256]{1,0:T(8,128)S(1)} %get-tuple-element.124, f32[512,256]{1,0:T(8,128)S(1)} %get-tuple-element.123, f32[2048,256]{1,0:T(8,128)S(1)} %copy-done.8, f32[2048,256]{1,0:T(8,128)S(1)} %copy-done.9, ...), kind=kLoop, calls=%fused_computation.6 | loop fusion | flops 18350080 | bytes 20971520 | tf_op jit(solution)/shard_map/concatenate | solution.py:115
  258.5 2.6 fusion.58
  266.4 1.1 broadcast_in_dim.283
  267.6 5.5 copy.71
  275.6 1.1 broadcast_in_dim.293
  276.8 2.4 copy.74
  279.4 1.1 broadcast_in_dim.294
  280.6 5.3 copy.75
  289.2 2.7 and_reduce_fusion.3
  430.3 2.3 select_bitcast_fusion.55
  432.7 2.1 select_bitcast_fusion.91
  434.8 1.1 maximum_dynamic-update-slice_fusion.7
  436.1 2.3 select_bitcast_fusion.47
  438.7 1.8 select_bitcast_fusion.39
  440.7 2.0 select_bitcast_fusion.29
  443.1 3.0 select_bitcast_fusion.83
  446.0 1.1 maximum_dynamic-update-slice_fusion.6
  448.2 1.9 select_bitcast_fusion.75
  450.1 1.2 maximum_dynamic-update-slice_fusion.4
  452.4 1.8 select_bitcast_fusion.67
  456.4 2.9 select_bitcast_fusion.63
  460.4 1.6 slice_multiply_fusion
  462.0 13.7 %all-reduce.2.cloned.1.call-done = f32[2560,1024]{1,0:T(8,128)} async-done(((f32[2560,1024]{1,0:T(8,128)}), f32[2560,1024]{1,0:T(8,128)}) %all-reduce.2.cloned.1.call-update) | async-done | bytes 10485776 | tf_op jit(solution)/shard_map/psum | solution.py:119
  475.7 9.9 %fusion = f32[2048,1024]{1,0:T(8,128)S(1)} fusion(f32[2048,1024]{1,0:T(8,128)} %bitcast.432, f32[2048,1024]{1,0:T(8,128)} %maximum_dynamic-update-slice_fusion, f32[2560,1024]{1,0:T(8,128)} %all-reduce.2.cloned.1.call-done), kind=kLoop, calls=%fused_computation.8 | loop fusion | flops 4194304 | bytes 33554432 | tf_op jit(solution)/shard_map/mul | solution.py:122
  485.6 7.6 %broadcast_multiply_fusion.1 = (f32[2048,512]{0,1:T(8,128)S(1)}, f32[2048,512]{0,1:T(8,128)S(1)}) fusion(f32[2048]{0:T(1024)S(1)} %bitcast.465, f32[1,2,512,512]{3,2,1,0:T(8,128)S(1)} %copy-done.11, f32[2048,1024]{1,0:T(8,128)S(1)} %fusion), kind=kOutput, calls=%fused_computation.39 | convolution fusion | flops 6443499520 | bytes 13639680 | tf_op jit(solution)/shard_map/dot_general | solution.py:13
  493.3 9.5 %fusion.27 = f32[2048,512]{1,0:T(8,128)S(1)} fusion(f32[2048,512]{0,1:T(8,128)S(1)} %get-tuple-element.181, f32[512,512]{1,0:T(8,128)S(1)} %bitcast.455, f32[2560,1024]{1,0:T(8,128)} %all-reduce.2.cloned.1.call-done, f32[256,256]{1,0:T(8,128)S(1)} %copy-done.13, f32[256,256]{1,0:T(8,128)S(1)} %copy-done.14, f32[256,256]{1,0:T(8,128)S(1)} %copy-done.15, ...), kind=kOutput, calls=%fused_computation.52 | convolution fusion | flops 6443761664 | bytes 11534336 | tf_op jit(solution)/shard_map/dot_general | solution.py:13
  502.9 8.8 %broadcast_multiply_fusion = (f32[2048,512]{0,1:T(8,128)}, f32[2048,512]{0,1:T(8,128)S(1)}) fusion(f32[2048]{0:T(1024)S(1)} %bitcast.464, f32[1,2,512,512]{3,2,1,0:T(8,128)S(1)} %copy-done.11, f32[2048,1024]{1,0:T(8,128)S(1)} %fusion, f32[2048,512]{1,0:T(8,128)S(1)} %fusion.27, f32[2048,512]{1,0:T(8,128)S(1)} %bitcast.445), kind=kOutput, calls=%fused_computation.38 | convolution fusion | flops 6445596672 | bytes 22028288 | tf_op jit(solution)/shard_map/dot_general | solution.py:13
  513.2 3.5 constant_dynamic-slice_fusion.8
  516.7 2.9 copy.56
  519.7 2.9 copy.57
  522.6 3.0 copy.58
  525.5 3.3 copy.59
  528.8 3.8 fusion.24
  532.7 5.1 fusion.18
  539.6 35.4 %fusion.1 = f32[1,2048,1024]{2,1,0:T(8,128)} fusion(f32[2048,256]{1,0:T(8,128)} %bitcast.459, f32[2048,256]{1,0:T(8,128)} %bitcast.458, f32[2048,256]{1,0:T(8,128)} %bitcast.457, f32[2048,256]{1,0:T(8,128)} %bitcast.456, f32[2048,1024]{1,0:T(8,128)} %bitcast.450, f32[2048,1024]{1,0:T(8,128)} %copy-done.19, f32[1,2048,1024]{2,1,0:T(8,128)} %param.7, ...), kind=kOutput, calls=%fused_computation.11 | convolution fusion | flops 25796018176 | bytes 56623104 | tf_op jit(solution)/shard_map/dot_general | solution.py:13
  (146 shorter events, 27.2 us)
Async XLA Ops:
  6.5 209.0 %all-gather.3.cloned.1.call-start = ((), (), s32[]{:S(2)}) async-start(), calls=%async_computation.1 | async-start | bytes 17301504 | tf_op jit(solution)/shard_map/all_gather | solution.py:57
  6.5 31.2 %collective-permute-start.6 = (f32[512,256]{1,0:T(8,128)}, f32[512,256]{1,0:T(8,128)S(1)}, u32[]{:S(2)}, u32[]{:S(2)}) collective-permute-start(f32[512,256]{1,0:T(8,128)} %bitcast.460), channel_id=1, source_target_pairs={{0,96},{32,0},{64,32},{96,64},{1,97},{33,1},{65,33},{97,65},{2,98}... | collective-permute-start | bytes 1572872 | tf_op jit(solution)/shard_map/ppermute | solution.py:40
  11.1 26.7 %collective-permute-start.7 = (f32[512,256]{1,0:T(8,128)}, f32[512,256]{1,0:T(8,128)S(1)}, u32[]{:S(2)}, u32[]{:S(2)}) collective-permute-start(f32[512,256]{1,0:T(8,128)} %bitcast.461), channel_id=1, source_target_pairs={{0,64},{32,96},{64,0},{96,32},{1,65},{33,97},{65,1},{97,33},{2,66}... | collective-permute-start | bytes 1572872 | tf_op jit(solution)/shard_map/ppermute | solution.py:40
  11.1 26.7 %collective-permute-start.8 = (f32[512,256]{1,0:T(8,128)}, f32[512,256]{1,0:T(8,128)S(1)}, u32[]{:S(2)}, u32[]{:S(2)}) collective-permute-start(f32[512,256]{1,0:T(8,128)} %bitcast.462), channel_id=1, source_target_pairs={{0,32},{32,64},{64,96},{96,0},{1,33},{33,65},{65,97},{97,1},{2,34}... | collective-permute-start | bytes 1572872 | tf_op jit(solution)/shard_map/ppermute | solution.py:40
  13.2 19.9 %collective-permute-start.3 = (s32[9]{0:T(128)S(1)}, s32[9]{0:T(128)S(1)}, u32[]{:S(2)}, u32[]{:S(2)}) collective-permute-start(s32[9]{0:T(128)S(1)} %pad_add_fusion.1), channel_id=1, source_target_pairs={{0,96},{32,0},{64,32},{96,64},{1,97},{33,1},{65,33},{97,65},{2,98}... | collective-permute-start | bytes 116 | tf_op jit(solution)/shard_map/ppermute | solution.py:41
  15.2 21.2 %collective-permute-start.4 = (s32[9]{0:T(128)S(1)}, s32[9]{0:T(128)S(1)}, u32[]{:S(2)}, u32[]{:S(2)}) collective-permute-start(s32[9]{0:T(128)S(1)} %pad_add_fusion.1), channel_id=1, source_target_pairs={{0,64},{32,96},{64,0},{96,32},{1,65},{33,97},{65,1},{97,33},{2,66}... | collective-permute-start | bytes 116 | tf_op jit(solution)/shard_map/ppermute | solution.py:41
  33.1 4.6 collective-permute-start.5
  39.8 435.9 %all-reduce.2.cloned.1.call-start = ((), (), s32[]{:S(2)}) async-start(), calls=%async_computation | async-start | bytes 20971520 | tf_op jit(solution)/shard_map/psum | solution.py:119
  54.5 2.5 copy-start.7
  56.9 10.4 %collective-permute-start = (f32[1024,1024]{1,0:T(8,128)}, f32[1024,1024]{1,0:T(8,128)}, u32[]{:S(2)}, u32[]{:S(2)}) collective-permute-start(f32[1024,1024]{1,0:T(8,128)} %pad_maximum_fusion.1), channel_id=1, source_target_pairs={{0,8},{8,0},{16,24},{24,16},{1,9},{9,1},{17,25},{25,17},{2,10},{10... | collective-permute-start | bytes 12582920 | tf_op jit(solution)/shard_map/ppermute | solution.py:93
  70.9 2.0 copy-start
  72.9 5.7 copy-start.20
  74.7 70.0 %collective-permute-start.1 = (f32[512,1024]{1,0:T(8,128)}, f32[512,1024]{1,0:T(8,128)}, u32[]{:S(2)}, u32[]{:S(2)}) collective-permute-start(f32[512,1024]{1,0:T(8,128)} %slice_select_fusion), channel_id=1, source_target_pairs={{0,16},{8,24},{16,0},{24,8},{1,17},{9,25},{17,1},{25,9},{2,18},{10... | collective-permute-start | bytes 6291464 | tf_op jit(solution)/shard_map/ppermute | solution.py:97
  79.2 65.5 %copy-start.1 = (f32[1024,1024]{1,0:T(8,128)S(1)}, f32[1024,1024]{1,0:T(8,128)}, u32[]{:S(2)}) copy-start(f32[1024,1024]{1,0:T(8,128)} %copy-done) | copy-start | bytes 12582916
  148.4 76.9 %collective-permute-start.2 = (f32[512,1024]{1,0:T(8,128)}, f32[512,1024]{1,0:T(8,128)}, u32[]{:S(2)}, u32[]{:S(2)}) collective-permute-start(f32[512,1024]{1,0:T(8,128)} %fusion.78), channel_id=1, source_target_pairs={{0,8},{8,0},{16,24},{24,16},{1,9},{9,1},{17,25},{25,17},{2,10},{10... | collective-permute-start | bytes 6291464 | tf_op jit(solution)/shard_map/ppermute | solution.py:98
  150.5 5.7 copy-start.22
  235.1 3.0 copy-start.10
  237.8 1.6 copy-start.8
  237.8 2.2 copy-start.9
  251.3 1.2 copy-start.21
  440.6 2.3 copy-start.17
  440.6 2.3 copy-start.18
  443.1 7.1 %copy-start.19 = (f32[2048,1024]{1,0:T(8,128)}, f32[2048,1024]{1,0:T(8,128)S(1)}, u32[]{:S(2)}) copy-start(f32[2048,1024]{1,0:T(8,128)S(1)} %maximum_dynamic-update-slice_fusion.8) | copy-start | bytes 25165828
  455.3 5.1 copy-start.5
  475.7 9.9 %copy-start.11 = (f32[1,2,512,512]{3,2,1,0:T(8,128)S(1)}, f32[1,2,512,512]{3,2,1,0:T(8,128)}, u32[]{:S(2)}) copy-start(f32[1,2,512,512]{3,2,1,0:T(8,128)} %param.13) | copy-start | bytes 6291460
  485.6 7.7 %copy-start.12 = (f32[64,8,2,256]{3,1,2,0:T(8,128)S(1)}, f32[64,8,2,256]{3,1,2,0:T(8,128)}, u32[]{:S(2)}) copy-start(f32[64,8,2,256]{3,1,2,0:T(8,128)} %copy.73) | copy-start | bytes 3145732
  485.6 7.7 %copy-start.13 = (f32[256,256]{1,0:T(8,128)S(1)}, f32[256,256]{1,0:T(8,128)}, u32[]{:S(2)}) copy-start(f32[256,256]{1,0:T(8,128)} %get-tuple-element.71) | copy-start | bytes 786436
  485.6 7.7 %copy-start.14 = (f32[256,256]{1,0:T(8,128)S(1)}, f32[256,256]{1,0:T(8,128)}, u32[]{:S(2)}) copy-start(f32[256,256]{1,0:T(8,128)} %get-tuple-element.72) | copy-start | bytes 786436
  485.6 7.7 %copy-start.15 = (f32[256,256]{1,0:T(8,128)S(1)}, f32[256,256]{1,0:T(8,128)}, u32[]{:S(2)}) copy-start(f32[256,256]{1,0:T(8,128)} %get-tuple-element.73) | copy-start | bytes 786436
  493.3 9.6 %copy-start.2 = (f32[2048,512]{0,1:T(8,128)}, f32[2048,512]{0,1:T(8,128)S(1)}, u32[]{:S(2)}) copy-start(f32[2048,512]{0,1:T(8,128)S(1)} %get-tuple-element.181) | copy-start | bytes 12582916
  493.3 9.6 %copy-start.4 = (f32[256,8,2,256]{3,1,2,0:T(8,128)S(1)}, f32[256,8,2,256]{3,1,2,0:T(8,128)}, u32[]{:S(2)}) copy-start(f32[256,8,2,256]{3,1,2,0:T(8,128)} %copy.74) | copy-start | bytes 12582916
  522.6 6.3 %copy-start.16 = (f32[256,256]{1,0:T(8,128)S(1)}, f32[256,256]{1,0:T(8,128)}, u32[]{:S(2)}) copy-start(f32[256,256]{1,0:T(8,128)} %get-tuple-element.17) | copy-start | bytes 786436
  528.8 3.9 copy-start.6
  532.7 6.9 %copy-start.3 = (f32[2048,512]{0,1:T(8,128)S(1)}, f32[2048,512]{0,1:T(8,128)}, u32[]{:S(2)}) copy-start(f32[2048,512]{0,1:T(8,128)} %copy-done.2) | copy-start | bytes 12582916
Sparse Core Ops, SparseCore 0:
  39.9 148.6 all-gather.2
  251.4 224.2 all-reduce.1

commit v6 on v3

--- a/solution.py
+++ b/solution.py
@@ -6,7 +6,7 @@
 BS = 256
 
 
-HIGH = lax.Precision.HIGHEST
+HIGH = lax.Precision.HIGH
 
 
 def dot(a, b):

time: 565 us -> 554 us (0.981)
  matrix products: 70.5 us -> 47.6 us
  other arithmetic: 85 us -> 93.2 us
    dot_general x6, matrix products: 70.5 us -> 47.6 us  [dot(): return jnp.dot(a, b, precision=HIGH, preferred_element_type=jnp.float32)]
    dynamic_update_slice x4, other arithmetic: 4.9 us -> 14 us  [body(): fresh = lax.dynamic_update_slice_in_dim(fresh, written, slot * BS, 1)]
where the time goes in v6:
time: 554 us; the launch traced here: 546 us
  waiting for transfers between devices  205 us (37%)
  local copies, waits for them, and re-layouts  158 us (29%)
  other arithmetic  93.2 us (17%)
  matrix products  47.6 us (9%)
  between operations  28.1 us (5%)
  starting transfers between devices  14.1 us (3%)
    psum x1, waiting for transfers between devices, body(): col_payload = lax.psum(col_payload, 'col')  86.2 us
    unnamed x62, local copies, waits for them, and re-layouts  67.2 us
    ppermute x1, waiting for transfers between devices, body(): mine = mine + lax.ppermute(mine, 'row', xor_perm(row_count, 2))  61.5 us
    dot_general x6, matrix products, dot(): return jnp.dot(a, b, precision=HIGH, preferred_element_type=jnp.float32)  47.6 us
    all_gather x1, waiting for transfers between devices, body(): gathered = lax.all_gather(best_piece, ('row', 'col'), axis=0, tiled=False)  29 us
    gather x3, local copies, waits for them, and re-layouts, child_blocks_at(): child_tiles[(rsrc // kid_rows)[:, None], (csrc // kid_cols)[None, :], (rs...  23.3 us
    ppermute x3, waiting for transfers between devices, body(): got_tags = lax.ppermute(tags, 'front', perm)  20.7 us
    dynamic_update_slice x4, other arithmetic, body(): fresh = lax.dynamic_update_slice_in_dim(fresh, written, slot * BS, 1)  14 us
  transfers between devices with their start and end apart: 11, of which 7 were waited for; matrix products, arithmetic and copies ran while one was open for 34% of the time, Pallas kernels for 0%

profile of v6, /device:TPU:1, one launch (start us, length us, event | category | flops | bytes accessed | tf_op | source)
XLA Modules:
  0.0 546.0 jit_solution(12198530277047215798)
XLA Ops:
  6.5 4.6 collective-permute-start.3
  13.2 2.0 collective-permute-start
  15.2 1.8 collective-permute-start.1
  16.9 16.2 %collective-permute-done = s32[9]{0:T(128)S(1)} collective-permute-done((s32[9]{0:T(128)S(1)}, s32[9]{0:T(128)S(1)}, u32[]{:S(2)}, u32[]{:S(2)}) %collective-permute-start) | collective-permute-done | bytes 68 | tf_op jit(solution)/shard_map/ppermute | solution.py:41
  33.2 3.2 collective-permute-done.1
  36.4 1.3 collective-permute-done.2
  37.8 2.0 select_select_fusion
  39.9 1.5 fusion.75
  51.8 2.8 select_bitcast_fusion.12
  54.6 2.5 pad_maximum_fusion
  57.1 2.3 collective-permute-start.6
  59.4 8.1 %collective-permute-done.6 = f32[1024,1024]{1,0:T(8,128)} collective-permute-done((f32[1024,1024]{1,0:T(8,128)}, f32[1024,1024]{1,0:T(8,128)}, u32[]{:S(2)}, u32[]{:S(2)}) %collective-permute-start.6) | collective-permute-done | bytes 4194336 | tf_op jit(solution)/shard_map/ppermute | solution.py:93
  67.5 3.5 fusion.72
  71.0 2.0 copy-done.1
  73.3 1.3 collective-permute-start.7
  74.6 2.7 fusion.54
  78.5 3.0 copy.127
  81.6 61.5 %collective-permute-done.7 = f32[512,1024]{1,0:T(8,128)} collective-permute-done((f32[512,1024]{1,0:T(8,128)S(1)}, f32[512,1024]{1,0:T(8,128)}, u32[]{:S(2)}, u32[]{:S(2)}) %collective-permute-start.7) | collective-permute-done | bytes 2097184 | tf_op jit(solution)/shard_map/ppermute | solution.py:97
  143.0 5.2 fusion.78
  148.3 1.5 collective-permute-start.8
  149.7 2.7 pad_add_fusion.1
  152.4 6.5 %select_bitcast_fusion.6 = (f32[2048,256]{1,0:T(8,128)S(1)}, f32[2048,256]{1,0:T(8,128)}, f32[2048,256]{1,0:T(8,128)}, f32[2048,256]{1,0:T(8,128)}) fusion(f32[1,2048,1024]{2,1,0:T(8,128)} %param.7, s32[]{:T(128)S(6)} %select_n.624, pred[]{:T(512)S(6)} %eq.142, s32[]{:T(128)S(6)} %select_n.642, pred[]{:T(512)S(6)} %eq.145, s32[]{:T(128)S(6)} %select_n.636, ...), kind=kLoop, calls=%fused_computation.52 | loop fusion | flops 2097152 | bytes 16777236 | tf_op jit(solution)/shard_map/jit(_where)/select_n | solution.py:121
  159.7 29.0 %all-gather.3.cloned.1.call-done = f32[16384,256]{1,0:T(8,128)} async-done(((f32[512,256]{1,0:T(8,128)}), f32[16384,256]{1,0:T(8,128)}) %all-gather.3.cloned.1.call-update) | async-done | bytes 16777232 | tf_op jit(solution)/shard_map/all_gather | solution.py:57
  188.7 8.6 %gather_fusion.7 = f32[16,256,256]{2,1,0:T(8,128)} fusion(f32[4,8,2,256,1,256]{5,3,2,1,0,4:T(8,128)} %bitcast.181, s32[16]{0:T(128)S(1)} %reshape.741), kind=kCustom, calls=%fused_computation.7 | custom fusion | bytes 8388864 | tf_op jit(solution)/shard_map/gather | solution.py:105
  197.2 2.7 select_bitcast_fusion.2
  199.9 2.7 copy.105
  203.7 1.1 copy-done.7
  204.8 6.0 %add_multiply_fusion = (f32[1024,1024]{1,0:T(8,128)}, f32[1024,1024]{1,0:T(8,128)S(1)}) fusion(f32[1024,1024]{1,0:T(8,128)S(1)} %bitcast.191, f32[1024,1024]{1,0:T(8,128)S(1)} %bitcast.192, f32[512,1024]{1,0:T(8,128)} %fusion.78, f32[512,1024]{1,0:T(8,128)} %collective-permute-done.8, pred[]{:T(512)S(6)} %eq.146), kind=kLoop, calls=%fused_computation.32 | loop fusion | flops 5242880 | bytes 20971520 | tf_op jit(solution)/shard_map/mul | solution.py:117
  213.7 10.9 %maximum_maximum_fusion = f32[2560,1024]{1,0:T(8,128)} fusion(f32[512,256]{1,0:T(8,128)S(1)} %get-tuple-element.34, f32[512,256]{1,0:T(8,128)S(1)} %get-tuple-element.33, f32[512,256]{1,0:T(8,128)S(1)} %get-tuple-element.32, f32[512,256]{1,0:T(8,128)S(1)} %get-tuple-element.31, f32[2048,256]{1,0:T(8,128)S(1)} %copy-done.9, f32[2048,256]{1,0:T(8,128)S(1)} %copy-done.10, ...), kind=kLoop, calls=%fused_computation.11 | loop fusion | flops 18350080 | bytes 20971520 | tf_op jit(solution)/shard_map/concatenate | solution.py:125
  226.4 9.3 %copy.91 = f32[1,2048,1024]{1,2,0:T(8,128)} copy(f32[1,2048,1024]{2,1,0:T(8,128)} %param.7) | data formatting | bytes 16777216 | tf_op args[0]
  235.7 2.7 fusion.55
  242.4 1.8 copy.132
  245.1 1.1 broadcast_in_dim.201
  246.2 5.4 copy.120
  252.8 1.1 copy.123
  254.2 1.1 broadcast_in_dim.371
  255.4 2.4 copy.125
  258.8 7.5 %copy.118 = f32[128,8,8,256]{3,1,2,0:T(8,128)} copy(f32[128,8,8,256]{3,2,1,0:T(8,128)S(1)} %bitcast.176) | data formatting | bytes 16777216
  267.8 6.6 %gather_fusion.10 = f32[4,256,256]{2,1,0:T(8,128)S(1)} fusion(f32[4,8,2,256,1,256]{5,3,2,1,0,4:T(8,128)} %bitcast.182, s32[4]{0:T(128)S(1)} %reshape.763), kind=kCustom, calls=%fused_computation.10 | custom fusion | bytes 2097216 | tf_op jit(solution)/shard_map/gather | solution.py:132
  275.4 1.0 copy.131
  276.4 10.2 %gather_fusion.2 = f32[32,256,256]{2,1,0:T(8,128)} fusion(f32[4,8,2,256,1,256]{5,3,2,1,0,4:T(8,128)} %bitcast.183, s32[32]{0:T(128)S(1)} %reshape.705), kind=kCustom, calls=%fused_computation.2 | custom fusion | bytes 16777728 | tf_op jit(solution)/shard_map/gather | solution.py:132
  286.6 7.8 %select_bitcast_fusion = f32[8,256,4,256]{3,1,2,0:T(8,128)} fusion(f32[8,4,256,256]{3,2,1,0:T(8,128)} %bitcast.174, pred[8,4]{1,0:T(8,128)(4,1)S(1)} %get-tuple-element.54), kind=kLoop, calls=%fused_computation.21 | loop fusion | flops 2097152 | bytes 16777248 | tf_op jit(solution)/shard_map/jit(_where)/select_n | solution.py:140
  294.4 12.1 %copy.112 = f32[8,256,4,256]{3,2,1,0:T(4,128)} copy(f32[8,256,4,256]{3,1,2,0:T(8,128)} %select_bitcast_fusion) | data formatting | bytes 16777216 | tf_op jit(solution)/shard_map/reshape | solution.py:142
  306.5 8.8 %copy.121 = f32[256,8,4,256]{3,1,2,0:T(8,128)} copy(f32[256,8,4,256]{3,2,1,0:T(4,128)} %bitcast.177) | data formatting | bytes 16777216
  315.3 6.5 %gather_fusion.5 = f32[4,256,256]{2,1,0:T(8,128)S(1)} fusion(f32[4,8,2,256,1,256]{5,3,2,1,0,4:T(8,128)} %bitcast.184, s32[4]{0:T(128)S(1)} %reshape.727), kind=kCustom, calls=%fused_computation.5 | custom fusion | bytes 2097216 | tf_op jit(solution)/shard_map/gather | solution.py:132
  322.8 1.1 copy.124
  323.9 10.4 %gather_fusion = f32[32,256,256]{2,1,0:T(8,128)} fusion(f32[4,8,2,256,1,256]{5,3,2,1,0,4:T(8,128)} %bitcast.185, s32[32]{0:T(128)S(1)} %reshape.691), kind=kCustom, calls=%fused_computation | custom fusion | bytes 16777728 | tf_op jit(solution)/shard_map/gather | solution.py:59
  334.3 8.0 %select_bitcast_fusion.1 = f32[8,256,4,256]{3,1,2,0:T(8,128)} fusion(f32[8,4,256,256]{3,2,1,0:T(8,128)} %bitcast.173, pred[8,4]{1,0:T(8,128)(4,1)S(1)} %get-tuple-element.55), kind=kLoop, calls=%fused_computation.22 | loop fusion | flops 2097152 | bytes 16777248 | tf_op jit(solution)/shard_map/jit(_where)/select_n | solution.py:68
  342.3 10.6 %copy.92 = f32[8,256,4,256]{1,0,3,2:T(8,128)} copy(f32[8,256,4,256]{3,1,2,0:T(8,128)} %select_bitcast_fusion.1) | data formatting | bytes 16777216 | tf_op jit(solution)/shard_map/jit(_where)/select_n | solution.py:68
  352.9 10.9 %copy.119 = f32[128,8,8,256]{3,1,2,0:T(8,128)} copy(f32[128,8,8,256]{3,2,1,0:T(8,128)} %bitcast.178) | data formatting | bytes 16777216
  364.2 86.2 %all-reduce.2.cloned.1.call-done = f32[2560,1024]{1,0:T(8,128)} async-done(((f32[2560,1024]{1,0:T(8,128)}), f32[2560,1024]{1,0:T(8,128)}) %all-reduce.2.cloned.1.call-update) | async-done | bytes 10485776 | tf_op jit(solution)/shard_map/psum | solution.py:129
  450.4 9.9 %fusion = f32[2048,1024]{1,0:T(8,128)S(1)} fusion(f32[2048,1024]{1,0:T(8,128)} %bitcast.179, f32[2048,1024]{1,0:T(8,128)} %bitcast.180, f32[2560,1024]{1,0:T(8,128)} %all-reduce.2.cloned.1.call-done), kind=kLoop, calls=%fused_computation.13 | loop fusion | flops 4194304 | bytes 33554432 | tf_op jit(solution)/shard_map/mul | solution.py:145
  460.3 5.3 broadcast_multiply_fusion.1
  465.6 5.9 %fusion.30 = f32[2048,512]{1,0:T(8,128)S(1)} fusion(f32[2048,512]{0,1:T(8,128)S(1)} %get-tuple-element.62, f32[512,512]{1,0:T(8,128)S(1)} %bitcast.196, f32[512,512]{1,0:T(8,128)S(1)} %bitcast.198, f32[2560,1024]{1,0:T(8,128)} %all-reduce.2.cloned.1.call-done), kind=kOutput, calls=%fused_computation.61 | convolution fusion | flops 3221749760 | bytes 11534336 | tf_op jit(solution)/shard_map/dot_general | solution.py:13
  471.6 6.1 %broadcast_multiply_fusion = (f32[2048,512]{0,1:T(8,128)}, f32[2048,512]{0,1:T(8,128)}) fusion(f32[2048]{0:T(1024)S(1)} %bitcast.210, f32[1,2,512,512]{3,2,1,0:T(8,128)S(1)} %copy-done.13, f32[2048,1024]{1,0:T(8,128)S(1)} %fusion, f32[2048,512]{1,0:T(8,128)S(1)} %fusion.30, f32[2048,512]{1,0:T(8,128)S(1)} %bitcast.186), kind=kOutput, calls=%fused_computation.47 | convolution fusion | flops 3224371200 | bytes 22028288 | tf_op jit(solution)/shard_map/dot_general | solution.py:13
  477.7 2.5 fusion.27
  480.2 3.5 fusion.21
  483.7 24.3 %fusion.6 = f32[2048,1024]{0,1:T(8,128)} fusion(f32[2048,1024]{0,1:T(8,128)} %bitcast.171, f32[2048,1024]{0,1:T(8,128)} %bitcast.172, f32[1,2048,1024]{1,2,0:T(8,128)} %copy.91, f32[2048,512]{0,1:T(8,128)} %get-tuple-element.64, f32[2048,512]{0,1:T(8,128)} %copy-done, f32[512,1024]{1,0:T(8,128)} %fusion.21, f32[512,1024]{1,0:T(8,128)S(1)} %slice_multiply_fusion), kind=kOutput, calls=%fused_computation.20 | convolution fusion | flops 12896436224 | bytes 46137344 | tf_op jit(solution)/shard_map/dot_general | solution.py:13
  508.0 4.0 fusion.20
  512.0 3.3 fusion.19
  515.4 3.3 fusion.18
  518.6 7.8 %copy.138 = f32[1,2048,1024]{1,2,0:T(8,128)} copy(f32[1,2048,1024]{1,2,0:T(8,128)} %bitcast.170) | data formatting | bytes 16777216
  526.4 3.3 fusion.17
  529.7 9.2 %copy.110 = f32[1,2048,1024]{2,1,0:T(8,128)} copy(f32[1,2048,1024]{1,2,0:T(8,128)} %fusion.17) | data formatting | bytes 16777216 | tf_op jit(solution)/shard_map/dynamic_update_slice | solution.py:188
  (136 shorter events, 18.1 us)
Async XLA Ops:
  6.5 182.1 %all-gather.3.cloned.1.call-start = ((), (), s32[]{:S(2)}) async-start(), calls=%async_computation.1 | async-start | bytes 17301504 | tf_op jit(solution)/shard_map/all_gather | solution.py:57
  6.5 31.2 %collective-permute-start.3 = (f32[512,256]{1,0:T(8,128)}, f32[512,256]{1,0:T(8,128)S(1)}, u32[]{:S(2)}, u32[]{:S(2)}) collective-permute-start(f32[512,256]{1,0:T(8,128)} %bitcast.205), channel_id=1, source_target_pairs={{0,96},{32,0},{64,32},{96,64},{1,97},{33,1},{65,33},{97,65},{2,98}... | collective-permute-start | bytes 1572872 | tf_op jit(solution)/shard_map/ppermute | solution.py:40
  11.1 26.7 %collective-permute-start.4 = (f32[512,256]{1,0:T(8,128)}, f32[512,256]{1,0:T(8,128)S(1)}, u32[]{:S(2)}, u32[]{:S(2)}) collective-permute-start(f32[512,256]{1,0:T(8,128)} %bitcast.206), channel_id=1, source_target_pairs={{0,64},{32,96},{64,0},{96,32},{1,65},{33,97},{65,1},{97,33},{2,66}... | collective-permute-start | bytes 1572872 | tf_op jit(solution)/shard_map/ppermute | solution.py:40
  11.1 26.7 %collective-permute-start.5 = (f32[512,256]{1,0:T(8,128)}, f32[512,256]{1,0:T(8,128)S(1)}, u32[]{:S(2)}, u32[]{:S(2)}) collective-permute-start(f32[512,256]{1,0:T(8,128)} %bitcast.207), channel_id=1, source_target_pairs={{0,32},{32,64},{64,96},{96,0},{1,33},{33,65},{65,97},{97,1},{2,34}... | collective-permute-start | bytes 1572872 | tf_op jit(solution)/shard_map/ppermute | solution.py:40
  13.2 19.9 %collective-permute-start = (s32[9]{0:T(128)S(1)}, s32[9]{0:T(128)S(1)}, u32[]{:S(2)}, u32[]{:S(2)}) collective-permute-start(s32[9]{0:T(128)S(1)} %pad_add_fusion), channel_id=1, source_target_pairs={{0,96},{32,0},{64,32},{96,64},{1,97},{33,1},{65,33},{97,65},{2,98}... | collective-permute-start | bytes 116 | tf_op jit(solution)/shard_map/ppermute | solution.py:41
  15.2 21.2 %collective-permute-start.1 = (s32[9]{0:T(128)S(1)}, s32[9]{0:T(128)S(1)}, u32[]{:S(2)}, u32[]{:S(2)}) collective-permute-start(s32[9]{0:T(128)S(1)} %pad_add_fusion), channel_id=1, source_target_pairs={{0,64},{32,96},{64,0},{96,32},{1,65},{33,97},{65,1},{97,33},{2,66}... | collective-permute-start | bytes 116 | tf_op jit(solution)/shard_map/ppermute | solution.py:41
  33.1 4.6 collective-permute-start.2
  39.8 410.6 %all-reduce.2.cloned.1.call-start = ((), (), s32[]{:S(2)}) async-start(), calls=%async_computation | async-start | bytes 20971520 | tf_op jit(solution)/shard_map/psum | solution.py:129
  54.6 2.5 copy-start.8
  57.1 10.4 %collective-permute-start.6 = (f32[1024,1024]{1,0:T(8,128)}, f32[1024,1024]{1,0:T(8,128)}, u32[]{:S(2)}, u32[]{:S(2)}) collective-permute-start(f32[1024,1024]{1,0:T(8,128)} %pad_maximum_fusion), channel_id=1, source_target_pairs={{0,8},{8,0},{16,24},{24,16},{1,9},{9,1},{17,25},{25,17},{2,10},{10... | collective-permute-start | bytes 12582920 | tf_op jit(solution)/shard_map/ppermute | solution.py:93
  71.0 2.0 copy-start.1
  72.9 4.3 copy-start.17
  73.3 69.7 %collective-permute-start.7 = (f32[512,1024]{1,0:T(8,128)S(1)}, f32[512,1024]{1,0:T(8,128)}, u32[]{:S(2)}, u32[]{:S(2)}) collective-permute-start(f32[512,1024]{1,0:T(8,128)S(1)} %slice_select_fusion.4), channel_id=1, source_target_pairs={{0,16},{8,24},{16,0},{24,8},{1,17},{9,25},{17,1},{25,9},{2,18},{10... | collective-permute-start | bytes 6291464 | tf_op jit(solution)/shard_map/ppermute | solution.py:97
  148.3 55.4 %collective-permute-start.8 = (f32[512,1024]{1,0:T(8,128)}, f32[512,1024]{1,0:T(8,128)}, u32[]{:S(2)}, u32[]{:S(2)}) collective-permute-start(f32[512,1024]{1,0:T(8,128)} %fusion.78), channel_id=1, source_target_pairs={{0,8},{8,0},{16,24},{24,16},{1,9},{9,1},{17,25},{25,17},{2,10},{10... | collective-permute-start | bytes 6291464 | tf_op jit(solution)/shard_map/ppermute | solution.py:98
  152.4 6.5 %copy-start.19 = (s32[1,8]{1,0:T(1,128)S(1)}, s32[1,8]{1,0:T(1,128)}, u32[]{:S(2)}) copy-start(s32[1,8]{1,0:T(1,128)} %param.10) | copy-start | bytes 100
  202.6 2.2 copy-start.7
  210.8 1.6 copy-start.11
  211.1 2.0 copy-start.9
  211.1 2.6 copy-start.10
  224.6 1.4 copy-start.18
  352.9 10.9 %copy-start.5 = (f32[1024,1024]{1,0:T(8,128)S(1)}, f32[1024,1024]{1,0:T(8,128)}, u32[]{:S(2)}) copy-start(f32[1024,1024]{1,0:T(8,128)} %get-tuple-element.17) | copy-start | bytes 12582916
  450.4 9.9 %copy-start.13 = (f32[1,2,512,512]{3,2,1,0:T(8,128)S(1)}, f32[1,2,512,512]{3,2,1,0:T(8,128)}, u32[]{:S(2)}) copy-start(f32[1,2,512,512]{3,2,1,0:T(8,128)} %param.13) | copy-start | bytes 6291460
  460.3 5.3 copy-start.14
  460.3 5.3 copy-start.16
  465.6 6.0 %copy-start = (f32[2048,512]{0,1:T(8,128)}, f32[2048,512]{0,1:T(8,128)S(1)}, u32[]{:S(2)}) copy-start(f32[2048,512]{0,1:T(8,128)S(1)} %get-tuple-element.62) | copy-start | bytes 12582916
  465.6 5.9 %copy-start.2 = (f32[256,8,2,256]{3,1,2,0:T(8,128)S(1)}, f32[256,8,2,256]{3,1,2,0:T(8,128)}, u32[]{:S(2)}) copy-start(f32[256,8,2,256]{3,1,2,0:T(8,128)} %copy.125) | copy-start | bytes 12582916
  471.6 6.1 %copy-start.15 = (f32[64,8,2,256]{3,1,2,0:T(8,128)S(1)}, f32[64,8,2,256]{3,1,2,0:T(8,128)}, u32[]{:S(2)}) copy-start(f32[64,8,2,256]{3,1,2,0:T(8,128)} %copy.131) | copy-start | bytes 3145732
  471.6 8.6 %copy-start.12 = (f32[64,8,4,256]{3,1,2,0:T(8,128)S(1)}, f32[64,8,4,256]{3,1,2,0:T(8,128)}, u32[]{:S(2)}) copy-start(f32[64,8,4,256]{3,1,2,0:T(8,128)} %copy.132) | copy-start | bytes 6291460
  477.7 2.5 copy-start.6
  508.0 4.0 copy-start.4
  512.0 3.3 copy-start.3
Sparse Core Ops, SparseCore 0:
  39.9 148.6 all-gather.2
  224.7 225.5 all-reduce.1

commit v7 on v6

--- a/solution.py
+++ b/solution.py
@@ -179,13 +179,18 @@
     update = dot(lowers, uppers)
     fresh = assembled - update * spread(mask_local)
 
-    replaced = [(piv[0], lower0[:, :BS], alive0_rows), (piv[1], lower0[:, BS:], alive0_rows),
-                (piv[2], lower1[:, :BS], alive1_rows), (piv[3], lower1[:, BS:], alive1_rows)]
-    for blk, values, live in replaced:
-        slot = blk % col_blocks
-        current = lax.dynamic_slice_in_dim(fresh, slot * BS, BS, 1)
-        written = jnp.where((live[:, None] > 0) & (col_id == blk // col_blocks), values, current)
-        fresh = lax.dynamic_update_slice_in_dim(fresh, written, slot * BS, 1)
+    lower_blocks = jnp.stack([lower0[:, :BS], lower0[:, BS:], lower1[:, :BS], lower1[:, BS:]])
+    live_blocks = jnp.stack([alive0_rows, alive0_rows, alive1_rows, alive1_rows]) > 0
+    local_blk = col_id * col_blocks + jnp.arange(col_blocks, dtype=jnp.int32)
+    hits = piv_arr[None, :] == local_blk[:, None]
+    which = jnp.sum(jnp.where(hits, jnp.arange(4, dtype=jnp.int32)[None, :], 0), axis=1)
+    owned = jnp.any(hits, axis=1)
+    take_lower = jnp.concatenate(
+        [jnp.broadcast_to((live_blocks[which[j]] & owned[j])[:, None], (loc_rows, BS)) for j in range(col_blocks)],
+        axis=1,
+    )
+    lower_cols = jnp.concatenate([lower_blocks[which[j]] for j in range(col_blocks)], axis=1)
+    fresh = jnp.where(take_lower, lower_cols, fresh)
     return fresh[None]
 
 

time: 554 us -> 537 us (0.969)
  local copies, waits for them, and re-layouts: 158 us -> 142 us
  between operations: 28.1 us -> 35.1 us
  other arithmetic: 93.2 us -> 87.4 us
    unnamed x62 -> x56, local copies, waits for them, and re-layouts: 67.2 us -> 44.3 us
    dynamic_update_slice x4 -> x0, other arithmetic: 14 us -> none  [body(): fresh = lax.dynamic_update_slice_in_dim(fresh, written, slot * BS, 1)]
    dynamic_slice x0 -> x5, local copies, waits for them, and re-layouts: none -> 13.7 us  [body(): lower_blocks[which[j]]]
    dynamic_update_slice x1 -> x0, local copies, waits for them, and re-layouts: 9.24 us -> none  [body(): fresh = lax.dynamic_update_slice_in_dim(fresh, written, slot * BS, 1)]
  transfers between devices with their start and end apart: 11 -> 11, of which waited for: 7 -> 7; matrix products, arithmetic and copies ran while one was open for 34% -> 33% of each run, Pallas kernels for 0% -> 0%
where the time goes in v7:
time: 537 us; the launch traced here: 530 us
  waiting for transfers between devices  207 us (39%)
  local copies, waits for them, and re-layouts  142 us (26%)
  other arithmetic  87.4 us (16%)
  matrix products  44.3 us (8%)
  between operations  35.1 us (7%)
  starting transfers between devices  14.1 us (3%)
    psum x1, waiting for transfers between devices, body(): col_payload = lax.psum(col_payload, 'col')  87.7 us
    ppermute x1, waiting for transfers between devices, body(): mine = mine + lax.ppermute(mine, 'row', xor_perm(row_count, 2))  61.6 us
    unnamed x56, local copies, waits for them, and re-layouts  44.3 us
    dot_general x6, matrix products, dot(): return jnp.dot(a, b, precision=HIGH, preferred_element_type=jnp.float32)  44.3 us
    all_gather x1, waiting for transfers between devices, body(): gathered = lax.all_gather(best_piece, ('row', 'col'), axis=0, tiled=False)  29.4 us
    gather x3, local copies, waits for them, and re-layouts, child_blocks_at(): child_tiles[(rsrc // kid_rows)[:, None], (csrc // kid_cols)[None, :], (rs...  23.2 us
    ppermute x3, waiting for transfers between devices, body(): got_tags = lax.ppermute(tags, 'front', perm)  20.7 us
    dynamic_slice x5, local copies, waits for them, and re-layouts, body(): lower_blocks[which[j]]  13.7 us
  transfers between devices with their start and end apart: 11, of which 7 were waited for; matrix products, arithmetic and copies ran while one was open for 33% of the time, Pallas kernels for 0%

profile of v7, /device:TPU:1, one launch (start us, length us, event | category | flops | bytes accessed | tf_op | source)
XLA Modules:
  0.0 530.1 jit_solution(15303116035145765563)
XLA Ops:
  6.5 4.6 collective-permute-start.6
  13.2 2.0 collective-permute-start.3
  15.2 1.8 collective-permute-start.4
  16.9 16.2 %collective-permute-done.3 = s32[9]{0:T(128)S(1)} collective-permute-done((s32[9]{0:T(128)S(1)}, s32[9]{0:T(128)S(1)}, u32[]{:S(2)}, u32[]{:S(2)}) %collective-permute-start.3) | collective-permute-done | bytes 68 | tf_op jit(solution)/shard_map/ppermute | solution.py:41
  33.2 3.2 collective-permute-done.4
  36.4 1.3 collective-permute-done.5
  37.8 2.0 select_select_fusion
  39.8 1.5 fusion.75
  51.5 2.8 select_bitcast_fusion.11
  54.3 2.5 pad_maximum_fusion.1
  56.7 2.3 collective-permute-start
  59.1 8.0 %collective-permute-done = f32[1024,1024]{1,0:T(8,128)} collective-permute-done((f32[1024,1024]{1,0:T(8,128)}, f32[1024,1024]{1,0:T(8,128)}, u32[]{:S(2)}, u32[]{:S(2)}) %collective-permute-start) | collective-permute-done | bytes 4194336 | tf_op jit(solution)/shard_map/ppermute | solution.py:93
  67.1 3.5 fusion.70
  70.6 2.0 copy-done
  73.0 1.4 collective-permute-start.1
  74.3 2.6 fusion.46
  78.2 3.0 copy.137
  81.3 61.6 %collective-permute-done.1 = f32[512,1024]{1,0:T(8,128)} collective-permute-done((f32[512,1024]{1,0:T(8,128)S(1)}, f32[512,1024]{1,0:T(8,128)}, u32[]{:S(2)}, u32[]{:S(2)}) %collective-permute-start.1) | collective-permute-done | bytes 2097184 | tf_op jit(solution)/shard_map/ppermute | solution.py:97
  142.9 5.2 fusion.78
  148.0 1.4 collective-permute-start.2
  149.4 2.6 pad_add_fusion
  152.0 6.5 %select_bitcast_fusion.5 = (f32[2048,256]{1,0:T(8,128)S(1)}, f32[2048,256]{1,0:T(8,128)}, f32[2048,256]{1,0:T(8,128)}, f32[2048,256]{1,0:T(8,128)}) fusion(f32[1,2048,1024]{2,1,0:T(8,128)} %param.7, s32[]{:T(128)S(6)} %select_n.595, pred[]{:T(512)S(6)} %eq.144, s32[]{:T(128)S(6)} %select_n.613, pred[]{:T(512)S(6)} %eq.147, s32[]{:T(128)S(6)} %select_n.607, ...), kind=kLoop, calls=%fused_computation.50 | loop fusion | flops 2097152 | bytes 16777236 | tf_op jit(solution)/shard_map/jit(_where)/select_n | solution.py:121
  159.3 29.4 %all-gather.3.cloned.1.call-done = f32[16384,256]{1,0:T(8,128)} async-done(((f32[512,256]{1,0:T(8,128)}), f32[16384,256]{1,0:T(8,128)}) %all-gather.3.cloned.1.call-update) | async-done | bytes 16777232 | tf_op jit(solution)/shard_map/all_gather | solution.py:57
  188.7 8.5 %gather_fusion.7 = f32[16,256,256]{2,1,0:T(8,128)} fusion(f32[4,8,2,256,1,256]{5,3,2,1,0,4:T(8,128)} %bitcast.201, s32[16]{0:T(128)S(1)} %reshape.743), kind=kCustom, calls=%fused_computation.7 | custom fusion | bytes 8388864 | tf_op jit(solution)/shard_map/gather | solution.py:105
  197.3 5.3 copy_select_fusion
  202.6 1.0 copy.138
  203.6 1.1 copy-done.6
  204.7 6.2 %add_multiply_fusion = (f32[1024,1024]{1,0:T(8,128)}, f32[1024,1024]{1,0:T(8,128)S(1)}) fusion(f32[1024,1024]{1,0:T(8,128)S(1)} %bitcast.211, f32[1024,1024]{1,0:T(8,128)S(1)} %bitcast.212, f32[512,1024]{1,0:T(8,128)} %fusion.78, f32[512,1024]{1,0:T(8,128)} %collective-permute-done.2, pred[]{:T(512)S(6)} %eq.148), kind=kLoop, calls=%fused_computation.36 | loop fusion | flops 5242880 | bytes 20971520 | tf_op jit(solution)/shard_map/mul | solution.py:117
  213.9 11.0 %maximum_maximum_fusion = f32[2560,1024]{1,0:T(8,128)} fusion(f32[512,256]{1,0:T(8,128)S(1)} %get-tuple-element.42, f32[512,256]{1,0:T(8,128)S(1)} %get-tuple-element.41, f32[512,256]{1,0:T(8,128)S(1)} %get-tuple-element.40, f32[512,256]{1,0:T(8,128)S(1)} %get-tuple-element.39, f32[2048,256]{1,0:T(8,128)S(1)} %copy-done.8, f32[2048,256]{1,0:T(8,128)S(1)} %copy-done.9, ...), kind=kLoop, calls=%fused_computation.11 | loop fusion | flops 18350080 | bytes 20971520 | tf_op jit(solution)/shard_map/concatenate | solution.py:125
  232.3 2.6 fusion.51
  238.9 1.8 copy.142
  241.5 1.1 broadcast_in_dim.193
  242.6 5.5 %copy.128 = f32[256,8,4,256]{3,1,2,0:T(8,128)} copy(f32[256,8,4,256]{3,2,1,0:T(4,128)S(1)} %bitcast.195) | data formatting | bytes 16777216
  249.7 1.1 broadcast_in_dim.218
  250.9 2.4 copy.133
  253.6 1.1 broadcast_in_dim.219
  254.7 5.3 copy.134
  263.3 2.5 and_reduce_fusion.3
  266.9 6.5 %gather_fusion.10 = f32[4,256,256]{2,1,0:T(8,128)S(1)} fusion(f32[4,8,2,256,1,256]{5,3,2,1,0,4:T(8,128)} %bitcast.202, s32[4]{0:T(128)S(1)} %reshape.765), kind=kCustom, calls=%fused_computation.10 | custom fusion | bytes 2097216 | tf_op jit(solution)/shard_map/gather | solution.py:132
  274.4 1.4 copy.141
  275.8 10.2 %gather_fusion.1 = f32[32,256,256]{2,1,0:T(8,128)} fusion(f32[4,8,2,256,1,256]{5,3,2,1,0,4:T(8,128)} %bitcast.203, s32[32]{0:T(128)S(1)} %reshape.701), kind=kCustom, calls=%fused_computation.1 | custom fusion | bytes 16777728 | tf_op jit(solution)/shard_map/gather | solution.py:132
  286.0 8.0 %select_bitcast_fusion.1 = f32[8,256,4,256]{3,1,2,0:T(8,128)} fusion(f32[8,4,256,256]{3,2,1,0:T(8,128)} %bitcast.194, pred[8,4]{1,0:T(8,128)(4,1)S(1)} %get-tuple-element.66), kind=kLoop, calls=%fused_computation.25 | loop fusion | flops 2097152 | bytes 16777248 | tf_op jit(solution)/shard_map/jit(_where)/select_n | solution.py:140
  294.0 12.0 %copy.119 = f32[8,256,4,256]{3,2,1,0:T(4,128)} copy(f32[8,256,4,256]{3,1,2,0:T(8,128)} %select_bitcast_fusion.1) | data formatting | bytes 16777216 | tf_op jit(solution)/shard_map/reshape | solution.py:142
  306.0 8.9 %copy.129 = f32[256,8,4,256]{3,1,2,0:T(8,128)} copy(f32[256,8,4,256]{3,2,1,0:T(4,128)} %bitcast.197) | data formatting | bytes 16777216
  314.9 6.5 %gather_fusion.4 = f32[4,256,256]{2,1,0:T(8,128)S(1)} fusion(f32[4,8,2,256,1,256]{5,3,2,1,0,4:T(8,128)} %bitcast.204, s32[4]{0:T(128)S(1)} %reshape.723), kind=kCustom, calls=%fused_computation.4 | custom fusion | bytes 2097216 | tf_op jit(solution)/shard_map/gather | solution.py:132
  322.4 10.1 %gather_fusion.5 = f32[32,256,256]{2,1,0:T(8,128)} fusion(f32[4,8,2,256,1,256]{5,3,2,1,0,4:T(8,128)} %bitcast.205, s32[32]{0:T(128)S(1)} %reshape.729), kind=kCustom, calls=%fused_computation.5 | custom fusion | bytes 16777728 | tf_op jit(solution)/shard_map/gather | solution.py:59
  332.5 7.8 %select_bitcast_fusion = f32[8,256,4,256]{3,1,2,0:T(8,128)} fusion(f32[8,4,256,256]{3,2,1,0:T(8,128)} %bitcast.193, pred[8,4]{1,0:T(8,128)(4,1)S(1)} %get-tuple-element.65), kind=kLoop, calls=%fused_computation.24 | loop fusion | flops 2097152 | bytes 16777248 | tf_op jit(solution)/shard_map/jit(_where)/select_n | solution.py:68
  340.3 12.2 %copy.114 = f32[8,256,4,256]{3,2,1,0:T(4,128)} copy(f32[8,256,4,256]{3,1,2,0:T(8,128)} %select_bitcast_fusion) | data formatting | bytes 16777216 | tf_op jit(solution)/shard_map/jit(_where)/select_n | solution.py:68
  352.5 8.9 %copy.135 = f32[256,8,4,256]{3,1,2,0:T(8,128)} copy(f32[256,8,4,256]{3,2,1,0:T(4,128)} %bitcast.198) | data formatting | bytes 16777216
  361.4 1.6 slice_multiply_fusion
  363.0 87.7 %all-reduce.2.cloned.1.call-done = f32[2560,1024]{1,0:T(8,128)} async-done(((f32[2560,1024]{1,0:T(8,128)}), f32[2560,1024]{1,0:T(8,128)}) %all-reduce.2.cloned.1.call-update) | async-done | bytes 10485776 | tf_op jit(solution)/shard_map/psum | solution.py:129
  450.7 10.1 %fusion = f32[2048,1024]{1,0:T(8,128)S(1)} fusion(f32[2048,1024]{1,0:T(8,128)} %bitcast.199, f32[2048,1024]{1,0:T(8,128)} %bitcast.200, f32[2560,1024]{1,0:T(8,128)} %all-reduce.2.cloned.1.call-done), kind=kLoop, calls=%fused_computation.13 | loop fusion | flops 4194304 | bytes 33554432 | tf_op jit(solution)/shard_map/mul | solution.py:145
  460.8 3.6 broadcast_multiply_fusion.1
  464.4 5.9 %fusion.26 = f32[2048,512]{1,0:T(8,128)S(1)} fusion(f32[2048,512]{0,1:T(8,128)S(1)} %get-tuple-element.82, f32[512,512]{1,0:T(8,128)S(1)} %bitcast.218, f32[512,512]{1,0:T(8,128)S(1)} %bitcast.220, f32[2560,1024]{1,0:T(8,128)} %all-reduce.2.cloned.1.call-done), kind=kOutput, calls=%fused_computation.59 | convolution fusion | flops 3221749760 | bytes 11534336 | tf_op jit(solution)/shard_map/dot_general | solution.py:13
  470.3 5.6 %broadcast_multiply_fusion = (f32[2048,512]{0,1:T(8,128)}, f32[2048,512]{0,1:T(8,128)S(1)}) fusion(f32[2048]{0:T(1024)S(1)} %bitcast.235, f32[1,2,512,512]{3,2,1,0:T(8,128)S(1)} %copy-done.13, f32[2048,1024]{1,0:T(8,128)S(1)} %fusion, f32[2048,512]{1,0:T(8,128)S(1)} %fusion.26, f32[2048,512]{1,0:T(8,128)S(1)} %bitcast.206), kind=kOutput, calls=%fused_computation.45 | convolution fusion | flops 3224371200 | bytes 22028288 | tf_op jit(solution)/shard_map/dot_general | solution.py:13
  476.8 1.0 pad_maximum_fusion
  477.9 2.8 constant_dynamic-slice_fusion.6
  480.7 2.9 copy.108
  483.6 2.9 copy.109
  486.5 1.8 copy.110
  488.3 3.3 copy.111
  491.6 3.0 fusion.23
  494.8 3.5 fusion.17
  500.0 22.8 %fusion.1 = f32[1,2048,1024]{2,1,0:T(8,128)} fusion(f32[2048,256]{1,0:T(8,128)} %bitcast.230, f32[2048,256]{1,0:T(8,128)} %bitcast.229, f32[2048,256]{1,0:T(8,128)} %bitcast.228, f32[2048,256]{1,0:T(8,128)} %bitcast.227, f32[2048,1024]{1,0:T(8,128)} %bitcast.214, f32[2048,1024]{1,0:T(8,128)} %bitcast.215, f32[1,2048,1024]{2,1,0:T(8,128)} %param.7, ...), kind=kOutput, calls=%fused_computation.16 | convolution fusion | flops 12911116288 | bytes 56623104 | tf_op jit(solution)/shard_map/dot_general | solution.py:13
  (137 shorter events, 20.3 us)
Async XLA Ops:
  6.5 182.2 %all-gather.3.cloned.1.call-start = ((), (), s32[]{:S(2)}) async-start(), calls=%async_computation.1 | async-start | bytes 17301504 | tf_op jit(solution)/shard_map/all_gather | solution.py:57
  6.5 31.2 %collective-permute-start.6 = (f32[512,256]{1,0:T(8,128)}, f32[512,256]{1,0:T(8,128)S(1)}, u32[]{:S(2)}, u32[]{:S(2)}) collective-permute-start(f32[512,256]{1,0:T(8,128)} %bitcast.231), channel_id=1, source_target_pairs={{0,96},{32,0},{64,32},{96,64},{1,97},{33,1},{65,33},{97,65},{2,98}... | collective-permute-start | bytes 1572872 | tf_op jit(solution)/shard_map/ppermute | solution.py:40
  11.1 26.7 %collective-permute-start.7 = (f32[512,256]{1,0:T(8,128)}, f32[512,256]{1,0:T(8,128)S(1)}, u32[]{:S(2)}, u32[]{:S(2)}) collective-permute-start(f32[512,256]{1,0:T(8,128)} %bitcast.232), channel_id=1, source_target_pairs={{0,64},{32,96},{64,0},{96,32},{1,65},{33,97},{65,1},{97,33},{2,66}... | collective-permute-start | bytes 1572872 | tf_op jit(solution)/shard_map/ppermute | solution.py:40
  11.1 26.7 %collective-permute-start.8 = (f32[512,256]{1,0:T(8,128)}, f32[512,256]{1,0:T(8,128)S(1)}, u32[]{:S(2)}, u32[]{:S(2)}) collective-permute-start(f32[512,256]{1,0:T(8,128)} %bitcast.233), channel_id=1, source_target_pairs={{0,32},{32,64},{64,96},{96,0},{1,33},{33,65},{65,97},{97,1},{2,34}... | collective-permute-start | bytes 1572872 | tf_op jit(solution)/shard_map/ppermute | solution.py:40
  13.2 19.9 %collective-permute-start.3 = (s32[9]{0:T(128)S(1)}, s32[9]{0:T(128)S(1)}, u32[]{:S(2)}, u32[]{:S(2)}) collective-permute-start(s32[9]{0:T(128)S(1)} %pad_add_fusion.1), channel_id=1, source_target_pairs={{0,96},{32,0},{64,32},{96,64},{1,97},{33,1},{65,33},{97,65},{2,98}... | collective-permute-start | bytes 116 | tf_op jit(solution)/shard_map/ppermute | solution.py:41
  15.2 21.2 %collective-permute-start.4 = (s32[9]{0:T(128)S(1)}, s32[9]{0:T(128)S(1)}, u32[]{:S(2)}, u32[]{:S(2)}) collective-permute-start(s32[9]{0:T(128)S(1)} %pad_add_fusion.1), channel_id=1, source_target_pairs={{0,64},{32,96},{64,0},{96,32},{1,65},{33,97},{65,1},{97,33},{2,66}... | collective-permute-start | bytes 116 | tf_op jit(solution)/shard_map/ppermute | solution.py:41
  33.1 4.6 collective-permute-start.5
  39.8 410.9 %all-reduce.2.cloned.1.call-start = ((), (), s32[]{:S(2)}) async-start(), calls=%async_computation | async-start | bytes 20971520 | tf_op jit(solution)/shard_map/psum | solution.py:129
  54.3 2.5 copy-start.7
  56.7 10.3 %collective-permute-start = (f32[1024,1024]{1,0:T(8,128)}, f32[1024,1024]{1,0:T(8,128)}, u32[]{:S(2)}, u32[]{:S(2)}) collective-permute-start(f32[1024,1024]{1,0:T(8,128)} %pad_maximum_fusion.1), channel_id=1, source_target_pairs={{0,8},{8,0},{16,24},{24,16},{1,9},{9,1},{17,25},{25,17},{2,10},{10... | collective-permute-start | bytes 12582920 | tf_op jit(solution)/shard_map/ppermute | solution.py:93
  70.6 2.0 copy-start
  72.6 4.4 copy-start.14
  73.0 69.9 %collective-permute-start.1 = (f32[512,1024]{1,0:T(8,128)S(1)}, f32[512,1024]{1,0:T(8,128)}, u32[]{:S(2)}, u32[]{:S(2)}) collective-permute-start(f32[512,1024]{1,0:T(8,128)S(1)} %slice_select_fusion), channel_id=1, source_target_pairs={{0,16},{8,24},{16,0},{24,8},{1,17},{9,25},{17,1},{25,9},{2,18},{10... | collective-permute-start | bytes 6291464 | tf_op jit(solution)/shard_map/ppermute | solution.py:97
  148.0 55.6 %collective-permute-start.2 = (f32[512,1024]{1,0:T(8,128)}, f32[512,1024]{1,0:T(8,128)}, u32[]{:S(2)}, u32[]{:S(2)}) collective-permute-start(f32[512,1024]{1,0:T(8,128)} %fusion.78), channel_id=1, source_target_pairs={{0,8},{8,0},{16,24},{24,16},{1,9},{9,1},{17,25},{25,17},{2,10},{10... | collective-permute-start | bytes 6291464 | tf_op jit(solution)/shard_map/ppermute | solution.py:98
  152.0 6.5 %copy-start.16 = (s32[1,8]{1,0:T(1,128)S(1)}, s32[1,8]{1,0:T(1,128)}, u32[]{:S(2)}) copy-start(s32[1,8]{1,0:T(1,128)} %param.10) | copy-start | bytes 100
  202.6 2.2 copy-start.6
  210.9 1.6 copy-start.10
  211.3 2.0 copy-start.8
  211.3 2.6 copy-start.9
  224.9 1.3 copy-start.15
  352.5 8.9 %copy-start.4 = (f32[1024,1024]{1,0:T(8,128)S(1)}, f32[1024,1024]{1,0:T(8,128)}, u32[]{:S(2)}) copy-start(f32[1024,1024]{1,0:T(8,128)} %get-tuple-element.17) | copy-start | bytes 12582916
  450.7 10.1 %copy-start.12 = (f32[1,2,512,512]{3,2,1,0:T(8,128)S(1)}, f32[1,2,512,512]{3,2,1,0:T(8,128)}, u32[]{:S(2)}) copy-start(f32[1,2,512,512]{3,2,1,0:T(8,128)} %param.13) | copy-start | bytes 6291460
  464.4 5.9 %copy-start.1 = (f32[2048,512]{0,1:T(8,128)}, f32[2048,512]{0,1:T(8,128)S(1)}, u32[]{:S(2)}) copy-start(f32[2048,512]{0,1:T(8,128)S(1)} %get-tuple-element.82) | copy-start | bytes 12582916
  464.4 5.9 %copy-start.3 = (f32[256,8,2,256]{3,1,2,0:T(8,128)S(1)}, f32[256,8,2,256]{3,1,2,0:T(8,128)}, u32[]{:S(2)}) copy-start(f32[256,8,2,256]{3,1,2,0:T(8,128)} %copy.133) | copy-start | bytes 12582916
  464.4 5.9 %copy-start.13 = (f32[1,2,512,512]{3,2,1,0:T(8,128)S(1)}, f32[1,2,512,512]{3,2,1,0:T(8,128)}, u32[]{:S(2)}) copy-start(f32[1,2,512,512]{3,2,1,0:T(8,128)} %param.13) | copy-start | bytes 6291460
  488.3 6.3 %copy-start.11 = (f32[64,8,4,256]{3,1,2,0:T(8,128)S(1)}, f32[64,8,4,256]{3,1,2,0:T(8,128)}, u32[]{:S(2)}) copy-start(f32[64,8,4,256]{3,1,2,0:T(8,128)} %copy.142) | copy-start | bytes 6291460
  491.6 3.1 copy-start.5
  494.8 5.3 copy-start.2
Sparse Core Ops, SparseCore 0:
  39.9 148.7 all-gather.2
  225.1 225.5 all-reduce.1

commit v8 on v7

--- a/solution.py
+++ b/solution.py
@@ -142,14 +142,17 @@
         return got.transpose(0, 2, 1, 3).reshape(nr * BS, nc * BS)
 
     mask_rows_local = lax.dynamic_slice_in_dim(mask_all, row_id * row_blocks, row_blocks, 0)
-    col_panels = spread(mask_rows_local[:, piv_arr]) * (
-        col_payload[:loc_rows] + child_blocks_at(row_src, row_has, prow_src, prow_has)
-    )
+    child_cp, child_x, child_y = lax.optimization_barrier((
+        child_blocks_at(row_src, row_has, prow_src, prow_has),
+        child_blocks_at(prow_src[:2], prow_has[:2], prow_src[2:], prow_has[2:]),
+        child_blocks_at(prow_src[2:], prow_has[2:], prow_src[:2], prow_has[:2]),
+    ))
+    col_panels = spread(mask_rows_local[:, piv_arr]) * (col_payload[:loc_rows] + child_cp)
     corner_x = spread(mask_all[piv_arr[:2]][:, piv_arr[2:]]) * (
-        col_payload[loc_rows:, : 2 * BS] + child_blocks_at(prow_src[:2], prow_has[:2], prow_src[2:], prow_has[2:])
+        col_payload[loc_rows:, : 2 * BS] + child_x
     )
     corner_y = spread(mask_all[piv_arr[2:]][:, piv_arr[:2]]) * (
-        col_payload[loc_rows:, 2 * BS:] + child_blocks_at(prow_src[2:], prow_has[2:], prow_src[:2], prow_has[:2])
+        col_payload[loc_rows:, 2 * BS:] + child_y
     )
 
     alive0_rows = jnp.repeat(lax.dynamic_slice_in_dim(alive0, row_id * row_blocks, row_blocks), BS)

time: 537 us -> 538 us (level)
  local copies, waits for them, and re-layouts: 142 us -> 152 us
  waiting for transfers between devices: 207 us -> 197 us
    reshape x1 -> x0, local copies, waits for them, and re-layouts: 12 us -> none  [child_blocks_at(): return got.transpose(0, 2, 1, 3).reshape(nr * BS, nc * BS)]
    select_n x2 -> x3, local copies, waits for them, and re-layouts: 1.62 us -> 12 us  [child_blocks_at(): got = jnp.where((rhas[:, None] & chas[None, :])[:, :, None, None], got, 0.0)]
    psum x1, waiting for transfers between devices: 87.7 us -> 77.4 us  [body(): col_payload = lax.psum(col_payload, 'col')]
    optimization_barrier x0 -> x1, local copies, waits for them, and re-layouts: none -> 9.48 us  [body(): lax.optimization_barrier((child_blocks_at(row_src, row_has, prow_src, pro...]
  transfers between devices with their start and end apart: 11 -> 11, of which waited for: 7 -> 7; matrix products, arithmetic and copies ran while one was open for 33% -> 35% of each run, Pallas kernels for 0% -> 0%
where the time goes in v8:
time: 538 us; the launch traced here: 530 us
  waiting for transfers between devices  197 us (37%)
  local copies, waits for them, and re-layouts  152 us (28%)
  other arithmetic  88 us (16%)
  matrix products  44.3 us (8%)
  between operations  35.1 us (7%)
  starting transfers between devices  14.1 us (3%)
    psum x1, waiting for transfers between devices, body(): col_payload = lax.psum(col_payload, 'col')  77.4 us
    ppermute x1, waiting for transfers between devices, body(): mine = mine + lax.ppermute(mine, 'row', xor_perm(row_count, 2))  61.6 us
    unnamed x56, local copies, waits for them, and re-layouts  46 us
    dot_general x6, matrix products, dot(): return jnp.dot(a, b, precision=HIGH, preferred_element_type=jnp.float32)  44.3 us
    all_gather x1, waiting for transfers between devices, body(): gathered = lax.all_gather(best_piece, ('row', 'col'), axis=0, tiled=False)  29.4 us
    gather x3, local copies, waits for them, and re-layouts, child_blocks_at(): child_tiles[(rsrc // kid_rows)[:, None], (csrc // kid_cols)[None, :], (rs...  23.3 us
    ppermute x3, waiting for transfers between devices, body(): got_tags = lax.ppermute(tags, 'front', perm)  20.7 us
    dynamic_slice x5, local copies, waits for them, and re-layouts, body(): lower_blocks[which[j]]  13.9 us
  transfers between devices with their start and end apart: 11, of which 7 were waited for; matrix products, arithmetic and copies ran while one was open for 35% of the time, Pallas kernels for 0%

profile of v8, /device:TPU:1, one launch (start us, length us, event | category | flops | bytes accessed | tf_op | source)
XLA Modules:
  0.0 530.2 jit_solution(4763977368228306991)
XLA Ops:
  6.5 4.6 collective-permute-start.6
  13.2 2.0 collective-permute-start.3
  15.2 1.8 collective-permute-start.4
  16.9 16.2 %collective-permute-done.3 = s32[9]{0:T(128)S(1)} collective-permute-done((s32[9]{0:T(128)S(1)}, s32[9]{0:T(128)S(1)}, u32[]{:S(2)}, u32[]{:S(2)}) %collective-permute-start.3) | collective-permute-done | bytes 68 | tf_op jit(solution)/shard_map/ppermute | solution.py:41
  33.2 3.2 collective-permute-done.4
  36.4 1.3 collective-permute-done.5
  37.8 2.0 select_select_fusion
  39.8 1.5 fusion.75
  51.5 2.8 select_bitcast_fusion.11
  54.3 2.5 pad_maximum_fusion.1
  56.7 2.3 collective-permute-start
  59.1 8.0 %collective-permute-done = f32[1024,1024]{1,0:T(8,128)} collective-permute-done((f32[1024,1024]{1,0:T(8,128)}, f32[1024,1024]{1,0:T(8,128)}, u32[]{:S(2)}, u32[]{:S(2)}) %collective-permute-start) | collective-permute-done | bytes 4194336 | tf_op jit(solution)/shard_map/ppermute | solution.py:93
  67.1 3.5 fusion.70
  70.6 2.0 copy-done
  73.0 1.4 collective-permute-start.1
  74.3 2.6 fusion.46
  78.2 3.0 copy.136
  81.3 61.6 %collective-permute-done.1 = f32[512,1024]{1,0:T(8,128)} collective-permute-done((f32[512,1024]{1,0:T(8,128)S(1)}, f32[512,1024]{1,0:T(8,128)}, u32[]{:S(2)}, u32[]{:S(2)}) %collective-permute-start.1) | collective-permute-done | bytes 2097184 | tf_op jit(solution)/shard_map/ppermute | solution.py:97
  142.9 5.2 fusion.78
  148.0 1.4 collective-permute-start.2
  149.4 2.6 pad_add_fusion
  152.0 6.5 %select_bitcast_fusion.5 = (f32[2048,256]{1,0:T(8,128)S(1)}, f32[2048,256]{1,0:T(8,128)}, f32[2048,256]{1,0:T(8,128)}, f32[2048,256]{1,0:T(8,128)}) fusion(f32[1,2048,1024]{2,1,0:T(8,128)} %param.7, s32[]{:T(128)S(6)} %select_n.595, pred[]{:T(512)S(6)} %eq.144, s32[]{:T(128)S(6)} %select_n.613, pred[]{:T(512)S(6)} %eq.147, s32[]{:T(128)S(6)} %select_n.607, ...), kind=kLoop, calls=%fused_computation.50 | loop fusion | flops 2097152 | bytes 16777236 | tf_op jit(solution)/shard_map/jit(_where)/select_n | solution.py:121
  159.3 29.4 %all-gather.3.cloned.1.call-done = f32[16384,256]{1,0:T(8,128)} async-done(((f32[512,256]{1,0:T(8,128)}), f32[16384,256]{1,0:T(8,128)}) %all-gather.3.cloned.1.call-update) | async-done | bytes 16777232 | tf_op jit(solution)/shard_map/all_gather | solution.py:57
  188.7 8.5 %gather_fusion.8 = f32[16,256,256]{2,1,0:T(8,128)} fusion(f32[4,8,2,256,1,256]{5,3,2,1,0,4:T(8,128)} %bitcast.203, s32[16]{0:T(128)S(1)} %reshape.749), kind=kCustom, calls=%fused_computation.8 | custom fusion | bytes 8388864 | tf_op jit(solution)/shard_map/gather | solution.py:105
  197.3 5.3 copy_select_fusion
  202.6 1.0 copy.137
  203.6 1.1 copy-done.6
  204.7 6.2 %add_multiply_fusion = (f32[1024,1024]{1,0:T(8,128)}, f32[1024,1024]{1,0:T(8,128)S(1)}) fusion(f32[1024,1024]{1,0:T(8,128)S(1)} %bitcast.213, f32[1024,1024]{1,0:T(8,128)S(1)} %bitcast.214, f32[512,1024]{1,0:T(8,128)} %fusion.78, f32[512,1024]{1,0:T(8,128)} %collective-permute-done.2, pred[]{:T(512)S(6)} %eq.148), kind=kLoop, calls=%fused_computation.36 | loop fusion | flops 5242880 | bytes 20971520 | tf_op jit(solution)/shard_map/mul | solution.py:117
  213.9 11.0 %maximum_maximum_fusion = f32[2560,1024]{1,0:T(8,128)} fusion(f32[512,256]{1,0:T(8,128)S(1)} %get-tuple-element.48, f32[512,256]{1,0:T(8,128)S(1)} %get-tuple-element.47, f32[512,256]{1,0:T(8,128)S(1)} %get-tuple-element.46, f32[512,256]{1,0:T(8,128)S(1)} %get-tuple-element.45, f32[2048,256]{1,0:T(8,128)S(1)} %copy-done.8, f32[2048,256]{1,0:T(8,128)S(1)} %copy-done.9, ...), kind=kLoop, calls=%fused_computation.11 | loop fusion | flops 18350080 | bytes 20971520 | tf_op jit(solution)/shard_map/concatenate | solution.py:125
  232.2 2.6 fusion.59
  238.8 1.8 copy.140
  241.5 1.1 broadcast_in_dim.193
  242.6 5.5 %copy.126 = f32[256,8,4,256]{3,1,2,0:T(8,128)} copy(f32[256,8,4,256]{3,2,1,0:T(4,128)S(1)} %bitcast.198) | data formatting | bytes 16777216
  249.7 1.1 broadcast_in_dim.222
  250.9 2.4 copy.132
  253.6 1.1 broadcast_in_dim.223
  254.7 5.3 copy.133
  263.3 2.5 and_reduce_fusion.3
  266.9 10.2 %gather_fusion.1 = f32[32,256,256]{2,1,0:T(8,128)} fusion(f32[4,8,2,256,1,256]{5,3,2,1,0,4:T(8,128)} %bitcast.204, s32[32]{0:T(128)S(1)} %reshape.701), kind=kCustom, calls=%fused_computation.1 | custom fusion | bytes 16777728 | tf_op jit(solution)/shard_map/gather | solution.py:132
  277.1 8.4 %select_bitcast_fusion.1 = f32[8,256,4,256]{3,1,2,0:T(8,128)} fusion(f32[8,4,256,256]{3,2,1,0:T(8,128)} %bitcast.196, pred[8,4]{1,0:T(8,128)(4,1)S(1)} %get-tuple-element.68), kind=kLoop, calls=%fused_computation.25 | loop fusion | flops 2097152 | bytes 16777248 | tf_op jit(solution)/shard_map/jit(_where)/select_n | solution.py:140
  285.4 10.4 %copy.102 = f32[8,256,4,256]{1,0,3,2:T(8,128)} copy(f32[8,256,4,256]{3,1,2,0:T(8,128)} %select_bitcast_fusion.1) | data formatting | bytes 16777216 | tf_op jit(solution)/shard_map/jit(_where)/select_n | solution.py:140
  295.9 10.8 %copy.127 = f32[128,8,8,256]{3,1,2,0:T(8,128)} copy(f32[128,8,8,256]{3,2,1,0:T(8,128)} %bitcast.200) | data formatting | bytes 16777216
  306.7 6.6 %gather_fusion.3 = f32[4,256,256]{2,1,0:T(8,128)S(1)} fusion(f32[4,8,2,256,1,256]{5,3,2,1,0,4:T(8,128)} %bitcast.205, s32[4]{0:T(128)S(1)} %reshape.713), kind=kCustom, calls=%fused_computation.3 | custom fusion | bytes 2097216 | tf_op jit(solution)/shard_map/gather | solution.py:132
  314.2 1.1 copy.129
  315.3 6.5 %gather_fusion.2 = f32[4,256,256]{2,1,0:T(8,128)S(1)} fusion(f32[4,8,2,256,1,256]{5,3,2,1,0,4:T(8,128)} %bitcast.206, s32[4]{0:T(128)S(1)} %reshape.707), kind=kCustom, calls=%fused_computation.2 | custom fusion | bytes 2097216 | tf_op jit(solution)/shard_map/gather | solution.py:132
  322.9 9.5 %copy.105 = f32[2048,1024]{1,0:T(8,128)} copy(f32[2048,1024]{0,1:T(8,128)} %bitcast.197) | data formatting | bytes 16777216 | tf_op jit(solution)/shard_map/optimization_barrier | solution.py:145
  332.3 10.2 %gather_fusion.6 = f32[32,256,256]{2,1,0:T(8,128)} fusion(f32[4,8,2,256,1,256]{5,3,2,1,0,4:T(8,128)} %bitcast.207, s32[32]{0:T(128)S(1)} %reshape.735), kind=kCustom, calls=%fused_computation.6 | custom fusion | bytes 16777728 | tf_op jit(solution)/shard_map/gather | solution.py:59
  342.5 8.1 %select_bitcast_fusion = f32[8,256,4,256]{3,1,2,0:T(8,128)} fusion(f32[8,4,256,256]{3,2,1,0:T(8,128)} %bitcast.195, pred[8,4]{1,0:T(8,128)(4,1)S(1)} %get-tuple-element.67), kind=kLoop, calls=%fused_computation.24 | loop fusion | flops 2097152 | bytes 16777248 | tf_op jit(solution)/shard_map/jit(_where)/select_n | solution.py:68
  350.6 12.0 %copy.115 = f32[8,256,4,256]{3,2,1,0:T(4,128)} copy(f32[8,256,4,256]{3,1,2,0:T(8,128)} %select_bitcast_fusion) | data formatting | bytes 16777216 | tf_op jit(solution)/shard_map/jit(_where)/select_n | solution.py:68
  362.6 9.0 %copy.134 = f32[256,8,4,256]{3,1,2,0:T(8,128)} copy(f32[256,8,4,256]{3,2,1,0:T(4,128)} %bitcast.201) | data formatting | bytes 16777216
  371.6 1.6 slice_multiply_fusion
  373.2 77.4 %all-reduce.2.cloned.1.call-done = f32[2560,1024]{1,0:T(8,128)} async-done(((f32[2560,1024]{1,0:T(8,128)}), f32[2560,1024]{1,0:T(8,128)}) %all-reduce.2.cloned.1.call-update) | async-done | bytes 10485776 | tf_op jit(solution)/shard_map/psum | solution.py:129
  450.6 10.1 %fusion = f32[2048,1024]{1,0:T(8,128)S(1)} fusion(f32[2048,1024]{1,0:T(8,128)} %bitcast.202, f32[2048,1024]{1,0:T(8,128)} %copy.105, f32[2560,1024]{1,0:T(8,128)} %all-reduce.2.cloned.1.call-done), kind=kLoop, calls=%fused_computation.13 | loop fusion | flops 4194304 | bytes 33554432 | tf_op jit(solution)/shard_map/mul | solution.py:150
  460.7 3.6 broadcast_multiply_fusion.1
  464.3 5.9 %fusion.26 = f32[2048,512]{1,0:T(8,128)S(1)} fusion(f32[2048,512]{0,1:T(8,128)S(1)} %get-tuple-element.88, f32[512,512]{1,0:T(8,128)S(1)} %bitcast.220, f32[512,512]{1,0:T(8,128)S(1)} %bitcast.222, f32[2560,1024]{1,0:T(8,128)} %all-reduce.2.cloned.1.call-done), kind=kOutput, calls=%fused_computation.59 | convolution fusion | flops 3221749760 | bytes 11534336 | tf_op jit(solution)/shard_map/dot_general | solution.py:13
  470.2 5.6 %broadcast_multiply_fusion = (f32[2048,512]{0,1:T(8,128)}, f32[2048,512]{0,1:T(8,128)S(1)}) fusion(f32[2048]{0:T(1024)S(1)} %bitcast.237, f32[1,2,512,512]{3,2,1,0:T(8,128)S(1)} %copy-done.13, f32[2048,1024]{1,0:T(8,128)S(1)} %fusion, f32[2048,512]{1,0:T(8,128)S(1)} %fusion.26, f32[2048,512]{1,0:T(8,128)S(1)} %bitcast.208), kind=kOutput, calls=%fused_computation.45 | convolution fusion | flops 3224371200 | bytes 22028288 | tf_op jit(solution)/shard_map/dot_general | solution.py:13
  477.8 2.9 constant_dynamic-slice_fusion.6
  480.8 2.9 copy.109
  483.7 2.9 copy.110
  486.6 1.8 copy.111
  488.4 3.3 copy.112
  491.7 3.0 fusion.23
  494.9 3.5 fusion.17
  500.1 22.8 %fusion.1 = f32[1,2048,1024]{2,1,0:T(8,128)} fusion(f32[2048,256]{1,0:T(8,128)} %bitcast.232, f32[2048,256]{1,0:T(8,128)} %bitcast.231, f32[2048,256]{1,0:T(8,128)} %bitcast.230, f32[2048,256]{1,0:T(8,128)} %bitcast.229, f32[2048,1024]{1,0:T(8,128)} %bitcast.216, f32[2048,1024]{1,0:T(8,128)} %bitcast.217, f32[1,2048,1024]{2,1,0:T(8,128)} %param.7, ...), kind=kOutput, calls=%fused_computation.16 | convolution fusion | flops 12911116288 | bytes 56623104 | tf_op jit(solution)/shard_map/dot_general | solution.py:13
  (138 shorter events, 21.3 us)
Async XLA Ops:
  6.5 182.2 %all-gather.3.cloned.1.call-start = ((), (), s32[]{:S(2)}) async-start(), calls=%async_computation.1 | async-start | bytes 17301504 | tf_op jit(solution)/shard_map/all_gather | solution.py:57
  6.5 31.2 %collective-permute-start.6 = (f32[512,256]{1,0:T(8,128)}, f32[512,256]{1,0:T(8,128)S(1)}, u32[]{:S(2)}, u32[]{:S(2)}) collective-permute-start(f32[512,256]{1,0:T(8,128)} %bitcast.233), channel_id=1, source_target_pairs={{0,96},{32,0},{64,32},{96,64},{1,97},{33,1},{65,33},{97,65},{2,98}... | collective-permute-start | bytes 1572872 | tf_op jit(solution)/shard_map/ppermute | solution.py:40
  11.1 26.7 %collective-permute-start.7 = (f32[512,256]{1,0:T(8,128)}, f32[512,256]{1,0:T(8,128)S(1)}, u32[]{:S(2)}, u32[]{:S(2)}) collective-permute-start(f32[512,256]{1,0:T(8,128)} %bitcast.234), channel_id=1, source_target_pairs={{0,64},{32,96},{64,0},{96,32},{1,65},{33,97},{65,1},{97,33},{2,66}... | collective-permute-start | bytes 1572872 | tf_op jit(solution)/shard_map/ppermute | solution.py:40
  11.1 26.7 %collective-permute-start.8 = (f32[512,256]{1,0:T(8,128)}, f32[512,256]{1,0:T(8,128)S(1)}, u32[]{:S(2)}, u32[]{:S(2)}) collective-permute-start(f32[512,256]{1,0:T(8,128)} %bitcast.235), channel_id=1, source_target_pairs={{0,32},{32,64},{64,96},{96,0},{1,33},{33,65},{65,97},{97,1},{2,34}... | collective-permute-start | bytes 1572872 | tf_op jit(solution)/shard_map/ppermute | solution.py:40
  13.2 19.9 %collective-permute-start.3 = (s32[9]{0:T(128)S(1)}, s32[9]{0:T(128)S(1)}, u32[]{:S(2)}, u32[]{:S(2)}) collective-permute-start(s32[9]{0:T(128)S(1)} %pad_add_fusion.1), channel_id=1, source_target_pairs={{0,96},{32,0},{64,32},{96,64},{1,97},{33,1},{65,33},{97,65},{2,98}... | collective-permute-start | bytes 116 | tf_op jit(solution)/shard_map/ppermute | solution.py:41
  15.2 21.2 %collective-permute-start.4 = (s32[9]{0:T(128)S(1)}, s32[9]{0:T(128)S(1)}, u32[]{:S(2)}, u32[]{:S(2)}) collective-permute-start(s32[9]{0:T(128)S(1)} %pad_add_fusion.1), channel_id=1, source_target_pairs={{0,64},{32,96},{64,0},{96,32},{1,65},{33,97},{65,1},{97,33},{2,66}... | collective-permute-start | bytes 116 | tf_op jit(solution)/shard_map/ppermute | solution.py:41
  33.1 4.6 collective-permute-start.5
  39.8 410.8 %all-reduce.2.cloned.1.call-start = ((), (), s32[]{:S(2)}) async-start(), calls=%async_computation | async-start | bytes 20971520 | tf_op jit(solution)/shard_map/psum | solution.py:129
  54.3 2.5 copy-start.7
  56.7 10.3 %collective-permute-start = (f32[1024,1024]{1,0:T(8,128)}, f32[1024,1024]{1,0:T(8,128)}, u32[]{:S(2)}, u32[]{:S(2)}) collective-permute-start(f32[1024,1024]{1,0:T(8,128)} %pad_maximum_fusion.1), channel_id=1, source_target_pairs={{0,8},{8,0},{16,24},{24,16},{1,9},{9,1},{17,25},{25,17},{2,10},{10... | collective-permute-start | bytes 12582920 | tf_op jit(solution)/shard_map/ppermute | solution.py:93
  70.6 2.0 copy-start
  72.6 4.4 copy-start.14
  73.0 69.9 %collective-permute-start.1 = (f32[512,1024]{1,0:T(8,128)S(1)}, f32[512,1024]{1,0:T(8,128)}, u32[]{:S(2)}, u32[]{:S(2)}) collective-permute-start(f32[512,1024]{1,0:T(8,128)S(1)} %slice_select_fusion), channel_id=1, source_target_pairs={{0,16},{8,24},{16,0},{24,8},{1,17},{9,25},{17,1},{25,9},{2,18},{10... | collective-permute-start | bytes 6291464 | tf_op jit(solution)/shard_map/ppermute | solution.py:97
  148.0 55.6 %collective-permute-start.2 = (f32[512,1024]{1,0:T(8,128)}, f32[512,1024]{1,0:T(8,128)}, u32[]{:S(2)}, u32[]{:S(2)}) collective-permute-start(f32[512,1024]{1,0:T(8,128)} %fusion.78), channel_id=1, source_target_pairs={{0,8},{8,0},{16,24},{24,16},{1,9},{9,1},{17,25},{25,17},{2,10},{10... | collective-permute-start | bytes 6291464 | tf_op jit(solution)/shard_map/ppermute | solution.py:98
  152.0 6.5 %copy-start.16 = (s32[1,8]{1,0:T(1,128)S(1)}, s32[1,8]{1,0:T(1,128)}, u32[]{:S(2)}) copy-start(s32[1,8]{1,0:T(1,128)} %param.10) | copy-start | bytes 100
  202.6 2.2 copy-start.6
  210.9 1.6 copy-start.10
  211.2 2.0 copy-start.8
  211.2 2.6 copy-start.9
  224.9 1.3 copy-start.15
  362.6 9.0 %copy-start.4 = (f32[1024,1024]{1,0:T(8,128)S(1)}, f32[1024,1024]{1,0:T(8,128)}, u32[]{:S(2)}) copy-start(f32[1024,1024]{1,0:T(8,128)} %get-tuple-element.21) | copy-start | bytes 12582916
  450.6 10.1 %copy-start.12 = (f32[1,2,512,512]{3,2,1,0:T(8,128)S(1)}, f32[1,2,512,512]{3,2,1,0:T(8,128)}, u32[]{:S(2)}) copy-start(f32[1,2,512,512]{3,2,1,0:T(8,128)} %param.13) | copy-start | bytes 6291460
  464.3 5.9 %copy-start.1 = (f32[2048,512]{0,1:T(8,128)}, f32[2048,512]{0,1:T(8,128)S(1)}, u32[]{:S(2)}) copy-start(f32[2048,512]{0,1:T(8,128)S(1)} %get-tuple-element.88) | copy-start | bytes 12582916
  464.3 5.9 %copy-start.3 = (f32[256,8,2,256]{3,1,2,0:T(8,128)S(1)}, f32[256,8,2,256]{3,1,2,0:T(8,128)}, u32[]{:S(2)}) copy-start(f32[256,8,2,256]{3,1,2,0:T(8,128)} %copy.132) | copy-start | bytes 12582916
  464.3 5.9 %copy-start.13 = (f32[1,2,512,512]{3,2,1,0:T(8,128)S(1)}, f32[1,2,512,512]{3,2,1,0:T(8,128)}, u32[]{:S(2)}) copy-start(f32[1,2,512,512]{3,2,1,0:T(8,128)} %param.13) | copy-start | bytes 6291460
  488.4 6.3 %copy-start.11 = (f32[64,8,4,256]{3,1,2,0:T(8,128)S(1)}, f32[64,8,4,256]{3,1,2,0:T(8,128)}, u32[]{:S(2)}) copy-start(f32[64,8,4,256]{3,1,2,0:T(8,128)} %copy.140) | copy-start | bytes 6291460
  491.7 3.1 copy-start.5
  494.9 5.3 copy-start.2
Sparse Core Ops, SparseCore 0:
  39.9 148.7 all-gather.2
  225.1 225.5 all-reduce.1
